TPU v7x, 128 devices: a whole 4x4x4 slice. The times are simulated.
128 devices in a mesh: gz: 16 (over z, x), gx: 8 (over y, core).
Axes of the slice: x: 4, y: 4, z: 4, core: 2. Of those that a mesh axis runs over, the one named last changes fastest.
Arguments:
- rhs_temp: float32 [1024, 128, 128], P('gz', 'gx'), may hold values from -24 to 24
- rhs_ion: float32 [1024, 128, 128], P('gz', 'gx'), may hold values from -24 to 24
- cond_temp: float32 [1024, 128, 128], P('gz', 'gx'), may hold values from 20000 to 300000
- cond_ion: float32 [1024, 128, 128], P('gz', 'gx'), may hold values from 20000 to 300000
- bubble_target: int32 [16, 2048], P('gz', 'gx'), may hold values from 0 to 8191, as said below
- bubble_sink: float32 [16, 2048, 128], P('gz', 'gx'), may hold values from 2 to 20
- bubble_void: float32 [16, 2048, 128], P('gz', 'gx'), may hold values from 0.05 to 0.5
Outputs:
- temp_new: float32 [1024, 128, 128], P('gz', 'gx')
- ion_new: float32 [1024, 128, 128], P('gz', 'gx')
Inputs may be any that keep to these rules, and one draw needn't show every extreme that they name: `bubble_target`: in every draw one index of gx receives exactly 96 blocks from every device of each gz index; no device sends more than 96 blocks to one index of gx; the other indices of gx receive a device's remaining blocks in nearly equal numbers; cells within a device are independent and may repeat.
All inputs are finite; a program needn't handle non-finite values.
Results may differ from a plain program's by a relative error of at most 0.0007.
Values sent between devices are 32-bit elements; how exact they have to be, the bound alone decides.
No kernel may reach another device: no remote copies, remote signals or barrier semaphores. Data moves between devices by JAX's collectives and lax.ppermute only.
A program may use at most 64 MiB of HBM per device.

v0:
```python
import jax
import jax.numpy as jnp
from jax import lax
from jax.sharding import PartitionSpec as P

ion_rate = 40.0


def shifted(block, axis, distance):
    devices = range(lax.axis_size(axis))
    route = [(i - distance, i) for i in devices if i - distance in devices]
    return lax.ppermute(block, axis, route)


def padded_2(cells, sides, width):
    for axis, dim in sides:
        count = lax.axis_size(axis)
        ends = count - 1
        head = lax.slice_in_dim(cells, 0, width, axis=dim)
        tail = lax.slice_in_dim(cells, cells.shape[dim] - width, cells.shape[dim], axis=dim)
        cells = jnp.concatenate(
            [
                lax.ppermute(tail, axis, [(i, (i + 1) % count) for i in range(ends)]),
                cells,
                lax.ppermute(head, axis, [((i + 1) % count, i) for i in range(ends)]),
            ],
            axis=dim,
        )
    return cells


def push_rows(values, stride, fill_value, axis_dim):
    row_total = values.shape[axis_dim]
    pad_shape = list(values.shape)
    pad_shape[axis_dim] = stride
    padding = jnp.full(tuple(pad_shape), fill_value, values.dtype)
    kept_rows = lax.slice_in_dim(values, 0, row_total - stride, axis=axis_dim)
    return jnp.concatenate([padding, kept_rows], axis=axis_dim)


def pull_rows(values, stride, fill_value, axis_dim):
    row_total = values.shape[axis_dim]
    pad_shape = list(values.shape)
    pad_shape[axis_dim] = stride
    padding = jnp.full(tuple(pad_shape), fill_value, values.dtype)
    kept_rows = lax.slice_in_dim(values, stride, row_total, axis=axis_dim)
    return jnp.concatenate([kept_rows, padding], axis=axis_dim)


def cyclic_reduce(lower_band, main_band, upper_band, rights):
    z_cells = main_band.shape[1]
    stride = 1
    while stride < z_cells:
        low_prev = push_rows(lower_band, stride, 0.0, 1)
        main_prev = push_rows(main_band, stride, 1.0, 1)
        up_prev = push_rows(upper_band, stride, 0.0, 1)
        right_prev = push_rows(rights, stride, 0.0, 2)
        low_next = pull_rows(lower_band, stride, 0.0, 1)
        main_next = pull_rows(main_band, stride, 1.0, 1)
        up_next = pull_rows(upper_band, stride, 0.0, 1)
        right_next = pull_rows(rights, stride, 0.0, 2)
        left_factor = lower_band / main_prev
        right_factor = upper_band / main_next
        main_band = main_band - left_factor * up_prev - right_factor * low_next
        lower_band = -left_factor * low_prev
        upper_band = -right_factor * up_next
        rights = rights - left_factor * right_prev - right_factor * right_next
        stride = stride * 2
    return rights / main_band


def mat_mul(left_mat, right_mat):
    return (
        left_mat[0] * right_mat[0] + left_mat[1] * right_mat[2],
        left_mat[0] * right_mat[1] + left_mat[1] * right_mat[3],
        left_mat[2] * right_mat[0] + left_mat[3] * right_mat[2],
        left_mat[2] * right_mat[1] + left_mat[3] * right_mat[3],
    )


def mat_vec(matrix, vector):
    return (
        matrix[0] * vector[0] + matrix[1] * vector[1],
        matrix[2] * vector[0] + matrix[3] * vector[1],
    )


def mat_inverse(matrix):
    determ = matrix[0] * matrix[3] - matrix[1] * matrix[2]
    return (matrix[3] / determ, -matrix[1] / determ, -matrix[2] / determ, matrix[0] / determ)


def negate(matrix):
    return tuple((-entry for entry in matrix))


def interface_doubling(first_y, last_y, near_first, near_last, far_first, far_last):
    zero_plane = jnp.zeros_like(first_y)
    rows_pack = jnp.stack(
        [
            zero_plane,
            near_first,
            zero_plane,
            near_last,
            far_first,
            zero_plane,
            far_last,
            zero_plane,
            first_y,
            last_y,
        ]
    )
    chain_size = lax.axis_size("gz")
    stride = 1
    while stride < chain_size:
        below_pack = shifted(rows_pack, "gz", stride)
        above_pack = shifted(rows_pack, "gz", -stride)
        own_rows = tuple((rows_pack[member] for member in range(10)))
        below_rows = tuple((below_pack[member] for member in range(10)))
        above_rows = tuple((above_pack[member] for member in range(10)))
        own_low, own_up, own_right = (own_rows[0:4], own_rows[4:8], own_rows[8:10])
        product_low = mat_mul(own_low, below_rows[4:8])
        product_up = mat_mul(own_up, above_rows[0:4])
        diagonal = (
            1.0 - product_low[0] - product_up[0],
            -product_low[1] - product_up[1],
            -product_low[2] - product_up[2],
            1.0 - product_low[3] - product_up[3],
        )
        inverse = mat_inverse(diagonal)
        new_low = mat_mul(inverse, negate(mat_mul(own_low, below_rows[0:4])))
        new_up = mat_mul(inverse, negate(mat_mul(own_up, above_rows[4:8])))
        carried_low = mat_vec(own_low, below_rows[8:10])
        carried_up = mat_vec(own_up, above_rows[8:10])
        new_right = mat_vec(
            inverse,
            (
                own_right[0] - carried_low[0] - carried_up[0],
                own_right[1] - carried_low[1] - carried_up[1],
            ),
        )
        rows_pack = jnp.stack(new_low + new_up + new_right)
        stride = stride * 2
    last_prev = shifted(rows_pack[9], "gz", 1)
    first_next = shifted(rows_pack[8], "gz", -1)
    return (last_prev, first_next)


def body(rhs_temp, rhs_ion, cond_temp, cond_ion, bubble_target, bubble_sink, bubble_void):
    z_cells, x_cells, y_cells = rhs_temp.shape
    cell_total = z_cells * x_cells
    groups = lax.axis_size("gx")
    target = bubble_target[0]
    payload = jnp.concatenate([bubble_sink[0], bubble_void[0]], axis=1)
    record_total = target.shape[0]
    slot_count = 3 * record_total // groups
    destination = target // cell_total
    cell_index = target % cell_total
    same_owner = destination[:, None] == destination[None, :]
    row_ids = lax.broadcasted_iota(jnp.int32, (record_total, record_total), 0)
    col_ids = lax.broadcasted_iota(jnp.int32, (record_total, record_total), 1)
    rank_within = jnp.sum((same_owner & (row_ids > col_ids)).astype(jnp.int32), axis=1)
    slot_index = destination * slot_count + rank_within
    send_rows = (
        jnp.zeros((groups * slot_count, 2 * y_cells), jnp.float32).at[slot_index].set(payload)
    )
    send_cells = (
        jnp.full((groups * slot_count,), cell_total, jnp.int32).at[slot_index].set(cell_index)
    )
    received_rows, received_cells = (
        lax.all_to_all(
            send_rows.reshape(groups, slot_count, 2 * y_cells),
            "gx",
            split_axis=0,
            concat_axis=0,
            tiled=True,
        ),
        lax.all_to_all(
            send_cells.reshape(groups, slot_count), "gx", split_axis=0, concat_axis=0, tiled=True
        ),
    )
    received_rows = received_rows.reshape(groups * slot_count, 2 * y_cells)
    received_cells = received_cells.reshape(groups * slot_count)
    sources = (
        jnp.zeros((cell_total, 2 * y_cells), jnp.float32)
        .at[received_cells]
        .add(received_rows, mode="drop")
    )
    sources = sources.reshape(z_cells, x_cells, 2, y_cells)
    absorb = jnp.stack([sources[:, :, 0], ion_rate * sources[:, :, 1]])
    position = lax.axis_index("gz")
    stacked = jnp.stack([cond_temp, cond_ion])
    padded = padded_2(stacked, (("gz", 1),), 1)
    inner_faces = 2.0 * padded[:, :-1] * padded[:, 1:] / (padded[:, :-1] + padded[:, 1:])
    below = inner_faces[:, :-1]
    above = inner_faces[:, 1:]
    below = below.at[:, 0].set(jnp.where(position == 0, 2.0 * stacked[:, 0], below[:, 0]))
    lower_full = -below
    upper_full = -above
    main_band = 1.0 + below + above + absorb
    lower_local = lower_full.at[:, 0].set(0.0)
    upper_local = upper_full.at[:, -1].set(0.0)
    rhs_both = jnp.stack([rhs_temp, rhs_ion])
    unit_first = jnp.zeros_like(rhs_both).at[:, 0].set(1.0)
    unit_last = jnp.zeros_like(rhs_both).at[:, -1].set(1.0)
    solved = cyclic_reduce(
        lower_local, main_band, upper_local, jnp.stack([rhs_both, unit_first, unit_last])
    )
    base_part, left_spike, right_spike = (solved[0], solved[1], solved[2])
    near_coef = lower_full[:, 0]
    far_coef = upper_full[:, -1]
    first_y = base_part[:, 0]
    last_y = base_part[:, -1]
    near_first = near_coef * left_spike[:, 0]
    near_last = near_coef * left_spike[:, -1]
    far_first = far_coef * right_spike[:, 0]
    far_last = far_coef * right_spike[:, -1]
    last_prev, first_next = interface_doubling(
        first_y, last_y, near_first, near_last, far_first, far_last
    )
    fields = (
        base_part
        - left_spike * (near_coef * last_prev)[:, None]
        - right_spike * (far_coef * first_next)[:, None]
    )
    return (fields[0], fields[1])


def solution(mesh):
    in_specs = (
        P("gz", "gx", None),
        P("gz", "gx", None),
        P("gz", "gx", None),
        P("gz", "gx", None),
        P("gz", "gx"),
        P("gz", "gx", None),
        P("gz", "gx", None),
    )
    out_specs = (P("gz", "gx", None), P("gz", "gx", None))
    return jax.shard_map(body, mesh=mesh, in_specs=in_specs, out_specs=out_specs, check_vma=False)
```

profile of v0, /device:TPU:96, one launch (start us, length us, event | category | flops | bytes accessed | tf_op | source)
XLA Modules:
  0.0 142.2 jit_solution(827689229007317747)
XLA Ops:
  0.7 0.8 and_select_fusion
  1.5 0.7 and_select_fusion.2
  2.4 0.7 compare_select_fusion.1
  3.1 1.4 scatter_custom_fusion
  4.5 0.7 all_to_all.9
  5.1 4.5 %all-to-all-start = ((s32[8,1,96]{2,1,0:T(1,128)}), s32[8,1,96]{2,1,0:T(1,128)S(1)}, u32[]{:S(2)}, u32[]{:S(2)}) async-start(s32[8,1,96]{2,1,0:T(1,128)} %all_to_all.9), calls=%async_computation | async-start | bytes 8192 | tf_op jit(solution)/shard_map/all_to_all | solution.py:178
  9.6 0.7 pad_maximum_fusion.3
  10.4 4.5 %collective-permute-start.1 = (f32[2,1,16,128]{3,2,0,1:T(8,128)S(1)}, f32[2,1,16,128]{3,2,0,1:T(8,128)S(1)}, u32[]{:S(2)}, u32[]{:S(2)}) collective-permute-start(f32[2,1,16,128]{3,2,0,1:T(8,128)S(1)} %get-tuple-element.313), channel_id=1, source_target_pairs={{8,0},{16,8},{24,16},{32,24},{40,32},{48,40},{56,48},{64,56},{72,6... | collective-permute-start | bytes 49160 | tf_op jit(solution)/shard_map/ppermute | solution.py:25
  14.9 1.9 %collective-permute-start = (f32[2,1,16,128]{3,2,0,1:T(8,128)S(1)}, f32[2,1,16,128]{3,2,0,1:T(8,128)S(1)}, u32[]{:S(2)}, u32[]{:S(2)}) collective-permute-start(f32[2,1,16,128]{3,2,0,1:T(8,128)S(1)} %get-tuple-element.312), channel_id=1, source_target_pairs={{0,8},{8,16},{16,24},{24,32},{32,40},{40,48},{48,56},{56,64},{64,7... | collective-permute-start | bytes 49160 | tf_op jit(solution)/shard_map/ppermute | solution.py:23
  16.8 1.3 maximum_bitcast_fusion
  18.1 1.1 copy-done.2
  19.5 3.4 %fusion.196 = (f32[3,2,63,16,128]{4,3,1,2,0:T(8,128)}, f32[3,2,63,16,128]{4,3,1,2,0:T(8,128)}) fusion(f32[3,2,64,16,128]{4,3,1,2,0:T(8,128)S(1)} %pad_maximum_fusion), kind=kLoop, calls=%fused_computation.549 | loop fusion | bytes 12386304 | tf_op jit(solution)/shard_map/slice | solution.py:37
  22.9 2.3 %scatter_custom_fusion.1 = f32[768,256]{1,0:T(8,128)} fusion(s32[256]{0:T(256)S(1)} %bitcast.1058, f32[]{:T(128)} %constant.184.clone.1, f32[256,128]{1,0:T(8,128)S(1)} %bitcast.1052, f32[]{:T(128)} %constant.303, f32[256,128]{1,0:T(8,128)S(1)} %bitcast.1053), kind=kCustom, calls=%fused_computation.55 | custom fusion | flops 65536 | bytes 1048584 | tf_op jit(solution)/shard_map/scatter | solution.py:165
  25.3 4.8 %all-to-all-start.1 = ((f32[8,96,256]{2,1,0:T(8,128)}), f32[8,96,256]{2,1,0:T(8,128)}, u32[]{:S(2)}, u32[]{:S(2)}) async-start(f32[8,96,256]{2,1,0:T(8,128)} %bitcast.12), calls=%async_computation.1 | async-start | bytes 1572864 | tf_op jit(solution)/shard_map/all_to_all | solution.py:171
  30.1 0.5 broadcast.876
  30.6 0.7 reduce.15
  32.2 0.7 copy-done.5
  33.3 1.5 %fusion.209 = (f32[2,63,16,128]{3,2,1,0:T(8,128)}, f32[2,63,16,128]{3,2,1,0:T(8,128)}) fusion(f32[2,64,16,128]{3,2,1,0:T(8,128)S(1)} %broadcast_dynamic-update-slice_fusion), kind=kLoop, calls=%fused_computation.562 | loop fusion | bytes 4128768 | tf_op jit(solution)/shard_map/slice | solution.py:46
  34.8 8.5 %all-to-all-done.1 = f32[8,96,256]{2,1,0:T(8,128)} async-done(((f32[8,96,256]{2,1,0:T(8,128)}), f32[8,96,256]{2,1,0:T(8,128)}, u32[]{:S(2)}, u32[]{:S(2)}) %all-to-all-start.1) | async-done | bytes 786464 | tf_op jit(solution)/shard_map/all_to_all | solution.py:171
  43.3 7.0 %scatter_custom_fusion.2 = f32[1024,256]{1,0:T(8,128)} fusion(s32[768]{0:T(1024)S(1)} %fusion.159, f32[768,256]{1,0:T(8,128)} %bitcast.13, f32[]{:T(128)} %constant.184.clone.1), kind=kCustom, calls=%fused_computation.53 | custom fusion | flops 196608 | bytes 1049088 | tf_op jit(solution)/shard_map/scatter-add | solution.py:187
  50.3 2.8 %reshape.617 = f32[64,16,2,128]{3,2,1,0:T(2,128)} reshape(f32[1024,256]{1,0:T(8,128)} %scatter_custom_fusion.2) | data formatting | bytes 2097152 | tf_op jit(solution)/shard_map/reshape | solution.py:189
  53.1 2.7 %fusion.213 = (f32[64,16,1,128]{3,2,1,0:T(1,128)S(1)}, f32[64,16,1,128]{3,2,1,0:T(1,128)S(1)}) fusion(f32[64,16,2,128]{3,2,1,0:T(2,128)} %reshape.617), kind=kLoop, calls=%fused_computation.566 | loop fusion | flops 131072 | bytes 2097152 | tf_op jit(solution)/shard_map/slice | solution.py:190
  56.5 1.0 copy-done.11
  58.0 1.4 copy-done
  59.3 0.9 copy-done.1
  61.1 1.3 multiply_subtract_fusion.4
  62.4 0.9 fusion.195
  63.7 0.9 copy-done.10
  65.5 1.3 multiply_subtract_fusion.3
  66.8 0.9 fusion.194
  69.0 1.3 multiply_subtract_fusion.2
  70.2 0.8 fusion.193
  72.3 1.4 %multiply_subtract_fusion.1 = f32[3,2,64,16,128]{4,3,1,2,0:T(8,128)S(1)} fusion(f32[3,2,56,16,128]{4,3,1,2,0:T(8,128)S(1)} %get-tuple-element.267, f32[3,2,64,16,128]{4,3,1,2,0:T(8,128)S(1)} %multiply_subtract_fusion.2, f32[3,2,56,16,128]{4,3,1,2,0:T(8,128)S(1)} %get-tuple-element.266, f32[2,64,16,128]{3,2,1,0:T(8,128)S(1)} %get-tuple-element.241, ...), kind=kLoop, calls=%fused_computation.6 | loop fusion | flops 3145728 | bytes 13893632 | tf_op jit(solution)/shard_map/sub | solution.py:67
  73.7 0.7 fusion.192
  75.6 1.1 multiply_subtract_fusion
  76.7 0.6 fusion.191
  77.9 1.1 subtract_divide_fusion
  79.3 0.7 constant_dynamic-update-slice_fusion.8
  80.1 0.7 constant_dynamic-update-slice_fusion.6
  80.8 0.7 constant_dynamic-update-slice_fusion.5
  81.5 0.7 constant_dynamic-update-slice_fusion.3
  82.2 2.8 %collective-permute-start.2 = (f32[10,2,16,128]{3,2,1,0:T(8,128)S(1)}, f32[10,2,16,128]{3,2,1,0:T(8,128)S(1)}, u32[]{:S(2)}, u32[]{:S(2)}) collective-permute-start(f32[10,2,16,128]{3,2,1,0:T(8,128)S(1)} %constant_dynamic-update-slice_fusion), channel_id=1, source_target_pairs={{0,8},{8,16},{16,24},{24,32},{32,40},{40,48},{48,56},{56,64},{64,7... | collective-permute-start | bytes 491528 | tf_op jit(solution)/shard_map/ppermute | solution.py:12
  85.1 5.1 %collective-permute-start.3 = (f32[10,2,16,128]{3,2,1,0:T(8,128)S(1)}, f32[10,2,16,128]{3,2,1,0:T(8,128)S(1)}, u32[]{:S(2)}, u32[]{:S(2)}) collective-permute-start(f32[10,2,16,128]{3,2,1,0:T(8,128)S(1)} %constant_dynamic-update-slice_fusion), channel_id=1, source_target_pairs={{8,0},{16,8},{24,16},{32,24},{40,32},{48,40},{56,48},{64,56},{72,6... | collective-permute-start | bytes 491528 | tf_op jit(solution)/shard_map/ppermute | solution.py:12
  90.2 2.0 %collective-permute-done.2 = f32[10,2,16,128]{3,2,1,0:T(8,128)S(1)} collective-permute-done((f32[10,2,16,128]{3,2,1,0:T(8,128)S(1)}, f32[10,2,16,128]{3,2,1,0:T(8,128)S(1)}, u32[]{:S(2)}, u32[]{:S(2)}) %collective-permute-start.2) | collective-permute-done | bytes 163872 | tf_op jit(solution)/shard_map/ppermute | solution.py:12
  92.2 1.2 collective-permute-done.3
  93.6 5.6 %collective-permute-start.5 = (f32[10,2,16,128]{3,2,1,0:T(8,128)S(1)}, f32[10,2,16,128]{3,2,1,0:T(8,128)S(1)}, u32[]{:S(2)}, u32[]{:S(2)}) collective-permute-start(f32[10,2,16,128]{3,2,1,0:T(8,128)S(1)} %get-tuple-element.196), channel_id=1, source_target_pairs={{16,0},{24,8},{32,16},{40,24},{48,32},{56,40},{64,48},{72,56},{80,... | collective-permute-start | bytes 491528 | tf_op jit(solution)/shard_map/ppermute | solution.py:12
  99.2 1.9 %collective-permute-start.4 = (f32[10,2,16,128]{3,2,1,0:T(8,128)S(1)}, f32[10,2,16,128]{3,2,1,0:T(8,128)S(1)}, u32[]{:S(2)}, u32[]{:S(2)}) collective-permute-start(f32[10,2,16,128]{3,2,1,0:T(8,128)S(1)} %get-tuple-element.196), channel_id=1, source_target_pairs={{0,16},{8,24},{16,32},{24,40},{32,48},{40,56},{48,64},{56,72},{64,... | collective-permute-start | bytes 491528 | tf_op jit(solution)/shard_map/ppermute | solution.py:12
  101.1 0.8 fusion.26
  101.9 1.2 collective-permute-done.5
  103.1 5.7 %collective-permute-done.4 = f32[10,2,16,128]{3,2,1,0:T(8,128)S(1)} collective-permute-done((f32[10,2,16,128]{3,2,1,0:T(8,128)S(1)}, f32[10,2,16,128]{3,2,1,0:T(8,128)S(1)}, u32[]{:S(2)}, u32[]{:S(2)}) %collective-permute-start.4) | collective-permute-done | bytes 163872 | tf_op jit(solution)/shard_map/ppermute | solution.py:12
  109.0 2.0 %collective-permute-start.7 = (f32[10,2,16,128]{3,2,1,0:T(8,128)S(1)}, f32[10,2,16,128]{3,2,1,0:T(8,128)S(1)}, u32[]{:S(2)}, u32[]{:S(2)}) collective-permute-start(f32[10,2,16,128]{3,2,1,0:T(8,128)S(1)} %get-tuple-element.149), channel_id=1, source_target_pairs={{32,0},{40,8},{48,16},{56,24},{64,32},{72,40},{80,48},{88,56},{96,... | collective-permute-start | bytes 491528 | tf_op jit(solution)/shard_map/ppermute | solution.py:12
  111.1 1.3 collective-permute-start.6
  112.5 1.4 collective-permute-done.7
  113.9 6.1 %collective-permute-done.6 = f32[10,2,16,128]{3,2,1,0:T(8,128)S(1)} collective-permute-done((f32[10,2,16,128]{3,2,1,0:T(8,128)S(1)}, f32[10,2,16,128]{3,2,1,0:T(8,128)S(1)}, u32[]{:S(2)}, u32[]{:S(2)}) %collective-permute-start.6) | collective-permute-done | bytes 163872 | tf_op jit(solution)/shard_map/ppermute | solution.py:12
  120.3 1.3 collective-permute-start.9
  121.6 1.3 collective-permute-start.8
  123.1 1.2 collective-permute-done.9
  124.4 5.9 %collective-permute-done.8 = f32[10,2,16,128]{3,2,1,0:T(8,128)S(1)} collective-permute-done((f32[10,2,16,128]{3,2,1,0:T(8,128)S(1)}, f32[10,2,16,128]{3,2,1,0:T(8,128)S(1)}, u32[]{:S(2)}, u32[]{:S(2)}) %collective-permute-start.8) | collective-permute-done | bytes 163872 | tf_op jit(solution)/shard_map/ppermute | solution.py:12
  130.4 1.9 %collective-permute-start.11 = (f32[2,16,128]{2,1,0:T(8,128)S(1)}, f32[2,16,128]{2,1,0:T(8,128)S(1)}, u32[]{:S(2)}, u32[]{:S(2)}) collective-permute-start(f32[2,16,128]{2,1,0:T(8,128)S(1)} %multiply_add_fusion), channel_id=1, source_target_pairs={{8,0},{16,8},{24,16},{32,24},{40,32},{48,40},{56,48},{64,56},{72,6... | collective-permute-start | bytes 49160 | tf_op jit(solution)/shard_map/ppermute | solution.py:12
  132.3 3.9 %collective-permute-start.10 = (f32[2,16,128]{2,1,0:T(8,128)S(1)}, f32[2,16,128]{2,1,0:T(8,128)S(1)}, u32[]{:S(2)}, u32[]{:S(2)}) collective-permute-start(f32[2,16,128]{2,1,0:T(8,128)S(1)} %get-tuple-element.62), channel_id=1, source_target_pairs={{0,8},{8,16},{16,24},{24,32},{32,40},{40,48},{48,56},{56,64},{64,7... | collective-permute-start | bytes 49160 | tf_op jit(solution)/shard_map/ppermute | solution.py:12
  136.2 0.7 bitcast_multiply_fusion.101
  137.0 3.1 %collective-permute-done.10 = f32[2,16,128]{2,1,0:T(8,128)S(1)} collective-permute-done((f32[2,16,128]{2,1,0:T(8,128)S(1)}, f32[2,16,128]{2,1,0:T(8,128)S(1)}, u32[]{:S(2)}, u32[]{:S(2)}) %collective-permute-start.10) | collective-permute-done | bytes 16416 | tf_op jit(solution)/shard_map/ppermute | solution.py:12
  140.0 0.7 bitcast_multiply_fusion.127
  141.1 1.0 slice_bitcast_fusion.3
  (130 shorter events, 10.8 us)
Async XLA Ops:
  0.6 18.5 %copy-start.6 = (f32[1,2,64,16,128]{4,3,1,2,0:T(8,128)S(1)}, f32[1,2,64,16,128]{4,3,1,2,0:T(8,128)}, u32[]{:S(2)}) copy-start(f32[1,2,64,16,128]{4,3,1,2,0:T(8,128)} %constant.179.clone.1) | copy-start | bytes 3145732
  0.6 18.5 %copy-start.8 = (f32[1,2,64,16,128]{4,3,1,2,0:T(8,128)S(1)}, f32[1,2,64,16,128]{4,3,1,2,0:T(8,128)}, u32[]{:S(2)}) copy-start(f32[1,2,64,16,128]{4,3,1,2,0:T(8,128)} %constant.178.clone.1) | copy-start | bytes 3145732
  5.1 20.1 %all-to-all-start = ((s32[8,1,96]{2,1,0:T(1,128)}), s32[8,1,96]{2,1,0:T(1,128)S(1)}, u32[]{:S(2)}, u32[]{:S(2)}) async-start(s32[8,1,96]{2,1,0:T(1,128)} %all_to_all.9), calls=%async_computation | async-start | bytes 8192 | tf_op jit(solution)/shard_map/all_to_all | solution.py:178
  10.4 21.0 %collective-permute-start.1 = (f32[2,1,16,128]{3,2,0,1:T(8,128)S(1)}, f32[2,1,16,128]{3,2,0,1:T(8,128)S(1)}, u32[]{:S(2)}, u32[]{:S(2)}) collective-permute-start(f32[2,1,16,128]{3,2,0,1:T(8,128)S(1)} %get-tuple-element.313), channel_id=1, source_target_pairs={{8,0},{16,8},{24,16},{32,24},{40,32},{48,40},{56,48},{64,56},{72,6... | collective-permute-start | bytes 49160 | tf_op jit(solution)/shard_map/ppermute | solution.py:25
  14.9 16.5 %collective-permute-start = (f32[2,1,16,128]{3,2,0,1:T(8,128)S(1)}, f32[2,1,16,128]{3,2,0,1:T(8,128)S(1)}, u32[]{:S(2)}, u32[]{:S(2)}) collective-permute-start(f32[2,1,16,128]{3,2,0,1:T(8,128)S(1)} %get-tuple-element.312), channel_id=1, source_target_pairs={{0,8},{8,16},{16,24},{24,32},{32,40},{40,48},{48,56},{56,64},{64,7... | collective-permute-start | bytes 49160 | tf_op jit(solution)/shard_map/ppermute | solution.py:23
  18.1 1.1 copy-start.2
  19.5 3.4 %copy-start.14 = (f32[1,256,128]{2,1,0:T(8,128)S(1)}, f32[1,256,128]{2,1,0:T(8,128)}, u32[]{:S(2)}) copy-start(f32[1,256,128]{2,1,0:T(8,128)} %param.23) | copy-start | bytes 393220
  19.5 3.4 %copy-start.15 = (f32[1,256,128]{2,1,0:T(8,128)S(1)}, f32[1,256,128]{2,1,0:T(8,128)}, u32[]{:S(2)}) copy-start(f32[1,256,128]{2,1,0:T(8,128)} %param.22) | copy-start | bytes 393220
  19.5 11.9 %copy-start.12 = (f32[64,16,128]{2,1,0:T(8,128)S(1)}, f32[64,16,128]{2,1,0:T(8,128)}, u32[]{:S(2)}) copy-start(f32[64,16,128]{2,1,0:T(8,128)} %param.20) | copy-start | bytes 1572868
  19.5 11.9 %copy-start.13 = (f32[64,16,128]{2,1,0:T(8,128)S(1)}, f32[64,16,128]{2,1,0:T(8,128)}, u32[]{:S(2)}) copy-start(f32[64,16,128]{2,1,0:T(8,128)} %param.19) | copy-start | bytes 1572868
  25.3 18.0 %all-to-all-start.1 = ((f32[8,96,256]{2,1,0:T(8,128)}), f32[8,96,256]{2,1,0:T(8,128)}, u32[]{:S(2)}, u32[]{:S(2)}) async-start(f32[8,96,256]{2,1,0:T(8,128)} %bitcast.12), calls=%async_computation.1 | async-start | bytes 1572864 | tf_op jit(solution)/shard_map/all_to_all | solution.py:171
  31.9 1.0 copy-start.5
  32.0 1.3 copy-start.4
  56.2 1.2 copy-start.11
  57.5 1.9 %copy-start = (f32[3,2,63,16,128]{4,3,1,2,0:T(8,128)S(1)}, f32[3,2,63,16,128]{4,3,1,2,0:T(8,128)}, u32[]{:S(2)}) copy-start(f32[3,2,63,16,128]{4,3,1,2,0:T(8,128)} %get-tuple-element.272) | copy-start | bytes 9289732
  57.5 2.8 %copy-start.1 = (f32[3,2,63,16,128]{4,3,1,2,0:T(8,128)S(1)}, f32[3,2,63,16,128]{4,3,1,2,0:T(8,128)}, u32[]{:S(2)}) copy-start(f32[3,2,63,16,128]{4,3,1,2,0:T(8,128)} %get-tuple-element.273) | copy-start | bytes 9289732
  57.5 3.0 %copy-start.3 = (f32[1,2,64,16,128]{4,3,1,2,0:T(8,128)S(1)}, f32[1,2,64,16,128]{4,3,1,2,0:T(8,128)}, u32[]{:S(2)}) copy-start(f32[1,2,64,16,128]{4,3,1,2,0:T(8,128)} %copy-done.2) | copy-start | bytes 3145732
  57.5 3.3 %copy-start.7 = (f32[1,2,64,16,128]{4,3,1,2,0:T(8,128)S(1)}, f32[1,2,64,16,128]{4,3,1,2,0:T(8,128)}, u32[]{:S(2)}) copy-start(f32[1,2,64,16,128]{4,3,1,2,0:T(8,128)} %constant.179.clone.1) | copy-start | bytes 3145732
  57.5 3.6 %copy-start.9 = (f32[1,2,64,16,128]{4,3,1,2,0:T(8,128)S(1)}, f32[1,2,64,16,128]{4,3,1,2,0:T(8,128)}, u32[]{:S(2)}) copy-start(f32[1,2,64,16,128]{4,3,1,2,0:T(8,128)} %constant.178.clone.1) | copy-start | bytes 3145732
  63.3 1.2 copy-start.10
  82.2 9.9 %collective-permute-start.2 = (f32[10,2,16,128]{3,2,1,0:T(8,128)S(1)}, f32[10,2,16,128]{3,2,1,0:T(8,128)S(1)}, u32[]{:S(2)}, u32[]{:S(2)}) collective-permute-start(f32[10,2,16,128]{3,2,1,0:T(8,128)S(1)} %constant_dynamic-update-slice_fusion), channel_id=1, source_target_pairs={{0,8},{8,16},{16,24},{24,32},{32,40},{40,48},{48,56},{56,64},{64,7... | collective-permute-start | bytes 491528 | tf_op jit(solution)/shard_map/ppermute | solution.py:12
  85.1 8.3 %collective-permute-start.3 = (f32[10,2,16,128]{3,2,1,0:T(8,128)S(1)}, f32[10,2,16,128]{3,2,1,0:T(8,128)S(1)}, u32[]{:S(2)}, u32[]{:S(2)}) collective-permute-start(f32[10,2,16,128]{3,2,1,0:T(8,128)S(1)} %constant_dynamic-update-slice_fusion), channel_id=1, source_target_pairs={{8,0},{16,8},{24,16},{32,24},{40,32},{48,40},{56,48},{64,56},{72,6... | collective-permute-start | bytes 491528 | tf_op jit(solution)/shard_map/ppermute | solution.py:12
  93.6 9.5 %collective-permute-start.5 = (f32[10,2,16,128]{3,2,1,0:T(8,128)S(1)}, f32[10,2,16,128]{3,2,1,0:T(8,128)S(1)}, u32[]{:S(2)}, u32[]{:S(2)}) collective-permute-start(f32[10,2,16,128]{3,2,1,0:T(8,128)S(1)} %get-tuple-element.196), channel_id=1, source_target_pairs={{16,0},{24,8},{32,16},{40,24},{48,32},{56,40},{64,48},{72,56},{80,... | collective-permute-start | bytes 491528 | tf_op jit(solution)/shard_map/ppermute | solution.py:12
  99.2 9.6 %collective-permute-start.4 = (f32[10,2,16,128]{3,2,1,0:T(8,128)S(1)}, f32[10,2,16,128]{3,2,1,0:T(8,128)S(1)}, u32[]{:S(2)}, u32[]{:S(2)}) collective-permute-start(f32[10,2,16,128]{3,2,1,0:T(8,128)S(1)} %get-tuple-element.196), channel_id=1, source_target_pairs={{0,16},{8,24},{16,32},{24,40},{32,48},{40,56},{48,64},{56,72},{64,... | collective-permute-start | bytes 491528 | tf_op jit(solution)/shard_map/ppermute | solution.py:12
  109.0 4.8 %collective-permute-start.7 = (f32[10,2,16,128]{3,2,1,0:T(8,128)S(1)}, f32[10,2,16,128]{3,2,1,0:T(8,128)S(1)}, u32[]{:S(2)}, u32[]{:S(2)}) collective-permute-start(f32[10,2,16,128]{3,2,1,0:T(8,128)S(1)} %get-tuple-element.149), channel_id=1, source_target_pairs={{32,0},{40,8},{48,16},{56,24},{64,32},{72,40},{80,48},{88,56},{96,... | collective-permute-start | bytes 491528 | tf_op jit(solution)/shard_map/ppermute | solution.py:12
  111.1 8.9 %collective-permute-start.6 = (f32[10,2,16,128]{3,2,1,0:T(8,128)S(1)}, f32[10,2,16,128]{3,2,1,0:T(8,128)S(1)}, u32[]{:S(2)}, u32[]{:S(2)}) collective-permute-start(f32[10,2,16,128]{3,2,1,0:T(8,128)S(1)} %get-tuple-element.149), channel_id=1, source_target_pairs={{0,32},{8,40},{16,48},{24,56},{32,64},{40,72},{48,80},{56,88},{64,... | collective-permute-start | bytes 491528 | tf_op jit(solution)/shard_map/ppermute | solution.py:12
  120.3 4.1 %collective-permute-start.9 = (f32[10,2,16,128]{3,2,1,0:T(8,128)S(1)}, f32[10,2,16,128]{3,2,1,0:T(8,128)S(1)}, u32[]{:S(2)}, u32[]{:S(2)}) collective-permute-start(f32[10,2,16,128]{3,2,1,0:T(8,128)S(1)} %constant_dynamic-update-slice_fusion.30), channel_id=1, source_target_pairs={{64,0},{72,8},{80,16},{88,24},{96,32},{104,40},{112,48},{120,56},{... | collective-permute-start | bytes 491528 | tf_op jit(solution)/shard_map/ppermute | solution.py:12
  121.6 8.7 %collective-permute-start.8 = (f32[10,2,16,128]{3,2,1,0:T(8,128)S(1)}, f32[10,2,16,128]{3,2,1,0:T(8,128)S(1)}, u32[]{:S(2)}, u32[]{:S(2)}) collective-permute-start(f32[10,2,16,128]{3,2,1,0:T(8,128)S(1)} %constant_dynamic-update-slice_fusion.30), channel_id=1, source_target_pairs={{0,64},{8,72},{16,80},{24,88},{32,96},{40,104},{48,112},{56,120},{... | collective-permute-start | bytes 491528 | tf_op jit(solution)/shard_map/ppermute | solution.py:12
  130.4 5.9 %collective-permute-start.11 = (f32[2,16,128]{2,1,0:T(8,128)S(1)}, f32[2,16,128]{2,1,0:T(8,128)S(1)}, u32[]{:S(2)}, u32[]{:S(2)}) collective-permute-start(f32[2,16,128]{2,1,0:T(8,128)S(1)} %multiply_add_fusion), channel_id=1, source_target_pairs={{8,0},{16,8},{24,16},{32,24},{40,32},{48,40},{56,48},{64,56},{72,6... | collective-permute-start | bytes 49160 | tf_op jit(solution)/shard_map/ppermute | solution.py:12
  132.3 7.7 %collective-permute-start.10 = (f32[2,16,128]{2,1,0:T(8,128)S(1)}, f32[2,16,128]{2,1,0:T(8,128)S(1)}, u32[]{:S(2)}, u32[]{:S(2)}) collective-permute-start(f32[2,16,128]{2,1,0:T(8,128)S(1)} %get-tuple-element.62), channel_id=1, source_target_pairs={{0,8},{8,16},{16,24},{24,32},{32,40},{40,48},{48,56},{56,64},{64,7... | collective-permute-start | bytes 49160 | tf_op jit(solution)/shard_map/ppermute | solution.py:12
where the time goes:
time: 143 us; the launch traced here: 142 us
  starting transfers between devices  42.9 us (30%)
  waiting for transfers between devices  36.3 us (25%)
  other arithmetic  36.1 us (25%)
  local copies, waits for them, and re-layouts  25.3 us (18%)
  between operations  1.63 us (1%)
    ppermute x10, waiting for transfers between devices, shifted(): return lax.ppermute(block, axis, route)  27.8 us
    ppermute x10, starting transfers between devices, shifted(): return lax.ppermute(block, axis, route)  27.2 us
    all_to_all x1, waiting for transfers between devices, body(): lax.all_to_all(send_rows.reshape(groups, slot_count, 2 * y_cells), 'gx',...  8.5 us
    slice x11, local copies, waits for them, and re-layouts, push_rows(): kept_rows = lax.slice_in_dim(values, 0, row_total - stride, axis=axis_dim)  7.9 us
    unnamed x38, local copies, waits for them, and re-layouts  7.35 us
    scatter-add x1, other arithmetic, body(): sources = jnp.zeros((cell_total, 2 * y_cells), jnp.float32).at[received_c...  7.02 us
    sub x5, other arithmetic, cyclic_reduce(): rights = rights - left_factor * right_prev - right_factor * right_next  6.4 us
    all_to_all x1, starting transfers between devices, body(): lax.all_to_all(send_rows.reshape(groups, slot_count, 2 * y_cells), 'gx',...  4.8 us
  transfers between devices with their start and end apart: 14, of which 10 were waited for; matrix products, arithmetic and copies ran while one was open for 9% of the time, Pallas kernels for 0%

commit v1 on v0

v1 whole, which is shorter than its diff:
```python
import functools

import jax
import jax.numpy as jnp
from jax import lax
from jax.experimental import pallas as pl
from jax.experimental.pallas import tpu as pltpu
from jax.sharding import PartitionSpec as P

ion_rate = 40.0
HIGHEST = lax.Precision.HIGHEST


def face(lower, upper):
    return 2.0 * lower * upper / (lower + upper)


def local_kernel(rt_ref, ri_ref, ct_ref, ci_ref, src_ref, lo_ref, hi_ref,
                 yt_ref, yi_ref, vt_ref, vi_ref, wt_ref, wi_ref):
    z_cells = rt_ref.shape[0]
    y_cells = rt_ref.shape[2]
    fields = (
        (rt_ref, ct_ref, yt_ref, vt_ref, wt_ref, 0, 1.0),
        (ri_ref, ci_ref, yi_ref, vi_ref, wi_ref, 1, ion_rate),
    )

    def absorb_of(k, z):
        part = src_ref[z, :, k * y_cells:(k + 1) * y_cells]
        return part if k == 0 else ion_rate * part

    carry = []
    for rhs_ref, c_ref, y_ref, v_ref, w_ref, k, _ in fields:
        below = lo_ref[k]
        above = face(c_ref[0], c_ref[1])
        main = 1.0 + below + above + absorb_of(k, 0)
        rp = 1.0 / main
        f = -above * rp
        dy = rhs_ref[0] * rp
        dv = rp
        w_ref[0] = f
        y_ref[0] = dy
        v_ref[0] = dv
        carry += [above, f, dy, dv]

    def fwd(z, carry):
        out = []
        for n, (rhs_ref, c_ref, y_ref, v_ref, w_ref, k, _) in enumerate(fields):
            below, f_prev, dy_prev, dv_prev = carry[4 * n:4 * n + 4]
            above = face(c_ref[z], c_ref[z + 1])
            main = 1.0 + below + above + absorb_of(k, z)
            pivot = main + below * f_prev
            rp = 1.0 / pivot
            f = -above * rp
            dy = (rhs_ref[z] + below * dy_prev) * rp
            dv = (below * dv_prev) * rp
            w_ref[z] = f
            y_ref[z] = dy
            v_ref[z] = dv
            out += [above, f, dy, dv]
        return tuple(out)

    carry = lax.fori_loop(1, z_cells - 1, fwd, tuple(carry), unroll=2)

    z = z_cells - 1
    back = []
    for n, (rhs_ref, c_ref, y_ref, v_ref, w_ref, k, _) in enumerate(fields):
        below, f_prev, dy_prev, dv_prev = carry[4 * n:4 * n + 4]
        above = hi_ref[k]
        main = 1.0 + below + above + absorb_of(k, z)
        pivot = main + below * f_prev
        rp = 1.0 / pivot
        dy = (rhs_ref[z] + below * dy_prev) * rp
        dv = (below * dv_prev) * rp
        y_ref[z] = dy
        v_ref[z] = dv
        w_ref[z] = rp
        back += [dy, dv, rp]

    def bwd(i, back):
        z = z_cells - 2 - i
        out = []
        for n, (rhs_ref, c_ref, y_ref, v_ref, w_ref, k, _) in enumerate(fields):
            y_next, v_next, w_next = back[3 * n:3 * n + 3]
            f = w_ref[z]
            y_val = y_ref[z] - f * y_next
            v_val = v_ref[z] - f * v_next
            w_val = -f * w_next
            y_ref[z] = y_val
            v_ref[z] = v_val
            w_ref[z] = w_val
            out += [y_val, v_val, w_val]
        return tuple(out)

    lax.fori_loop(0, z_cells - 1, bwd, tuple(back), unroll=2)


def local_solve(rhs_temp, rhs_ion, cond_temp, cond_ion, sources, lo, hi):
    shape = jax.ShapeDtypeStruct(rhs_temp.shape, jnp.float32)
    vmem = pl.BlockSpec(memory_space=pltpu.VMEM)
    return pl.pallas_call(
        local_kernel,
        out_shape=(shape,) * 6,
        in_specs=[vmem] * 7,
        out_specs=(vmem,) * 6,
    )(rhs_temp, rhs_ion, cond_temp, cond_ion, sources, lo, hi)


def deposit(bubble_target, bubble_sink, bubble_void, z_cells, x_cells, y_cells):
    cell_total = z_cells * x_cells
    groups = lax.axis_size("gx")
    target = bubble_target[0]
    record_total = target.shape[0]
    slot_count = 3 * record_total // groups
    width = 2 * y_cells
    payload = jnp.concatenate([bubble_sink[0], bubble_void[0]], axis=1)
    destination = target // cell_total
    cell_index = target % cell_total
    same_owner = destination[:, None] == destination[None, :]
    row_ids = lax.broadcasted_iota(jnp.int32, (record_total, record_total), 0)
    col_ids = lax.broadcasted_iota(jnp.int32, (record_total, record_total), 1)
    rank_within = jnp.sum((same_owner & (row_ids > col_ids)).astype(jnp.int32), axis=1)
    slot_index = destination * slot_count + rank_within
    slot_ids = lax.broadcasted_iota(jnp.int32, (groups * slot_count, record_total), 0)
    pick = slot_ids == slot_index[None, :]
    send_rows = jnp.dot(pick.astype(jnp.float32), payload, precision=HIGHEST)
    cell_plus = (cell_index + 1).astype(jnp.float32)
    send_cells = jnp.sum(jnp.where(pick, cell_plus[None, :], 0.0), axis=1) - 1.0
    cell_row = jnp.pad(send_cells.reshape(groups, 1, slot_count), ((0, 0), (0, 0), (0, width - slot_count)))
    send = jnp.concatenate([send_rows.reshape(groups, slot_count, width), cell_row], axis=1)
    received = lax.all_to_all(send, "gx", split_axis=0, concat_axis=0, tiled=True)
    rows = received[:, :slot_count, :].reshape(groups * slot_count, width)
    cells = received[:, slot_count, :slot_count].reshape(groups * slot_count)
    cell_ids = lax.broadcasted_iota(jnp.int32, (cell_total, groups * slot_count), 0).astype(jnp.float32)
    spread = (cell_ids == cells[None, :]).astype(jnp.float32)
    sources = jnp.dot(spread, rows, precision=HIGHEST)
    return sources.reshape(z_cells, x_cells, width)


def body(rhs_temp, rhs_ion, cond_temp, cond_ion, bubble_target, bubble_sink, bubble_void):
    z_cells, x_cells, y_cells = rhs_temp.shape
    chain = lax.axis_size("gz")
    position = lax.axis_index("gz")
    sources = deposit(bubble_target, bubble_sink, bubble_void, z_cells, x_cells, y_cells)

    first = jnp.stack([cond_temp[0], cond_ion[0]])
    last = jnp.stack([cond_temp[-1], cond_ion[-1]])
    from_below = lax.ppermute(last, "gz", [(i, i + 1) for i in range(chain - 1)])
    from_above = lax.ppermute(first, "gz", [(i + 1, i) for i in range(chain - 1)])
    lo = jnp.where(position == 0, 2.0 * first, face(from_below, first))
    hi = jnp.where(position == chain - 1, 0.0, face(last, from_above))

    yt, yi, vt, vi, wt, wi = local_solve(rhs_temp, rhs_ion, cond_temp, cond_ion, sources, lo, hi)
    y = (yt, yi)
    v = (vt, vi)
    w = (wt, wi)
    beta = jnp.where(position == 0, 0.0, lo)
    alpha = hi
    pack = []
    for k in range(2):
        pack += [
            -v[k][0] * beta[k],
            -w[k][0] * alpha[k],
            -v[k][-1] * beta[k],
            -w[k][-1] * alpha[k],
            y[k][0],
            y[k][-1],
        ]
    gathered = lax.all_gather(jnp.stack(pack), "gz")

    outs = []
    for k in range(2):
        a, b, c, e, yf, yl = (gathered[:, 6 * k + m] for m in range(6))
        g1_prev = jnp.zeros_like(a[0])
        zl_prev = jnp.zeros_like(a[0])
        g0s, z0s, g1s, zls = [], [], [], []
        for d in range(chain):
            p = 1.0 - a[d] * g1_prev
            g0 = b[d] / p
            z0 = (yf[d] - a[d] * zl_prev) / p
            t = c[d] * g1_prev
            g1 = e[d] + t * g0
            zl = yl[d] - c[d] * zl_prev + t * z0
            g0s.append(g0)
            z0s.append(z0)
            g1s.append(g1)
            zls.append(zl)
            g1_prev, zl_prev = g1, zl
        f_next = jnp.zeros_like(a[0])
        firsts = [None] * chain
        lasts = [None] * chain
        for d in reversed(range(chain)):
            firsts[d] = z0s[d] - g0s[d] * f_next
            lasts[d] = zls[d] - g1s[d] * f_next
            f_next = firsts[d]
        zero = jnp.zeros_like(a[0])
        last_prev = jnp.stack([zero] + lasts[:-1])[position]
        first_next = jnp.stack(firsts[1:] + [zero])[position]
        outs.append(
            y[k]
            + v[k] * (beta[k] * last_prev)[None]
            + w[k] * (alpha[k] * first_next)[None]
        )
    return tuple(outs)


def solution(mesh):
    in_specs = (
        P("gz", "gx", None),
        P("gz", "gx", None),
        P("gz", "gx", None),
        P("gz", "gx", None),
        P("gz", "gx"),
        P("gz", "gx", None),
        P("gz", "gx", None),
    )
    out_specs = (P("gz", "gx", None), P("gz", "gx", None))
    return jax.shard_map(body, mesh=mesh, in_specs=in_specs, out_specs=out_specs, check_vma=False)
```

time: 143 us -> 109 us (0.76)
  the two profiles are of different devices: /device:TPU:96 before, /device:TPU:0 now
where the time goes in v1:
time: 109 us; the launch traced here: 108 us
  waiting for transfers between devices  54.8 us (50%)
  other arithmetic  15.4 us (14%)
  between operations  14.4 us (13%)
  starting transfers between devices  9.28 us (9%)
  Pallas kernels  5.12 us (5%)
  local copies, waits for them, and re-layouts  4.54 us (4%)
  matrix products  4 us (4%)
    all_gather x1, waiting for transfers between devices, body(): gathered = lax.all_gather(jnp.stack(pack), 'gz')  47.7 us
    unnamed x36, other arithmetic  9.62 us
    pallas_call x1, Pallas kernels, local_solve(): pl.pallas_call(local_kernel, out_shape=(shape,) * 6, in_specs=[vmem] * 7,...  5.12 us
    all_to_all x1, starting transfers between devices, deposit(): lax.all_to_all(send, 'gx', split_axis=0, concat_axis=0, tiled=True)  4.58 us
    ppermute x1, waiting for transfers between devices, body(): lax.ppermute(first, 'gz', [(i + 1, i) for i in range(chain - 1)])  4.33 us
    ppermute x1, starting transfers between devices, body(): lax.ppermute(last, 'gz', [(i, i + 1) for i in range(chain - 1)])  3.38 us
    unnamed x22, local copies, waits for them, and re-layouts  2.85 us
    dot_general x1, matrix products, deposit(): sources = jnp.dot(spread, rows, precision=HIGHEST)  2.51 us
  transfers between devices with their start and end apart: 4, of which 4 were waited for; matrix products, arithmetic and copies ran while one was open for 2% of the time, Pallas kernels for 0%

profile of v1, /device:TPU:0, one launch (start us, length us, event | category | flops | bytes accessed | tf_op | source)
XLA Modules:
  0.0 107.7 jit_solution(10837740623683014526)
XLA Ops:
  7.2 0.7 and_select_fusion.1
  7.9 0.7 and_select_fusion.2
  8.5 0.2 convert_reduce_fusion
  8.7 0.2 select_reduce_fusion
  8.9 0.1 sub.14271
  9.0 1.5 %fusion.4 = f32[768,256]{1,0:T(8,128)S(1)} fusion(s32[256]{0:T(256)S(1)} %bitcast.1973, f32[256,128]{1,0:T(8,128)} %bitcast.1970, f32[256,128]{1,0:T(8,128)} %bitcast.1971), kind=kOutput, calls=%fused_computation.8 | convolution fusion | flops 604241920 | bytes 1049600 | tf_op jit(solution)/shard_map/dot_general | solution.py:125
  10.5 1.0 select_maximum_fusion
  11.5 4.6 %all-to-all-start = ((f32[8,97,256]{2,1,0:T(8,128)}), f32[8,97,256]{2,1,0:T(8,128)S(1)}, u32[]{:S(2)}, u32[]{:S(2)}) async-start(f32[8,97,256]{2,1,0:T(8,128)} %select_maximum_fusion), calls=%async_computation | async-start | bytes 1703936 | tf_op jit(solution)/shard_map/all_to_all | solution.py:130
  16.1 0.0 all-gather.3.cloned.1.call-start
  16.1 0.8 fusion.295
  16.9 1.3 %collective-permute-start.1 = (f32[2,16,128]{2,1,0:T(8,128)S(1)}, f32[2,16,128]{2,1,0:T(8,128)S(1)}, u32[]{:S(2)}, u32[]{:S(2)}) collective-permute-start(f32[2,16,128]{2,1,0:T(8,128)S(1)} %pad_maximum_fusion), channel_id=1, source_target_pairs={{8,0},{16,8},{24,16},{32,24},{40,32},{48,40},{56,48},{64,56},{72,6... | collective-permute-start | bytes 49160 | tf_op jit(solution)/shard_map/ppermute | solution.py:148
  18.2 4.3 %collective-permute-done.1 = f32[2,16,128]{2,1,0:T(8,128)S(1)} collective-permute-done((f32[2,16,128]{2,1,0:T(8,128)S(1)}, f32[2,16,128]{2,1,0:T(8,128)S(1)}, u32[]{:S(2)}, u32[]{:S(2)}) %collective-permute-start.1) | collective-permute-done | bytes 16416 | tf_op jit(solution)/shard_map/ppermute | solution.py:148
  22.5 0.6 divide_select_fusion
  23.1 3.4 %collective-permute-start = (f32[2,16,128]{2,1,0:T(8,128)S(1)}, f32[2,16,128]{2,1,0:T(8,128)S(1)}, u32[]{:S(2)}, u32[]{:S(2)}) collective-permute-start(f32[2,16,128]{2,1,0:T(8,128)S(1)} %get-tuple-element.119), channel_id=1, source_target_pairs={{0,8},{8,16},{16,24},{24,32},{32,40},{40,48},{48,56},{56,64},{64,7... | collective-permute-start | bytes 49160 | tf_op jit(solution)/shard_map/ppermute | solution.py:147
  26.5 1.4 %collective-permute-done = f32[2,16,128]{2,1,0:T(8,128)S(1)} collective-permute-done((f32[2,16,128]{2,1,0:T(8,128)S(1)}, f32[2,16,128]{2,1,0:T(8,128)S(1)}, u32[]{:S(2)}, u32[]{:S(2)}) %collective-permute-start) | collective-permute-done | bytes 16416 | tf_op jit(solution)/shard_map/ppermute | solution.py:147
  27.9 0.6 broadcast_select_fusion
  28.6 1.4 %all-to-all-done = f32[8,97,256]{2,1,0:T(8,128)S(1)} async-done(((f32[8,97,256]{2,1,0:T(8,128)}), f32[8,97,256]{2,1,0:T(8,128)S(1)}, u32[]{:S(2)}, u32[]{:S(2)}) %all-to-all-start) | async-done | bytes 794656 | tf_op jit(solution)/shard_map/all_to_all | solution.py:130
  29.9 0.1 eq.56
  30.0 0.1 slice.1287
  30.1 2.5 %fusion.src_ref = f32[64,16,256]{2,1,0:T(8,128)} fusion(f32[768,256,1]{1,0,2:T(8,128)S(1)} %bitcast.1969, f32[768]{0:T(1024)S(1)} %eq.56, f32[64,16]{1,0:T(8,128)S(1)} %add_convert_fusion), kind=kOutput, calls=%fused_computation | convolution fusion | flops 2416705536 | bytes 1842176 | tf_op jit(solution)/shard_map/dot_general | solution.py:135
  32.6 0.0 copy-start.6
  32.6 5.1 %shard_map.86 = (f32[64,16,128]{2,1,0:T(8,128)}, f32[64,16,128]{2,1,0:T(8,128)}, f32[64,16,128]{2,1,0:T(8,128)}, f32[64,16,128]{2,1,0:T(8,128)}, f32[64,16,128]{2,1,0:T(8,128)}, /*index=5*/f32[64,16,128]{2,1,0:T(8,128)}) custom-call(f32[64,16,128]{2,1,0:T(8,128)} %rt_ref.1, f32[64,16,128]{2,1,0:T(8,128)} %ri_ref.1, f32[64,16,128]{2,1,0:T(8,128)} %ct_ref.1, ...), custom_call_target="tpu_custom_call" | custom-call | tf_op jit(solution)/shard_map/pallas_call | solution.py:100
  37.7 0.7 constant_dynamic-update-slice_fusion.11
  38.4 0.0 copy-done.6
  38.4 0.7 constant_dynamic-update-slice_fusion.10
  39.1 0.7 constant_dynamic-update-slice_fusion.9
  39.8 0.7 constant_dynamic-update-slice_fusion.8
  40.5 0.7 constant_dynamic-update-slice_fusion.7
  41.2 0.7 constant_dynamic-update-slice_fusion.6
  41.9 0.7 constant_dynamic-update-slice_fusion.5
  42.6 0.7 constant_dynamic-update-slice_fusion.4
  43.3 0.7 constant_dynamic-update-slice_fusion.3
  44.0 0.7 constant_dynamic-update-slice_fusion.2
  44.7 0.7 constant_dynamic-update-slice_fusion.1
  45.4 0.7 constant_dynamic-update-slice_fusion
  46.1 0.0 copy-start.7
  46.1 0.6 copy-done.7
  46.7 0.0 all-gather.3.cloned.1.call-update
  46.8 47.7 %all-gather.3.cloned.1.call-done = f32[192,16,128]{2,1,0:T(8,128)} async-done(((f32[12,16,128]{2,1,0:T(8,128)}), f32[192,16,128]{2,1,0:T(8,128)}) %all-gather.3.cloned.1.call-update) | async-done | bytes 1572880 | tf_op jit(solution)/shard_map/all_gather | solution.py:168
  94.5 1.5 %constant_dynamic-update-slice_fusion.58 = (f32[16,16,128]{2,1,0:T(8,128)S(1)}, f32[1,16,128]{2,1,0:T(8,128)S(1)}, f32[1,16,128]{2,1,0:T(8,128)S(1)}, f32[1,16,1...) fusion(f32[16,16,128]{2,1,0:T(8,128)S(1)} %constant_dynamic-upd, ...), kind=kLoop, calls=%fused_computation.76 | loop fusion | flops 473088 | bytes 1130496
  96.0 0.0 copy-start.3
  96.0 0.0 copy-start.4
  96.0 0.0 copy-start.5
  96.0 1.6 %constant_dynamic-update-slice_fusion.26 = (f32[16,16,128]{2,1,0:T(8,128)S(1)}, f32[1,16,128]{2,1,0:T(8,128)S(1)}, f32[1,16,128]{2,1,0:T(8,128)S(1)}, f32[1,16,1...) fusion(f32[16,16,128]{2,1,0:T(8,128)S(1)} %constant_dynamic-upd, ...), kind=kLoop, calls=%fused_computation.44 | loop fusion | flops 473088 | bytes 1130496
  97.6 0.8 constant_dynamic-update-slice_fusion.75
  98.6 0.0 copy-start
  98.6 0.0 copy-start.1
  98.6 0.0 copy-start.2
  98.9 0.0 copy-done.3
  98.9 0.0 copy-done.4
  98.9 0.0 copy-done.5
  98.9 0.9 multiply_add_fusion.1
  99.8 0.0 copy-done
  99.8 0.0 copy-done.1
  99.8 0.1 copy-done.2
  99.9 0.9 multiply_add_fusion
  (39 shorter events, 0.3 us)
Async XLA Ops:
  11.5 18.4 %all-to-all-start = ((f32[8,97,256]{2,1,0:T(8,128)}), f32[8,97,256]{2,1,0:T(8,128)S(1)}, u32[]{:S(2)}, u32[]{:S(2)}) async-start(f32[8,97,256]{2,1,0:T(8,128)} %select_maximum_fusion), calls=%async_computation | async-start | bytes 1703936 | tf_op jit(solution)/shard_map/all_to_all | solution.py:130
  16.1 78.4 %all-gather.3.cloned.1.call-start = ((), (), s32[]{:S(2)}) async-start(), calls=%async_computation.1 | async-start | bytes 1671168 | tf_op jit(solution)/shard_map/all_gather | solution.py:168
  16.9 5.6 %collective-permute-start.1 = (f32[2,16,128]{2,1,0:T(8,128)S(1)}, f32[2,16,128]{2,1,0:T(8,128)S(1)}, u32[]{:S(2)}, u32[]{:S(2)}) collective-permute-start(f32[2,16,128]{2,1,0:T(8,128)S(1)} %pad_maximum_fusion), channel_id=1, source_target_pairs={{8,0},{16,8},{24,16},{32,24},{40,32},{48,40},{56,48},{64,56},{72,6... | collective-permute-start | bytes 49160 | tf_op jit(solution)/shard_map/ppermute | solution.py:148
  23.1 4.8 %collective-permute-start = (f32[2,16,128]{2,1,0:T(8,128)S(1)}, f32[2,16,128]{2,1,0:T(8,128)S(1)}, u32[]{:S(2)}, u32[]{:S(2)}) collective-permute-start(f32[2,16,128]{2,1,0:T(8,128)S(1)} %get-tuple-element.119), channel_id=1, source_target_pairs={{0,8},{8,16},{16,24},{24,32},{32,40},{40,48},{48,56},{56,64},{64,7... | collective-permute-start | bytes 49160 | tf_op jit(solution)/shard_map/ppermute | solution.py:147
  32.6 5.8 %copy-start.6 = (f32[2,16,128]{2,1,0:T(8,128)S(1)}, f32[2,16,128]{2,1,0:T(8,128)}, u32[]{:S(2)}) copy-start(f32[2,16,128]{2,1,0:T(8,128)} %get-tuple-element.118.hi_ref) | copy-start | bytes 49156
  46.1 0.6 copy-start.7
  96.0 2.9 %copy-start.3 = (f32[64,16,128]{2,1,0:T(8,128)S(1)}, f32[64,16,128]{2,1,0:T(8,128)}, u32[]{:S(2)}) copy-start(f32[64,16,128]{2,1,0:T(8,128)} %get-tuple-element.8) | copy-start | bytes 1572868
  96.0 2.9 %copy-start.4 = (f32[64,16,128]{2,1,0:T(8,128)S(1)}, f32[64,16,128]{2,1,0:T(8,128)}, u32[]{:S(2)}) copy-start(f32[64,16,128]{2,1,0:T(8,128)} %get-tuple-element.9) | copy-start | bytes 1572868
  96.0 2.9 %copy-start.5 = (f32[64,16,128]{2,1,0:T(8,128)S(1)}, f32[64,16,128]{2,1,0:T(8,128)}, u32[]{:S(2)}) copy-start(f32[64,16,128]{2,1,0:T(8,128)} %get-tuple-element.10) | copy-start | bytes 1572868
  98.6 1.3 %copy-start = (f32[64,16,128]{2,1,0:T(8,128)S(1)}, f32[64,16,128]{2,1,0:T(8,128)}, u32[]{:S(2)}) copy-start(f32[64,16,128]{2,1,0:T(8,128)} %get-tuple-element.13) | copy-start | bytes 1572868
  98.6 1.3 %copy-start.1 = (f32[64,16,128]{2,1,0:T(8,128)S(1)}, f32[64,16,128]{2,1,0:T(8,128)}, u32[]{:S(2)}) copy-start(f32[64,16,128]{2,1,0:T(8,128)} %get-tuple-element.11) | copy-start | bytes 1572868
  98.6 1.3 %copy-start.2 = (f32[64,16,128]{2,1,0:T(8,128)S(1)}, f32[64,16,128]{2,1,0:T(8,128)}, u32[]{:S(2)}) copy-start(f32[64,16,128]{2,1,0:T(8,128)} %get-tuple-element.12) | copy-start | bytes 1572868
Sparse Core Ops, SparseCore 0:
  46.9 47.5 all-gather.2

commit v2 on v1

--- a/solution.py
+++ b/solution.py
@@ -15,8 +15,8 @@
     return 2.0 * lower * upper / (lower + upper)
 
 
-def local_kernel(rt_ref, ri_ref, ct_ref, ci_ref, src_ref, lo_ref, hi_ref,
-                 yt_ref, yi_ref, vt_ref, vi_ref, wt_ref, wi_ref):
+def local_kernel(rt_ref, ri_ref, ct_ref, ci_ref, src_ref, lo_ref, hi_ref, beta_ref,
+                 yt_ref, yi_ref, vt_ref, vi_ref, wt_ref, wi_ref, pack_ref):
     z_cells = rt_ref.shape[0]
     y_cells = rt_ref.shape[2]
     fields = (
@@ -91,18 +91,90 @@
             out += [y_val, v_val, w_val]
         return tuple(out)
 
-    lax.fori_loop(0, z_cells - 1, bwd, tuple(back), unroll=2)
-
-
-def local_solve(rhs_temp, rhs_ion, cond_temp, cond_ion, sources, lo, hi):
+    back = lax.fori_loop(0, z_cells - 1, bwd, tuple(back), unroll=2)
+    for n, (rhs_ref, c_ref, y_ref, v_ref, w_ref, k, _) in enumerate(fields):
+        y_first, v_first, w_first = back[3 * n:3 * n + 3]
+        beta = beta_ref[k]
+        alpha = hi_ref[k]
+        pack_ref[0, k] = -v_first * beta
+        pack_ref[1, k] = -w_first * alpha
+        pack_ref[2, k] = -v_ref[z_cells - 1] * beta
+        pack_ref[3, k] = -w_ref[z_cells - 1] * alpha
+        pack_ref[4, k] = y_first
+        pack_ref[5, k] = y_ref[z_cells - 1]
+
+
+def local_solve(rhs_temp, rhs_ion, cond_temp, cond_ion, sources, lo, hi, beta):
     shape = jax.ShapeDtypeStruct(rhs_temp.shape, jnp.float32)
+    pack = jax.ShapeDtypeStruct((6,) + lo.shape, jnp.float32)
     vmem = pl.BlockSpec(memory_space=pltpu.VMEM)
     return pl.pallas_call(
         local_kernel,
-        out_shape=(shape,) * 6,
-        in_specs=[vmem] * 7,
-        out_specs=(vmem,) * 6,
-    )(rhs_temp, rhs_ion, cond_temp, cond_ion, sources, lo, hi)
+        out_shape=(shape,) * 6 + (pack,),
+        in_specs=[vmem] * 8,
+        out_specs=(vmem,) * 7,
+    )(rhs_temp, rhs_ion, cond_temp, cond_ion, sources, lo, hi, beta)
+
+
+def chain_solve(packs, rights):
+    count = len(packs)
+    g1_prev = None
+    zl_prev = None
+    steps = []
+    for i in range(count):
+        a, b, c, e = packs[i]
+        if g1_prev is None:
+            z0 = [yf for yf, yl in rights[i]]
+            zl = [yl for yf, yl in rights[i]]
+            g0 = b
+            g1 = e
+        else:
+            p = 1.0 - a * g1_prev
+            rp = 1.0 / p
+            g0 = b * rp
+            t = c * g1_prev
+            g1 = e + t * g0
+            z0 = [(yf - a * zp) * rp for (yf, yl), zp in zip(rights[i], zl_prev)]
+            zl = [yl - c * zp + t * z for (yf, yl), zp, z in zip(rights[i], zl_prev, z0)]
+        steps.append((g0, g1, z0, zl))
+        g1_prev, zl_prev = g1, zl
+    firsts = [None] * count
+    lasts = [None] * count
+    f_next = None
+    for i in reversed(range(count)):
+        g0, g1, z0, zl = steps[i]
+        if f_next is None:
+            firsts[i], lasts[i] = z0, zl
+        else:
+            firsts[i] = [z - g0 * f for z, f in zip(z0, f_next)]
+            lasts[i] = [z - g1 * f for z, f in zip(zl, f_next)]
+        f_next = firsts[i]
+    return firsts, lasts
+
+
+def gather_ring(pack, size, stride, index):
+    chain = lax.axis_size("gz")
+    got = {0: pack}
+    for s in range(1, size):
+        route = []
+        for i in range(chain):
+            base = i - (i // stride % size) * stride
+            route.append((i, base + ((i // stride + s) % size) * stride))
+        got[s] = lax.ppermute(pack, "gz", route)
+    ordered = []
+    for member in range(size):
+        pick = got[0]
+        for s in range(1, size):
+            pick = jnp.where((index - member) % size == s, got[s], pick)
+        ordered.append(pick)
+    return ordered
+
+
+def select(values, index):
+    out = jnp.zeros_like(values[0])
+    for i, value in enumerate(values):
+        out = jnp.where(index == i, value, out)
+    return out
 
 
 def deposit(bubble_target, bubble_sink, bubble_void, z_cells, x_cells, y_cells):
@@ -149,56 +221,59 @@
     lo = jnp.where(position == 0, 2.0 * first, face(from_below, first))
     hi = jnp.where(position == chain - 1, 0.0, face(last, from_above))
 
-    yt, yi, vt, vi, wt, wi = local_solve(rhs_temp, rhs_ion, cond_temp, cond_ion, sources, lo, hi)
+    beta = jnp.where(position == 0, 0.0, lo)
+    alpha = hi
+    yt, yi, vt, vi, wt, wi, pack = local_solve(
+        rhs_temp, rhs_ion, cond_temp, cond_ion, sources, lo, hi, beta
+    )
+    size = 4 if chain % 4 == 0 and chain > 4 else chain
+    groups_z = chain // size
+    member = position % size
+    group = position // size
+    zero = jnp.zeros_like(lo)
+
+    members = gather_ring(pack, size, 1, member)
+    packs, rights = [], []
+    for r, m in enumerate(members):
+        a, b, c, e, yf, yl = (m[j] for j in range(6))
+        right_sets = [(yf, yl), (zero, zero), (zero, zero)]
+        if r == 0:
+            right_sets[1] = (-a, -c)
+            a, c = zero, zero
+        if r == size - 1:
+            right_sets[2] = (-b, -e)
+            b, e = zero, zero
+        packs.append((a, b, c, e))
+        rights.append(right_sets)
+    firsts, lasts = chain_solve(packs, rights)
+    if groups_z > 1:
+        group_pack = jnp.stack([
+            -firsts[0][1], -firsts[0][2], -lasts[-1][1], -lasts[-1][2], firsts[0][0], lasts[-1][0]
+        ])
+        tops = gather_ring(group_pack, groups_z, size, group)
+        gpacks = [(t[0], t[1], t[2], t[3]) for t in tops]
+        grights = [[(t[4], t[5])] for t in tops]
+        gfirsts, glasts = chain_solve(gpacks, grights)
+        outside_low = select([zero] + [l[0] for l in glasts[:-1]], group)
+        outside_high = select([f[0] for f in gfirsts[1:]] + [zero], group)
+    else:
+        outside_low = zero
+        outside_high = zero
+
+    def value(parts):
+        return parts[0] + outside_low * parts[1] + outside_high * parts[2]
+
+    last_prev = select([outside_low] + [value(l) for l in lasts[:-1]], member)
+    first_next = select([value(f) for f in firsts[1:]] + [outside_high], member)
     y = (yt, yi)
     v = (vt, vi)
     w = (wt, wi)
-    beta = jnp.where(position == 0, 0.0, lo)
-    alpha = hi
-    pack = []
-    for k in range(2):
-        pack += [
-            -v[k][0] * beta[k],
-            -w[k][0] * alpha[k],
-            -v[k][-1] * beta[k],
-            -w[k][-1] * alpha[k],
-            y[k][0],
-            y[k][-1],
-        ]
-    gathered = lax.all_gather(jnp.stack(pack), "gz")
-
     outs = []
     for k in range(2):
-        a, b, c, e, yf, yl = (gathered[:, 6 * k + m] for m in range(6))
-        g1_prev = jnp.zeros_like(a[0])
-        zl_prev = jnp.zeros_like(a[0])
-        g0s, z0s, g1s, zls = [], [], [], []
-        for d in range(chain):
-            p = 1.0 - a[d] * g1_prev
-            g0 = b[d] / p
-            z0 = (yf[d] - a[d] * zl_prev) / p
-            t = c[d] * g1_prev
-            g1 = e[d] + t * g0
-            zl = yl[d] - c[d] * zl_prev + t * z0
-            g0s.append(g0)
-            z0s.append(z0)
-            g1s.append(g1)
-            zls.append(zl)
-            g1_prev, zl_prev = g1, zl
-        f_next = jnp.zeros_like(a[0])
-        firsts = [None] * chain
-        lasts = [None] * chain
-        for d in reversed(range(chain)):
-            firsts[d] = z0s[d] - g0s[d] * f_next
-            lasts[d] = zls[d] - g1s[d] * f_next
-            f_next = firsts[d]
-        zero = jnp.zeros_like(a[0])
-        last_prev = jnp.stack([zero] + lasts[:-1])[position]
-        first_next = jnp.stack(firsts[1:] + [zero])[position]
         outs.append(
             y[k]
-            + v[k] * (beta[k] * last_prev)[None]
-            + w[k] * (alpha[k] * first_next)[None]
+            + v[k] * (beta[k] * last_prev[k])[None]
+            + w[k] * (alpha[k] * first_next[k])[None]
         )
     return tuple(outs)
 

time: 109 us -> 57.5 us (0.53)
  waiting for transfers between devices: 54.8 us -> 18.4 us
  between operations: 14.4 us -> 0.91 us
  starting transfers between devices: 9.28 us -> 19.8 us
  other arithmetic: 15.4 us -> 7.17 us
  local copies, waits for them, and re-layouts: 4.54 us -> 1.63 us
    all_gather x1 -> x0, waiting for transfers between devices: 47.7 us -> none  [body(): gathered = lax.all_gather(jnp.stack(pack), 'gz')]
    ppermute x0 -> x6, waiting for transfers between devices: none -> 11.3 us  [gather_ring(): got[s] = lax.ppermute(pack, 'gz', route)]
    ppermute x0 -> x6, starting transfers between devices: none -> 10.6 us  [gather_ring(): got[s] = lax.ppermute(pack, 'gz', route)]
    unnamed x36 -> x5, other arithmetic: 9.62 us -> 0.14 us
    unnamed x22 -> x16, local copies, waits for them, and re-layouts: 2.85 us -> 0.65 us
    select_n x0 -> x4, other arithmetic: none -> 1.19 us  [the longest x2 1 us: gather_ring(): pick = jnp.where((index - member) % size == s, got[s], pick)]
  transfers between devices with their start and end apart: 4 -> 9, of which waited for: 4 -> 9; matrix products, arithmetic and copies ran while one was open for 2% -> 3% of each run, Pallas kernels for 0% -> 0%
where the time goes in v2:
time: 57.5 us; the launch traced here: 57.2 us
  starting transfers between devices  19.8 us (34%)
  waiting for transfers between devices  18.4 us (32%)
  other arithmetic  7.17 us (12%)
  Pallas kernels  5.15 us (9%)
  matrix products  4.03 us (7%)
  local copies, waits for them, and re-layouts  1.63 us (3%)
  between operations  0.91 us (2%)
    ppermute x6, waiting for transfers between devices, gather_ring(): got[s] = lax.ppermute(pack, 'gz', route)  11.3 us
    ppermute x6, starting transfers between devices, gather_ring(): got[s] = lax.ppermute(pack, 'gz', route)  10.6 us
    pallas_call x1, Pallas kernels, local_solve(): pl.pallas_call(local_kernel, out_shape=(shape,) * 6 + (pack,), in_specs=[...  5.15 us
    all_to_all x1, starting transfers between devices, deposit(): lax.all_to_all(send, 'gx', split_axis=0, concat_axis=0, tiled=True)  4.58 us
    ppermute x1, waiting for transfers between devices, body(): lax.ppermute(first, 'gz', [(i + 1, i) for i in range(chain - 1)])  4.33 us
    ppermute x1, starting transfers between devices, body(): lax.ppermute(last, 'gz', [(i, i + 1) for i in range(chain - 1)])  3.38 us
    dot_general x1, matrix products, deposit(): sources = jnp.dot(spread, rows, precision=HIGHEST)  2.54 us
    add x2, other arithmetic, body(): y[k] + v[k] * (beta[k] * last_prev[k])[None]  1.79 us
  transfers between devices with their start and end apart: 9, of which 9 were waited for; matrix products, arithmetic and copies ran while one was open for 3% of the time, Pallas kernels for 0%

profile of v2, /device:TPU:0, one launch (start us, length us, event | category | flops | bytes accessed | tf_op | source)
XLA Modules:
  0.0 57.2 jit_solution(11394424441534022267)
XLA Ops:
  0.6 0.7 %and_select_fusion.1 = (s32[1,256]{1,0:T(1,128)S(1)}, s32[1,256]{1,0:T(1,128)S(1)}) fusion(s32[1,256]{1,0:T(1,128)} %param.11), kind=kLoop, calls=%fused_computation.203 | loop fusion | flops 3840 | bytes 3072 | tf_op jit(solution)/shard_map/jit(floor_divide)/jit(_where)/select_n | solution.py:188
  1.3 0.7 %and_select_fusion.2 = s32[256]{0:T(256)S(1)} fusion(s32[256]{0:T(256)} %bitcast.613), kind=kLoop, calls=%fused_computation.208 | loop fusion | flops 3840 | bytes 2048 | tf_op jit(solution)/shard_map/jit(floor_divide)/jit(_where)/select_n | solution.py:188
  2.0 0.2 convert_reduce_fusion
  2.2 0.2 select_reduce_fusion
  2.4 0.1 sub.315
  2.5 1.5 %fusion.4 = f32[768,256]{1,0:T(8,128)S(1)} fusion(s32[256]{0:T(256)S(1)} %bitcast.610, f32[256,128]{1,0:T(8,128)} %bitcast.607, f32[256,128]{1,0:T(8,128)} %bitcast.608), kind=kOutput, calls=%fused_computation.8 | convolution fusion | flops 604241920 | bytes 1049600 | tf_op jit(solution)/shard_map/dot_general | solution.py:197
  4.0 1.0 %select_maximum_fusion = f32[8,97,256]{2,1,0:T(8,128)} fusion(f32[8,1,96]{2,1,0:T(1,128)S(1)} %sub.315, f32[8,96,256]{2,1,0:T(8,128)S(1)} %bitcast.605), kind=kLoop, calls=%fused_computation.4 | loop fusion | flops 595968 | bytes 1584128 | tf_op jit(solution)/shard_map/concatenate | solution.py:201
  5.0 4.6 %all-to-all-start = ((f32[8,97,256]{2,1,0:T(8,128)}), f32[8,97,256]{2,1,0:T(8,128)S(1)}, u32[]{:S(2)}, u32[]{:S(2)}) async-start(f32[8,97,256]{2,1,0:T(8,128)} %select_maximum_fusion), calls=%async_computation | async-start | bytes 1703936 | tf_op jit(solution)/shard_map/all_to_all | solution.py:202
  9.6 0.7 %fusion.87 = (f32[1,16,128]{2,1,0:T(8,128)S(1)}, f32[1,16,128]{2,1,0:T(8,128)S(1)}, f32[1,16,128]{2,1,0:T(8,128)S(1)}, f32[1,16,128]{2,1,0:T(8,128)S(1)}) fusion(f32[64,16,128]{2,1,0:T(8,128)} %ct_ref.1, f32[64,16,128]{2,1,0:T(8,128)} %ci_ref.1), kind=kLoop, calls=%fused_computation.216 | loop fusion | bytes 65536 | tf_op jit(solution)/shard_map/slice | solution.py:217
  10.3 1.3 %collective-permute-start.1 = (f32[2,16,128]{2,1,0:T(8,128)S(1)}, f32[2,16,128]{2,1,0:T(8,128)S(1)}, u32[]{:S(2)}, u32[]{:S(2)}) collective-permute-start(f32[2,16,128]{2,1,0:T(8,128)S(1)} %pad_maximum_fusion), channel_id=1, source_target_pairs={{8,0},{16,8},{24,16},{32,24},{40,32},{48,40},{56,48},{64,56},{72,6... | collective-permute-start | bytes 49160 | tf_op jit(solution)/shard_map/ppermute | solution.py:220
  11.6 4.3 %collective-permute-done.1 = f32[2,16,128]{2,1,0:T(8,128)S(1)} collective-permute-done((f32[2,16,128]{2,1,0:T(8,128)S(1)}, f32[2,16,128]{2,1,0:T(8,128)S(1)}, u32[]{:S(2)}, u32[]{:S(2)}) %collective-permute-start.1) | collective-permute-done | bytes 16416 | tf_op jit(solution)/shard_map/ppermute | solution.py:220
  15.9 0.6 %divide_select_fusion = (f32[2,16,128]{2,1,0:T(8,128)}, f32[2,16,128]{2,1,0:T(8,128)S(1)}) fusion(f32[2,16,128]{2,1,0:T(8,128)S(1)} %collective-permute-done.1, pred[]{:T(512)S(6)} %eq.190, f32[1,16,128]{2,1,0:T(8,128)S(1)} %get-tuple-element.59, f32[1,16,128]{2,1,0:T(8,128)S(1)} %get-tuple-element.40), kind=kLoop, calls=%fused_computation.183 | loop fusion | flops 24576 | bytes 65537 | tf_op jit(solution)/shard_map/jit(_where)/select_n | solution.py:222
  16.5 3.4 %collective-permute-start = (f32[2,16,128]{2,1,0:T(8,128)S(1)}, f32[2,16,128]{2,1,0:T(8,128)S(1)}, u32[]{:S(2)}, u32[]{:S(2)}) collective-permute-start(f32[2,16,128]{2,1,0:T(8,128)S(1)} %get-tuple-element.56), channel_id=1, source_target_pairs={{0,8},{8,16},{16,24},{24,32},{32,40},{40,48},{48,56},{56,64},{64,7... | collective-permute-start | bytes 49160 | tf_op jit(solution)/shard_map/ppermute | solution.py:219
  20.0 1.4 %collective-permute-done = f32[2,16,128]{2,1,0:T(8,128)S(1)} collective-permute-done((f32[2,16,128]{2,1,0:T(8,128)S(1)}, f32[2,16,128]{2,1,0:T(8,128)S(1)}, u32[]{:S(2)}, u32[]{:S(2)}) %collective-permute-start) | collective-permute-done | bytes 16416 | tf_op jit(solution)/shard_map/ppermute | solution.py:219
  21.4 0.6 %broadcast_select_fusion = (f32[2,16,128]{2,1,0:T(8,128)}, f32[2,16,128]{2,1,0:T(8,128)}) fusion(pred[]{:T(512)S(6)} %eq.189, f32[2,16,128]{2,1,0:T(8,128)S(1)} %collective-permute-done, f32[1,16,128]{2,1,0:T(8,128)S(1)} %get-tuple-element.60, f32[1,16,128]{2,1,0:T(8,128)S(1)} %get-tuple-element.39), kind=kLoop, calls=%fused_computation.200 | loop fusion | flops 32768 | bytes 65537 | tf_op jit(solution)/shard_map/jit(_where)/select_n | solution.py:224
  22.0 1.4 %all-to-all-done = f32[8,97,256]{2,1,0:T(8,128)S(1)} async-done(((f32[8,97,256]{2,1,0:T(8,128)}), f32[8,97,256]{2,1,0:T(8,128)S(1)}, u32[]{:S(2)}, u32[]{:S(2)}) %all-to-all-start) | async-done | bytes 794656 | tf_op jit(solution)/shard_map/all_to_all | solution.py:202
  23.4 0.1 eq.186
  23.5 0.1 slice.217
  23.5 2.5 %fusion.src_ref = f32[64,16,256]{2,1,0:T(8,128)} fusion(f32[768,256,1]{1,0,2:T(8,128)S(1)} %bitcast.606, f32[768]{0:T(1024)S(1)} %eq.186, f32[64,16]{1,0:T(8,128)S(1)} %add_convert_fusion), kind=kOutput, calls=%fused_computation | convolution fusion | flops 2416705536 | bytes 1842176 | tf_op jit(solution)/shard_map/dot_general | solution.py:207
  26.1 5.1 %shard_map.86 = (f32[64,16,128]{2,1,0:T(8,128)}, f32[64,16,128]{2,1,0:T(8,128)}, f32[64,16,128]{2,1,0:T(8,128)}, f32[64,16,128]{2,1,0:T(8,128)}, f32[64,16,128]{...) custom-call(f32[64,16,128]{2,1,0:T(8,128)} %rt_ref.1, f32[64,16,128]{2,1,0:T(8,128)} %ri_ref.1, ...), custom_call_target="tpu_custom_call" | custom-call | tf_op jit(solution)/shard_map/pallas_call | solution.py:111
  31.2 4.3 %collective-permute-start.2 = (f32[6,2,16,128]{3,2,1,0:T(8,128)}, f32[6,2,16,128]{3,2,1,0:T(8,128)S(1)}, u32[]{:S(2)}, u32[]{:S(2)}) collective-permute-start(f32[6,2,16,128]{3,2,1,0:T(8,128)} %get-tuple-element.11), channel_id=1, source_target_pairs={{0,24},{8,0},{16,8},{24,16},{32,56},{40,32},{48,40},{56,48},{64,88... | collective-permute-start | bytes 294920 | tf_op jit(solution)/shard_map/ppermute | solution.py:163
  35.5 0.0 collective-permute-start.3
  35.5 0.9 %collective-permute-start.4 = (f32[6,2,16,128]{3,2,1,0:T(8,128)}, f32[6,2,16,128]{3,2,1,0:T(8,128)S(1)}, u32[]{:S(2)}, u32[]{:S(2)}) collective-permute-start(f32[6,2,16,128]{3,2,1,0:T(8,128)} %get-tuple-element.11), channel_id=1, source_target_pairs={{0,8},{8,16},{16,24},{24,0},{32,40},{40,48},{48,56},{56,32},{64,72... | collective-permute-start | bytes 294920 | tf_op jit(solution)/shard_map/ppermute | solution.py:163
  36.5 2.6 %collective-permute-done.2 = f32[6,2,16,128]{3,2,1,0:T(8,128)S(1)} collective-permute-done((f32[6,2,16,128]{3,2,1,0:T(8,128)}, f32[6,2,16,128]{3,2,1,0:T(8,128)S(1)}, u32[]{:S(2)}, u32[]{:S(2)}) %collective-permute-start.2) | collective-permute-done | bytes 98336 | tf_op jit(solution)/shard_map/ppermute | solution.py:163
  39.1 2.9 %collective-permute-done.3 = f32[6,2,16,128]{3,2,1,0:T(8,128)S(1)} collective-permute-done((f32[6,2,16,128]{3,2,1,0:T(8,128)}, f32[6,2,16,128]{3,2,1,0:T(8,128)S(1)}, u32[]{:S(2)}, u32[]{:S(2)}) %collective-permute-start.3) | collective-permute-done | bytes 98336 | tf_op jit(solution)/shard_map/ppermute | solution.py:163
  41.9 0.7 %collective-permute-done.4 = f32[6,2,16,128]{3,2,1,0:T(8,128)S(1)} collective-permute-done((f32[6,2,16,128]{3,2,1,0:T(8,128)}, f32[6,2,16,128]{3,2,1,0:T(8,128)S(1)}, u32[]{:S(2)}, u32[]{:S(2)}) %collective-permute-start.4) | collective-permute-done | bytes 98336 | tf_op jit(solution)/shard_map/ppermute | solution.py:163
  42.6 0.9 %select_select_fusion.6 = (f32[6,2,16,128]{3,2,1,0:T(8,128)S(1)}, f32[6,2,16,128]{3,2,1,0:T(8,128)S(1)}, f32[6,2,16,128]{3,2,1,0:T(8,128)S(1)}, f32[6,2,16,128]{3,2,1,0:T(8,128)S(1)}) fusion(f32[6,2,16,128]{3,2,1,0:T(8,128)S(1)} %collective-permute-done.2, f32[6,2,16,128]{3,2,1,0:T(8,128)S(1)} %collective-permute-done.3, ...), kind=kLoop, calls=%fused_computation.24 | loop fusion | flops 294912 | bytes 786444 | tf_op jit(solution)/shard_map/jit(_where)/select_n | solution.py:168
  43.7 0.0 copy-start.7
  43.8 0.0 copy-start.6
  43.8 0.0 copy-start.3
  43.8 0.0 copy-start.4
  43.8 0.0 copy-start.5
  43.8 3.3 %collective-permute-start.5 = (f32[6,2,16,128]{3,2,1,0:T(8,128)S(1)}, f32[6,2,16,128]{3,2,1,0:T(8,128)S(1)}, u32[]{:S(2)}, u32[]{:S(2)}) collective-permute-start(f32[6,2,16,128]{3,2,1,0:T(8,128)S(1)} %fusion.25), channel_id=1, source_target_pairs={{0,96},{8,104},{16,112},{24,120},{32,0},{40,8},{48,16},{56,24},{64... | collective-permute-start | bytes 294920 | tf_op jit(solution)/shard_map/ppermute | solution.py:163
  47.1 0.8 %collective-permute-start.6 = (f32[6,2,16,128]{3,2,1,0:T(8,128)S(1)}, f32[6,2,16,128]{3,2,1,0:T(8,128)S(1)}, u32[]{:S(2)}, u32[]{:S(2)}) collective-permute-start(f32[6,2,16,128]{3,2,1,0:T(8,128)S(1)} %fusion.25), channel_id=1, source_target_pairs={{0,64},{8,72},{16,80},{24,88},{32,96},{40,104},{48,112},{56,120},{... | collective-permute-start | bytes 294920 | tf_op jit(solution)/shard_map/ppermute | solution.py:163
  47.9 1.3 %collective-permute-start.7 = (f32[6,2,16,128]{3,2,1,0:T(8,128)S(1)}, f32[6,2,16,128]{3,2,1,0:T(8,128)S(1)}, u32[]{:S(2)}, u32[]{:S(2)}) collective-permute-start(f32[6,2,16,128]{3,2,1,0:T(8,128)S(1)} %fusion.25), channel_id=1, source_target_pairs={{0,32},{8,40},{16,48},{24,56},{32,64},{40,72},{48,80},{56,88},{64,... | collective-permute-start | bytes 294920 | tf_op jit(solution)/shard_map/ppermute | solution.py:163
  49.2 0.4 collective-permute-done.5
  49.6 3.7 %collective-permute-done.6 = f32[6,2,16,128]{3,2,1,0:T(8,128)S(1)} collective-permute-done((f32[6,2,16,128]{3,2,1,0:T(8,128)S(1)}, f32[6,2,16,128]{3,2,1,0:T(8,128)S(1)}, u32[]{:S(2)}, u32[]{:S(2)}) %collective-permute-start.6) | collective-permute-done | bytes 98336 | tf_op jit(solution)/shard_map/ppermute | solution.py:163
  53.3 1.1 %collective-permute-done.7 = f32[6,2,16,128]{3,2,1,0:T(8,128)S(1)} collective-permute-done((f32[6,2,16,128]{3,2,1,0:T(8,128)S(1)}, f32[6,2,16,128]{3,2,1,0:T(8,128)S(1)}, u32[]{:S(2)}, u32[]{:S(2)}) %collective-permute-start.7) | collective-permute-done | bytes 98336 | tf_op jit(solution)/shard_map/ppermute | solution.py:163
  54.4 0.1 select_select_fusion.1
  54.4 0.1 fusion.44
  54.6 0.0 copy-done.7
  54.6 0.1 select_select_fusion.8
  54.7 0.0 copy-done.6
  54.7 0.0 copy-done.3
  54.7 0.0 copy-done.4
  54.7 0.0 copy-done.5
  54.7 0.0 copy-start
  54.7 0.0 copy-start.1
  54.7 0.0 copy-start.2
  54.7 0.9 %multiply_add_fusion = f32[64,16,128]{2,1,0:T(8,128)} fusion(f32[64,16,128]{2,1,0:T(8,128)S(1)} %copy-done.5, f32[64,16,128]{2,1,0:T(8,128)S(1)} %copy-done.3, f32[64,16,128]{2,1,0:T(8,128)S(1)} %copy-done.4, f32[16,128]{1,0:T(8,128)S(1)} %get-tuple-element.53, f32[16,128]{1,0:T(8,128)S(1)} %get-tuple-element.51), kind=kLoop, calls=%fused_computation.9 | loop fusion | flops 524288 | bytes 2113536 | tf_op jit(solution)/shard_map/add | solution.py:274
  55.6 0.1 copy-done
  55.8 0.3 copy-done.1
  56.1 0.2 copy-done.2
  56.3 0.9 %multiply_add_fusion.1 = f32[64,16,128]{2,1,0:T(8,128)} fusion(f32[64,16,128]{2,1,0:T(8,128)S(1)} %copy-done.2, f32[64,16,128]{2,1,0:T(8,128)S(1)} %copy-done, f32[64,16,128]{2,1,0:T(8,128)S(1)} %copy-done.1, f32[16,128]{1,0:T(8,128)S(1)} %get-tuple-element.54, f32[16,128]{1,0:T(8,128)S(1)} %get-tuple-element.52), kind=kLoop, calls=%fused_computation.10 | loop fusion | flops 524288 | bytes 2113536 | tf_op jit(solution)/shard_map/add | solution.py:274
  (15 shorter events, 0.2 us)
Async XLA Ops:
  5.0 18.4 %all-to-all-start = ((f32[8,97,256]{2,1,0:T(8,128)}), f32[8,97,256]{2,1,0:T(8,128)S(1)}, u32[]{:S(2)}, u32[]{:S(2)}) async-start(f32[8,97,256]{2,1,0:T(8,128)} %select_maximum_fusion), calls=%async_computation | async-start | bytes 1703936 | tf_op jit(solution)/shard_map/all_to_all | solution.py:202
  10.3 5.6 %collective-permute-start.1 = (f32[2,16,128]{2,1,0:T(8,128)S(1)}, f32[2,16,128]{2,1,0:T(8,128)S(1)}, u32[]{:S(2)}, u32[]{:S(2)}) collective-permute-start(f32[2,16,128]{2,1,0:T(8,128)S(1)} %pad_maximum_fusion), channel_id=1, source_target_pairs={{8,0},{16,8},{24,16},{32,24},{40,32},{48,40},{56,48},{64,56},{72,6... | collective-permute-start | bytes 49160 | tf_op jit(solution)/shard_map/ppermute | solution.py:220
  16.5 4.8 %collective-permute-start = (f32[2,16,128]{2,1,0:T(8,128)S(1)}, f32[2,16,128]{2,1,0:T(8,128)S(1)}, u32[]{:S(2)}, u32[]{:S(2)}) collective-permute-start(f32[2,16,128]{2,1,0:T(8,128)S(1)} %get-tuple-element.56), channel_id=1, source_target_pairs={{0,8},{8,16},{16,24},{24,32},{32,40},{40,48},{48,56},{56,64},{64,7... | collective-permute-start | bytes 49160 | tf_op jit(solution)/shard_map/ppermute | solution.py:219
  31.2 7.8 %collective-permute-start.2 = (f32[6,2,16,128]{3,2,1,0:T(8,128)}, f32[6,2,16,128]{3,2,1,0:T(8,128)S(1)}, u32[]{:S(2)}, u32[]{:S(2)}) collective-permute-start(f32[6,2,16,128]{3,2,1,0:T(8,128)} %get-tuple-element.11), channel_id=1, source_target_pairs={{0,24},{8,0},{16,8},{24,16},{32,56},{40,32},{48,40},{56,48},{64,88... | collective-permute-start | bytes 294920 | tf_op jit(solution)/shard_map/ppermute | solution.py:163
  35.5 6.4 %collective-permute-start.3 = (f32[6,2,16,128]{3,2,1,0:T(8,128)}, f32[6,2,16,128]{3,2,1,0:T(8,128)S(1)}, u32[]{:S(2)}, u32[]{:S(2)}) collective-permute-start(f32[6,2,16,128]{3,2,1,0:T(8,128)} %get-tuple-element.11), channel_id=1, source_target_pairs={{0,16},{8,24},{16,0},{24,8},{32,48},{40,56},{48,32},{56,40},{64,80... | collective-permute-start | bytes 294920 | tf_op jit(solution)/shard_map/ppermute | solution.py:163
  35.5 7.1 %collective-permute-start.4 = (f32[6,2,16,128]{3,2,1,0:T(8,128)}, f32[6,2,16,128]{3,2,1,0:T(8,128)S(1)}, u32[]{:S(2)}, u32[]{:S(2)}) collective-permute-start(f32[6,2,16,128]{3,2,1,0:T(8,128)} %get-tuple-element.11), channel_id=1, source_target_pairs={{0,8},{8,16},{16,24},{24,0},{32,40},{40,48},{48,56},{56,32},{64,72... | collective-permute-start | bytes 294920 | tf_op jit(solution)/shard_map/ppermute | solution.py:163
  43.7 10.8 %copy-start.7 = (f32[2,16,128]{2,1,0:T(8,128)S(1)}, f32[2,16,128]{2,1,0:T(8,128)}, u32[]{:S(2)}) copy-start(f32[2,16,128]{2,1,0:T(8,128)} %get-tuple-element.35.beta_ref) | copy-start | bytes 49156
  43.8 10.9 %copy-start.6 = (f32[2,16,128]{2,1,0:T(8,128)S(1)}, f32[2,16,128]{2,1,0:T(8,128)}, u32[]{:S(2)}) copy-start(f32[2,16,128]{2,1,0:T(8,128)} %get-tuple-element.55.hi_ref) | copy-start | bytes 49156
  43.8 10.9 %copy-start.3 = (f32[64,16,128]{2,1,0:T(8,128)S(1)}, f32[64,16,128]{2,1,0:T(8,128)}, u32[]{:S(2)}) copy-start(f32[64,16,128]{2,1,0:T(8,128)} %get-tuple-element.13) | copy-start | bytes 1572868
  43.8 10.9 %copy-start.4 = (f32[64,16,128]{2,1,0:T(8,128)S(1)}, f32[64,16,128]{2,1,0:T(8,128)}, u32[]{:S(2)}) copy-start(f32[64,16,128]{2,1,0:T(8,128)} %get-tuple-element.14) | copy-start | bytes 1572868
  43.8 10.9 %copy-start.5 = (f32[64,16,128]{2,1,0:T(8,128)S(1)}, f32[64,16,128]{2,1,0:T(8,128)}, u32[]{:S(2)}) copy-start(f32[64,16,128]{2,1,0:T(8,128)} %get-tuple-element.15) | copy-start | bytes 1572868
  43.8 5.8 %collective-permute-start.5 = (f32[6,2,16,128]{3,2,1,0:T(8,128)S(1)}, f32[6,2,16,128]{3,2,1,0:T(8,128)S(1)}, u32[]{:S(2)}, u32[]{:S(2)}) collective-permute-start(f32[6,2,16,128]{3,2,1,0:T(8,128)S(1)} %fusion.25), channel_id=1, source_target_pairs={{0,96},{8,104},{16,112},{24,120},{32,0},{40,8},{48,16},{56,24},{64... | collective-permute-start | bytes 294920 | tf_op jit(solution)/shard_map/ppermute | solution.py:163
  47.1 6.2 %collective-permute-start.6 = (f32[6,2,16,128]{3,2,1,0:T(8,128)S(1)}, f32[6,2,16,128]{3,2,1,0:T(8,128)S(1)}, u32[]{:S(2)}, u32[]{:S(2)}) collective-permute-start(f32[6,2,16,128]{3,2,1,0:T(8,128)S(1)} %fusion.25), channel_id=1, source_target_pairs={{0,64},{8,72},{16,80},{24,88},{32,96},{40,104},{48,112},{56,120},{... | collective-permute-start | bytes 294920 | tf_op jit(solution)/shard_map/ppermute | solution.py:163
  47.9 6.5 %collective-permute-start.7 = (f32[6,2,16,128]{3,2,1,0:T(8,128)S(1)}, f32[6,2,16,128]{3,2,1,0:T(8,128)S(1)}, u32[]{:S(2)}, u32[]{:S(2)}) collective-permute-start(f32[6,2,16,128]{3,2,1,0:T(8,128)S(1)} %fusion.25), channel_id=1, source_target_pairs={{0,32},{8,40},{16,48},{24,56},{32,64},{40,72},{48,80},{56,88},{64,... | collective-permute-start | bytes 294920 | tf_op jit(solution)/shard_map/ppermute | solution.py:163
  54.7 1.1 %copy-start = (f32[64,16,128]{2,1,0:T(8,128)S(1)}, f32[64,16,128]{2,1,0:T(8,128)}, u32[]{:S(2)}) copy-start(f32[64,16,128]{2,1,0:T(8,128)} %get-tuple-element.9) | copy-start | bytes 1572868
  54.7 1.4 %copy-start.1 = (f32[64,16,128]{2,1,0:T(8,128)S(1)}, f32[64,16,128]{2,1,0:T(8,128)}, u32[]{:S(2)}) copy-start(f32[64,16,128]{2,1,0:T(8,128)} %get-tuple-element.10) | copy-start | bytes 1572868
  54.7 1.5 %copy-start.2 = (f32[64,16,128]{2,1,0:T(8,128)S(1)}, f32[64,16,128]{2,1,0:T(8,128)}, u32[]{:S(2)}) copy-start(f32[64,16,128]{2,1,0:T(8,128)} %get-tuple-element.12) | copy-start | bytes 1572868

commit v3 on v2

--- a/solution.py
+++ b/solution.py
@@ -8,7 +8,7 @@
 from jax.sharding import PartitionSpec as P
 
 ion_rate = 40.0
-HIGHEST = lax.Precision.HIGHEST
+HIGH = lax.Precision.HIGH
 
 
 def face(lower, upper):
@@ -59,7 +59,7 @@
             out += [above, f, dy, dv]
         return tuple(out)
 
-    carry = lax.fori_loop(1, z_cells - 1, fwd, tuple(carry), unroll=2)
+    carry = lax.fori_loop(1, z_cells - 1, fwd, tuple(carry), unroll=8)
 
     z = z_cells - 1
     back = []
@@ -91,7 +91,7 @@
             out += [y_val, v_val, w_val]
         return tuple(out)
 
-    back = lax.fori_loop(0, z_cells - 1, bwd, tuple(back), unroll=2)
+    back = lax.fori_loop(0, z_cells - 1, bwd, tuple(back), unroll=8)
     for n, (rhs_ref, c_ref, y_ref, v_ref, w_ref, k, _) in enumerate(fields):
         y_first, v_first, w_first = back[3 * n:3 * n + 3]
         beta = beta_ref[k]
@@ -187,24 +187,36 @@
     payload = jnp.concatenate([bubble_sink[0], bubble_void[0]], axis=1)
     destination = target // cell_total
     cell_index = target % cell_total
-    same_owner = destination[:, None] == destination[None, :]
+    owners = lax.broadcasted_iota(jnp.int32, (record_total, groups), 1)
+    owner_hot = (destination[:, None] == owners).astype(jnp.float32)
     row_ids = lax.broadcasted_iota(jnp.int32, (record_total, record_total), 0)
     col_ids = lax.broadcasted_iota(jnp.int32, (record_total, record_total), 1)
-    rank_within = jnp.sum((same_owner & (row_ids > col_ids)).astype(jnp.int32), axis=1)
-    slot_index = destination * slot_count + rank_within
-    slot_ids = lax.broadcasted_iota(jnp.int32, (groups * slot_count, record_total), 0)
-    pick = slot_ids == slot_index[None, :]
-    send_rows = jnp.dot(pick.astype(jnp.float32), payload, precision=HIGHEST)
+    earlier = (row_ids > col_ids).astype(jnp.float32)
+    before = jnp.dot(earlier, owner_hot, precision=HIGH)
+    rank_within = jnp.sum(before * owner_hot, axis=1).astype(jnp.int32)
+    rows_per = slot_count + 1
+    out_dest = lax.broadcasted_iota(jnp.int32, (groups, rows_per, 2 * record_total), 0)
+    out_slot = lax.broadcasted_iota(jnp.int32, (groups, rows_per, 2 * record_total), 1)
+    source = lax.broadcasted_iota(jnp.int32, (groups, rows_per, 2 * record_total), 2)
+    record = source % record_total
+    dest_of = destination[record]
+    rank_of = rank_within[record]
+    pick = jnp.where(
+        source < record_total,
+        (dest_of == out_dest) & (rank_of == out_slot),
+        (dest_of == out_dest) & (out_slot == slot_count),
+    ).astype(jnp.float32)
+    lanes = lax.broadcasted_iota(jnp.int32, (record_total, width), 1)
     cell_plus = (cell_index + 1).astype(jnp.float32)
-    send_cells = jnp.sum(jnp.where(pick, cell_plus[None, :], 0.0), axis=1) - 1.0
-    cell_row = jnp.pad(send_cells.reshape(groups, 1, slot_count), ((0, 0), (0, 0), (0, width - slot_count)))
-    send = jnp.concatenate([send_rows.reshape(groups, slot_count, width), cell_row], axis=1)
+    cell_lanes = jnp.where(lanes == rank_within[:, None], cell_plus[:, None], 0.0)
+    stacked = jnp.concatenate([payload, cell_lanes], axis=0)
+    send = jnp.einsum("dsr,rk->dsk", pick, stacked, precision=HIGH)
     received = lax.all_to_all(send, "gx", split_axis=0, concat_axis=0, tiled=True)
     rows = received[:, :slot_count, :].reshape(groups * slot_count, width)
-    cells = received[:, slot_count, :slot_count].reshape(groups * slot_count)
+    cells = received[:, slot_count, :slot_count].reshape(groups * slot_count) - 1.0
     cell_ids = lax.broadcasted_iota(jnp.int32, (cell_total, groups * slot_count), 0).astype(jnp.float32)
     spread = (cell_ids == cells[None, :]).astype(jnp.float32)
-    sources = jnp.dot(spread, rows, precision=HIGHEST)
+    sources = jnp.dot(spread, rows, precision=HIGH)
     return sources.reshape(z_cells, x_cells, width)
 
 

time: 57.5 us -> 6170 us (107.30)
  local copies, waits for them, and re-layouts: 1.63 us -> 6110 us
    gather x0 -> x4, local copies, waits for them, and re-layouts: none -> 6110 us  [the longest x2 4170 us: deposit(): dest_of = destination[record]]
  transfers between devices with their start and end apart: 9 -> 9, of which waited for: 9 -> 9; matrix products, arithmetic and copies ran while one was open for 3% -> 0% of each run, Pallas kernels for 0% -> 0%
where the time goes in v3:
time: 6170 us
  local copies, waits for them, and re-layouts  6110 us (99%)
    gather x2, local copies, waits for them, and re-layouts, deposit(): dest_of = destination[record]  4170 us
    gather x2, local copies, waits for them, and re-layouts, deposit(): rank_of = rank_within[record]  1940 us
  transfers between devices with their start and end apart: 9, of which 9 were waited for; matrix products, arithmetic and copies ran while one was open for 0% of the time, Pallas kernels for 0%

profile of v3, /device:TPU:0, one launch (start us, length us, event | category | flops | bytes accessed | tf_op | source)
XLA Modules:
  0.0 6169.1 jit_solution(17510663896884925727)
XLA Ops:
  0.7 0.6 iota_compare_fusion.9
  1.2 0.6 iota_compare_fusion.8
  1.8 1.3 fusion.98
  3.1 0.2 fusion.9
  3.3 0.6 convert_element_type.24
  3.8 0.2 compare_select_fusion
  4.0 0.2 reshape.100
  4.2 0.2 broadcast_clamp_fusion
  4.5 4166.0 %gather_fusion = s32[397312]{0:T(1024)} fusion(s32[256]{0:T(256)S(1)} %get-tuple-element.56, s32[397312]{0:T(1024)S(1)} %broadcast_clamp_fusion), kind=kCustom, calls=%fused_computation | custom fusion | bytes 4767744 | tf_op jit(solution)/shard_map/gather | solution.py:202
  4170.5 1940.4 %gather_fusion.1 = s32[397312]{0:T(1024)S(1)} fusion(s32[256]{0:T(256)} %convert_element_type.24, s32[397312]{0:T(1024)S(1)} %broadcast_clamp_fusion), kind=kCustom, calls=%fused_computation.1 | custom fusion | bytes 4767744 | tf_op jit(solution)/shard_map/gather | solution.py:203
  6110.8 0.0 copy-start.1
  6110.9 1.4 reshape.107
  6112.3 0.5 copy-done.1
  6112.8 0.0 copy-start.13
  6112.8 0.0 copy-start.14
  6112.8 1.5 reshape.99
  6114.3 0.0 copy-done
  6114.3 0.0 copy-done.12
  6114.3 0.1 fusion.16
  6114.4 0.5 copy-done.2
  6114.9 0.0 copy-done.11
  6114.9 0.0 copy-done.13
  6114.9 0.0 copy-done.14
  6114.9 3.2 fusion.4
  6118.1 4.6 all-to-all-start
  6122.7 0.7 fusion.100
  6123.4 1.3 collective-permute-start.1
  6124.7 4.3 collective-permute-done.1
  6129.0 0.6 divide_select_fusion
  6129.6 3.4 collective-permute-start
  6133.1 1.4 collective-permute-done
  6134.5 0.6 broadcast_select_fusion
  6135.1 1.4 all-to-all-done
  6136.5 0.1 sub.312
  6136.6 0.1 slice.221
  6136.6 2.0 fusion.src_ref
  6138.6 4.9 shard_map.86
  6143.5 4.3 collective-permute-start.2
  6147.8 0.0 collective-permute-start.3
  6147.8 0.9 collective-permute-start.4
  6148.7 2.6 collective-permute-done.2
  6151.3 2.9 collective-permute-done.3
  6154.2 0.7 collective-permute-done.4
  6154.9 0.9 select_select_fusion.6
  6155.8 0.0 copy-start.9
  6155.9 0.0 copy-start.10
  6155.9 0.0 copy-start.6
  6155.9 0.0 copy-start.7
  6155.9 0.0 copy-start.8
  6156.1 3.3 collective-permute-start.5
  6159.4 0.8 collective-permute-start.6
  6160.2 1.3 collective-permute-start.7
  6161.5 0.4 collective-permute-done.5
  6161.9 3.7 collective-permute-done.6
  6165.6 1.1 collective-permute-done.7
  6166.6 0.1 select_select_fusion.1
  6166.7 0.0 copy-start.3
  6166.7 0.0 copy-start.4
  6166.7 0.1 fusion.51
  6166.9 0.1 select_select_fusion.8
  6167.0 0.0 copy-done.10
  6167.0 0.9 multiply_add_fusion.1
  6167.9 0.2 copy-done.5
  6168.2 0.9 multiply_add_fusion
  (26 shorter events, 0.3 us)
Async XLA Ops:
  6110.8 1.9 copy-start.1
  6112.8 1.5 copy-start
  6112.8 1.5 copy-start.12
  6112.8 2.1 copy-start.2
  6112.8 2.1 copy-start.11
  6112.8 2.1 copy-start.13
  6112.8 2.1 copy-start.14
  6118.1 18.4 all-to-all-start
  6123.4 5.6 collective-permute-start.1
  6129.6 4.8 collective-permute-start
  6143.5 7.8 collective-permute-start.2
  6147.8 6.4 collective-permute-start.3
  6147.8 7.1 collective-permute-start.4
  6155.8 11.1 copy-start.9
  6155.9 11.1 copy-start.10
  6155.9 11.1 copy-start.6
  6155.9 11.1 copy-start.7
  6155.9 11.1 copy-start.8
  6156.1 5.8 collective-permute-start.5
  6159.4 6.2 collective-permute-start.6
  6160.2 6.5 collective-permute-start.7
  6166.7 1.2 copy-start.3
  6166.7 1.2 copy-start.4
  6166.7 1.4 copy-start.5

commit v4 on v3

--- a/solution.py
+++ b/solution.py
@@ -195,16 +195,11 @@
     before = jnp.dot(earlier, owner_hot, precision=HIGH)
     rank_within = jnp.sum(before * owner_hot, axis=1).astype(jnp.int32)
     rows_per = slot_count + 1
-    out_dest = lax.broadcasted_iota(jnp.int32, (groups, rows_per, 2 * record_total), 0)
-    out_slot = lax.broadcasted_iota(jnp.int32, (groups, rows_per, 2 * record_total), 1)
-    source = lax.broadcasted_iota(jnp.int32, (groups, rows_per, 2 * record_total), 2)
-    record = source % record_total
-    dest_of = destination[record]
-    rank_of = rank_within[record]
-    pick = jnp.where(
-        source < record_total,
-        (dest_of == out_dest) & (rank_of == out_slot),
-        (dest_of == out_dest) & (out_slot == slot_count),
+    out_dest = lax.broadcasted_iota(jnp.int32, (groups, rows_per, record_total), 0)
+    out_slot = lax.broadcasted_iota(jnp.int32, (groups, rows_per, record_total), 1)
+    mine = destination[None, None, :] == out_dest
+    pick = jnp.concatenate(
+        [mine & (rank_within[None, None, :] == out_slot), mine & (out_slot == slot_count)], axis=2
     ).astype(jnp.float32)
     lanes = lax.broadcasted_iota(jnp.int32, (record_total, width), 1)
     cell_plus = (cell_index + 1).astype(jnp.float32)

time: 6170 us -> 56.1 us (0.01)
  local copies, waits for them, and re-layouts: 6110 us -> 1.54 us
    gather x4 -> x0, local copies, waits for them, and re-layouts: 6110 us -> none  [the longest x2 4170 us: deposit(): dest_of = destination[record]]
  transfers between devices with their start and end apart: 9 -> 9, of which waited for: 9 -> 9; matrix products, arithmetic and copies ran while one was open for 0% -> 4% of each run, Pallas kernels for 0% -> 0%
where the time goes in v4:
time: 56.1 us; the launch traced here: 55.8 us
  starting transfers between devices  19.8 us (35%)
  waiting for transfers between devices  18.4 us (33%)
  other arithmetic  5.48 us (10%)
  Pallas kernels  4.86 us (9%)
  matrix products  4.72 us (8%)
  local copies, waits for them, and re-layouts  1.54 us (3%)
  between operations  0.91 us (2%)
    ppermute x6, waiting for transfers between devices, gather_ring(): got[s] = lax.ppermute(pack, 'gz', route)  11.3 us
    ppermute x6, starting transfers between devices, gather_ring(): got[s] = lax.ppermute(pack, 'gz', route)  10.6 us
    pallas_call x1, Pallas kernels, local_solve(): pl.pallas_call(local_kernel, out_shape=(shape,) * 6 + (pack,), in_specs=[...  4.86 us
    all_to_all x1, starting transfers between devices, deposit(): lax.all_to_all(send, 'gx', split_axis=0, concat_axis=0, tiled=True)  4.58 us
    ppermute x1, waiting for transfers between devices, body(): lax.ppermute(first, 'gz', [(i + 1, i) for i in range(chain - 1)])  4.33 us
    ppermute x1, starting transfers between devices, body(): lax.ppermute(last, 'gz', [(i, i + 1) for i in range(chain - 1)])  3.38 us
    dot_general x1, matrix products, deposit(): send = jnp.einsum('dsr,rk->dsk', pick, stacked, precision=HIGH)  2.51 us
    dot_general x1, matrix products, deposit(): sources = jnp.dot(spread, rows, precision=HIGH)  2.02 us
  transfers between devices with their start and end apart: 9, of which 9 were waited for; matrix products, arithmetic and copies ran while one was open for 4% of the time, Pallas kernels for 0%

profile of v4, /device:TPU:0, one launch (start us, length us, event | category | flops | bytes accessed | tf_op | source)
XLA Modules:
  0.0 55.8 jit_solution(703491978842185213)
XLA Ops:
  0.6 0.7 %fusion.93 = (f32[256]{0:T(256)S(1)}, s32[256]{0:T(256)S(1)}) fusion(s32[256]{0:T(256)} %bitcast.604), kind=kLoop, calls=%fused_computation.217 | loop fusion | flops 5376 | bytes 3072 | tf_op jit(solution)/shard_map/convert_element_type | solution.py:205
  1.3 0.2 fusion.8
  1.5 0.2 fusion.10
  1.8 0.1 fusion.15
  1.9 2.5 %fusion.2 = f32[8,97,256]{2,1,0:T(8,128)} fusion(pred[8,97,256]{2,1,0:T(8,128)(4,1)S(1)} %get-tuple-element.58, pred[8,97,256]{2,1,0:T(8,128)(4,1)S(1)} %get-tuple-element.57, f32[256,256]{1,0:T(8,128)S(1)} %fusion.15, f32[256,128]{1,0:T(8,128)} %bitcast.605, f32[256,128]{1,0:T(8,128)} %bitcast.606), kind=kOutput, calls=%fused_computation.2 | convolution fusion | flops 610930688 | bytes 1716224 | tf_op jit(solution)/shard_map/dsr,rk->dsk/dot_general | solution.py:208
  4.4 4.6 %all-to-all-start = ((f32[8,97,256]{2,1,0:T(8,128)}), f32[8,97,256]{2,1,0:T(8,128)S(1)}, u32[]{:S(2)}, u32[]{:S(2)}) async-start(f32[8,97,256]{2,1,0:T(8,128)} %fusion.2), calls=%async_computation | async-start | bytes 1703936 | tf_op jit(solution)/shard_map/all_to_all | solution.py:209
  9.0 0.7 %fusion.96 = (f32[1,16,128]{2,1,0:T(8,128)S(1)}, f32[1,16,128]{2,1,0:T(8,128)S(1)}, f32[1,16,128]{2,1,0:T(8,128)S(1)}, f32[1,16,128]{2,1,0:T(8,128)S(1)}) fusion(f32[64,16,128]{2,1,0:T(8,128)} %ct_ref.1, f32[64,16,128]{2,1,0:T(8,128)} %ci_ref.1), kind=kLoop, calls=%fused_computation.223 | loop fusion | bytes 65536 | tf_op jit(solution)/shard_map/slice | solution.py:224
  9.7 1.3 %collective-permute-start.1 = (f32[2,16,128]{2,1,0:T(8,128)S(1)}, f32[2,16,128]{2,1,0:T(8,128)S(1)}, u32[]{:S(2)}, u32[]{:S(2)}) collective-permute-start(f32[2,16,128]{2,1,0:T(8,128)S(1)} %pad_maximum_fusion), channel_id=1, source_target_pairs={{8,0},{16,8},{24,16},{32,24},{40,32},{48,40},{56,48},{64,56},{72,6... | collective-permute-start | bytes 49160 | tf_op jit(solution)/shard_map/ppermute | solution.py:227
  11.0 4.3 %collective-permute-done.1 = f32[2,16,128]{2,1,0:T(8,128)S(1)} collective-permute-done((f32[2,16,128]{2,1,0:T(8,128)S(1)}, f32[2,16,128]{2,1,0:T(8,128)S(1)}, u32[]{:S(2)}, u32[]{:S(2)}) %collective-permute-start.1) | collective-permute-done | bytes 16416 | tf_op jit(solution)/shard_map/ppermute | solution.py:227
  15.4 0.6 %divide_select_fusion = (f32[2,16,128]{2,1,0:T(8,128)}, f32[2,16,128]{2,1,0:T(8,128)S(1)}) fusion(f32[2,16,128]{2,1,0:T(8,128)S(1)} %collective-permute-done.1, pred[]{:T(512)S(6)} %eq.204, f32[1,16,128]{2,1,0:T(8,128)S(1)} %get-tuple-element.59, f32[1,16,128]{2,1,0:T(8,128)S(1)} %get-tuple-element.38), kind=kLoop, calls=%fused_computation.189 | loop fusion | flops 24576 | bytes 65537 | tf_op jit(solution)/shard_map/jit(_where)/select_n | solution.py:229
  16.0 3.4 %collective-permute-start = (f32[2,16,128]{2,1,0:T(8,128)S(1)}, f32[2,16,128]{2,1,0:T(8,128)S(1)}, u32[]{:S(2)}, u32[]{:S(2)}) collective-permute-start(f32[2,16,128]{2,1,0:T(8,128)S(1)} %get-tuple-element.54), channel_id=1, source_target_pairs={{0,8},{8,16},{16,24},{24,32},{32,40},{40,48},{48,56},{56,64},{64,7... | collective-permute-start | bytes 49160 | tf_op jit(solution)/shard_map/ppermute | solution.py:226
  19.4 1.4 %collective-permute-done = f32[2,16,128]{2,1,0:T(8,128)S(1)} collective-permute-done((f32[2,16,128]{2,1,0:T(8,128)S(1)}, f32[2,16,128]{2,1,0:T(8,128)S(1)}, u32[]{:S(2)}, u32[]{:S(2)}) %collective-permute-start) | collective-permute-done | bytes 16416 | tf_op jit(solution)/shard_map/ppermute | solution.py:226
  20.8 0.6 %broadcast_select_fusion = (f32[2,16,128]{2,1,0:T(8,128)}, f32[2,16,128]{2,1,0:T(8,128)}) fusion(pred[]{:T(512)S(6)} %eq.203, f32[2,16,128]{2,1,0:T(8,128)S(1)} %collective-permute-done, f32[1,16,128]{2,1,0:T(8,128)S(1)} %get-tuple-element.60, f32[1,16,128]{2,1,0:T(8,128)S(1)} %get-tuple-element.37), kind=kLoop, calls=%fused_computation.206 | loop fusion | flops 32768 | bytes 65537 | tf_op jit(solution)/shard_map/jit(_where)/select_n | solution.py:231
  21.4 1.4 %all-to-all-done = f32[8,97,256]{2,1,0:T(8,128)S(1)} async-done(((f32[8,97,256]{2,1,0:T(8,128)}), f32[8,97,256]{2,1,0:T(8,128)S(1)}, u32[]{:S(2)}, u32[]{:S(2)}) %all-to-all-start) | async-done | bytes 794656 | tf_op jit(solution)/shard_map/all_to_all | solution.py:209
  22.8 0.1 sub.312
  22.9 0.1 slice.217
  23.0 2.0 %fusion.src_ref = f32[64,16,256]{2,1,0:T(8,128)} fusion(f32[768,256,1]{1,0,2:T(8,128)S(1)} %bitcast.603, f32[768]{0:T(1024)S(1)} %sub.312, f32[64,16]{1,0:T(8,128)S(1)} %add_convert_fusion), kind=kOutput, calls=%fused_computation | convolution fusion | flops 1208745984 | bytes 1842176 | tf_op jit(solution)/shard_map/dot_general | solution.py:214
  25.0 4.9 %shard_map.86 = (f32[64,16,128]{2,1,0:T(8,128)}, f32[64,16,128]{2,1,0:T(8,128)}, f32[64,16,128]{2,1,0:T(8,128)}, f32[64,16,128]{2,1,0:T(8,128)}, f32[64,16,128]{...) custom-call(f32[64,16,128]{2,1,0:T(8,128)} %rt_ref.1, f32[64,16,128]{2,1,0:T(8,128)} %ri_ref.1, ...), custom_call_target="tpu_custom_call" | custom-call | tf_op jit(solution)/shard_map/pallas_call | solution.py:111
  29.9 4.3 %collective-permute-start.2 = (f32[6,2,16,128]{3,2,1,0:T(8,128)}, f32[6,2,16,128]{3,2,1,0:T(8,128)S(1)}, u32[]{:S(2)}, u32[]{:S(2)}) collective-permute-start(f32[6,2,16,128]{3,2,1,0:T(8,128)} %get-tuple-element.11), channel_id=1, source_target_pairs={{0,24},{8,0},{16,8},{24,16},{32,56},{40,32},{48,40},{56,48},{64,88... | collective-permute-start | bytes 294920 | tf_op jit(solution)/shard_map/ppermute | solution.py:163
  34.1 0.0 collective-permute-start.3
  34.1 0.9 %collective-permute-start.4 = (f32[6,2,16,128]{3,2,1,0:T(8,128)}, f32[6,2,16,128]{3,2,1,0:T(8,128)S(1)}, u32[]{:S(2)}, u32[]{:S(2)}) collective-permute-start(f32[6,2,16,128]{3,2,1,0:T(8,128)} %get-tuple-element.11), channel_id=1, source_target_pairs={{0,8},{8,16},{16,24},{24,0},{32,40},{40,48},{48,56},{56,32},{64,72... | collective-permute-start | bytes 294920 | tf_op jit(solution)/shard_map/ppermute | solution.py:163
  35.1 2.6 %collective-permute-done.2 = f32[6,2,16,128]{3,2,1,0:T(8,128)S(1)} collective-permute-done((f32[6,2,16,128]{3,2,1,0:T(8,128)}, f32[6,2,16,128]{3,2,1,0:T(8,128)S(1)}, u32[]{:S(2)}, u32[]{:S(2)}) %collective-permute-start.2) | collective-permute-done | bytes 98336 | tf_op jit(solution)/shard_map/ppermute | solution.py:163
  37.7 2.9 %collective-permute-done.3 = f32[6,2,16,128]{3,2,1,0:T(8,128)S(1)} collective-permute-done((f32[6,2,16,128]{3,2,1,0:T(8,128)}, f32[6,2,16,128]{3,2,1,0:T(8,128)S(1)}, u32[]{:S(2)}, u32[]{:S(2)}) %collective-permute-start.3) | collective-permute-done | bytes 98336 | tf_op jit(solution)/shard_map/ppermute | solution.py:163
  40.6 0.7 %collective-permute-done.4 = f32[6,2,16,128]{3,2,1,0:T(8,128)S(1)} collective-permute-done((f32[6,2,16,128]{3,2,1,0:T(8,128)}, f32[6,2,16,128]{3,2,1,0:T(8,128)S(1)}, u32[]{:S(2)}, u32[]{:S(2)}) %collective-permute-start.4) | collective-permute-done | bytes 98336 | tf_op jit(solution)/shard_map/ppermute | solution.py:163
  41.2 0.9 %select_select_fusion.6 = (f32[6,2,16,128]{3,2,1,0:T(8,128)S(1)}, f32[6,2,16,128]{3,2,1,0:T(8,128)S(1)}, f32[6,2,16,128]{3,2,1,0:T(8,128)S(1)}, f32[6,2,16,128]{3,2,1,0:T(8,128)S(1)}) fusion(f32[6,2,16,128]{3,2,1,0:T(8,128)S(1)} %collective-permute-done.2, f32[6,2,16,128]{3,2,1,0:T(8,128)S(1)} %collective-permute-done.3, ...), kind=kLoop, calls=%fused_computation.30 | loop fusion | flops 294912 | bytes 786444 | tf_op jit(solution)/shard_map/jit(_where)/select_n | solution.py:168
  42.3 0.0 copy-start.7
  42.4 0.0 copy-start.6
  42.4 0.0 copy-start.3
  42.4 0.0 copy-start.4
  42.4 0.0 copy-start.5
  42.5 3.3 %collective-permute-start.5 = (f32[6,2,16,128]{3,2,1,0:T(8,128)S(1)}, f32[6,2,16,128]{3,2,1,0:T(8,128)S(1)}, u32[]{:S(2)}, u32[]{:S(2)}) collective-permute-start(f32[6,2,16,128]{3,2,1,0:T(8,128)S(1)} %fusion.31), channel_id=1, source_target_pairs={{0,96},{8,104},{16,112},{24,120},{32,0},{40,8},{48,16},{56,24},{64... | collective-permute-start | bytes 294920 | tf_op jit(solution)/shard_map/ppermute | solution.py:163
  45.7 0.8 %collective-permute-start.6 = (f32[6,2,16,128]{3,2,1,0:T(8,128)S(1)}, f32[6,2,16,128]{3,2,1,0:T(8,128)S(1)}, u32[]{:S(2)}, u32[]{:S(2)}) collective-permute-start(f32[6,2,16,128]{3,2,1,0:T(8,128)S(1)} %fusion.31), channel_id=1, source_target_pairs={{0,64},{8,72},{16,80},{24,88},{32,96},{40,104},{48,112},{56,120},{... | collective-permute-start | bytes 294920 | tf_op jit(solution)/shard_map/ppermute | solution.py:163
  46.5 1.3 %collective-permute-start.7 = (f32[6,2,16,128]{3,2,1,0:T(8,128)S(1)}, f32[6,2,16,128]{3,2,1,0:T(8,128)S(1)}, u32[]{:S(2)}, u32[]{:S(2)}) collective-permute-start(f32[6,2,16,128]{3,2,1,0:T(8,128)S(1)} %fusion.31), channel_id=1, source_target_pairs={{0,32},{8,40},{16,48},{24,56},{32,64},{40,72},{48,80},{56,88},{64,... | collective-permute-start | bytes 294920 | tf_op jit(solution)/shard_map/ppermute | solution.py:163
  47.8 0.4 collective-permute-done.5
  48.2 3.7 %collective-permute-done.6 = f32[6,2,16,128]{3,2,1,0:T(8,128)S(1)} collective-permute-done((f32[6,2,16,128]{3,2,1,0:T(8,128)S(1)}, f32[6,2,16,128]{3,2,1,0:T(8,128)S(1)}, u32[]{:S(2)}, u32[]{:S(2)}) %collective-permute-start.6) | collective-permute-done | bytes 98336 | tf_op jit(solution)/shard_map/ppermute | solution.py:163
  51.9 1.1 %collective-permute-done.7 = f32[6,2,16,128]{3,2,1,0:T(8,128)S(1)} collective-permute-done((f32[6,2,16,128]{3,2,1,0:T(8,128)S(1)}, f32[6,2,16,128]{3,2,1,0:T(8,128)S(1)}, u32[]{:S(2)}, u32[]{:S(2)}) %collective-permute-start.7) | collective-permute-done | bytes 98336 | tf_op jit(solution)/shard_map/ppermute | solution.py:163
  53.0 0.1 select_select_fusion.1
  53.0 0.1 fusion.50
  53.2 0.0 copy-done.7
  53.2 0.1 select_select_fusion.8
  53.3 0.0 copy-done.6
  53.3 0.0 copy-done.3
  53.3 0.0 copy-done.4
  53.3 0.0 copy-done.5
  53.3 0.0 copy-start
  53.3 0.0 copy-start.1
  53.3 0.0 copy-start.2
  53.3 0.9 %multiply_add_fusion = f32[64,16,128]{2,1,0:T(8,128)} fusion(f32[64,16,128]{2,1,0:T(8,128)S(1)} %copy-done.5, f32[64,16,128]{2,1,0:T(8,128)S(1)} %copy-done.3, f32[64,16,128]{2,1,0:T(8,128)S(1)} %copy-done.4, f32[16,128]{1,0:T(8,128)S(1)} %get-tuple-element.51, f32[16,128]{1,0:T(8,128)S(1)} %get-tuple-element.49), kind=kLoop, calls=%fused_computation.19 | loop fusion | flops 524288 | bytes 2113536 | tf_op jit(solution)/shard_map/add | solution.py:281
  54.2 0.1 copy-done
  54.4 0.3 copy-done.1
  54.7 0.2 copy-done.2
  54.9 0.9 %multiply_add_fusion.1 = f32[64,16,128]{2,1,0:T(8,128)} fusion(f32[64,16,128]{2,1,0:T(8,128)S(1)} %copy-done.2, f32[64,16,128]{2,1,0:T(8,128)S(1)} %copy-done, f32[64,16,128]{2,1,0:T(8,128)S(1)} %copy-done.1, f32[16,128]{1,0:T(8,128)S(1)} %get-tuple-element.52, f32[16,128]{1,0:T(8,128)S(1)} %get-tuple-element.50), kind=kLoop, calls=%fused_computation.20 | loop fusion | flops 524288 | bytes 2113536 | tf_op jit(solution)/shard_map/add | solution.py:281
  (15 shorter events, 0.2 us)
Async XLA Ops:
  4.4 18.4 %all-to-all-start = ((f32[8,97,256]{2,1,0:T(8,128)}), f32[8,97,256]{2,1,0:T(8,128)S(1)}, u32[]{:S(2)}, u32[]{:S(2)}) async-start(f32[8,97,256]{2,1,0:T(8,128)} %fusion.2), calls=%async_computation | async-start | bytes 1703936 | tf_op jit(solution)/shard_map/all_to_all | solution.py:209
  9.7 5.6 %collective-permute-start.1 = (f32[2,16,128]{2,1,0:T(8,128)S(1)}, f32[2,16,128]{2,1,0:T(8,128)S(1)}, u32[]{:S(2)}, u32[]{:S(2)}) collective-permute-start(f32[2,16,128]{2,1,0:T(8,128)S(1)} %pad_maximum_fusion), channel_id=1, source_target_pairs={{8,0},{16,8},{24,16},{32,24},{40,32},{48,40},{56,48},{64,56},{72,6... | collective-permute-start | bytes 49160 | tf_op jit(solution)/shard_map/ppermute | solution.py:227
  16.0 4.8 %collective-permute-start = (f32[2,16,128]{2,1,0:T(8,128)S(1)}, f32[2,16,128]{2,1,0:T(8,128)S(1)}, u32[]{:S(2)}, u32[]{:S(2)}) collective-permute-start(f32[2,16,128]{2,1,0:T(8,128)S(1)} %get-tuple-element.54), channel_id=1, source_target_pairs={{0,8},{8,16},{16,24},{24,32},{32,40},{40,48},{48,56},{56,64},{64,7... | collective-permute-start | bytes 49160 | tf_op jit(solution)/shard_map/ppermute | solution.py:226
  29.9 7.8 %collective-permute-start.2 = (f32[6,2,16,128]{3,2,1,0:T(8,128)}, f32[6,2,16,128]{3,2,1,0:T(8,128)S(1)}, u32[]{:S(2)}, u32[]{:S(2)}) collective-permute-start(f32[6,2,16,128]{3,2,1,0:T(8,128)} %get-tuple-element.11), channel_id=1, source_target_pairs={{0,24},{8,0},{16,8},{24,16},{32,56},{40,32},{48,40},{56,48},{64,88... | collective-permute-start | bytes 294920 | tf_op jit(solution)/shard_map/ppermute | solution.py:163
  34.1 6.4 %collective-permute-start.3 = (f32[6,2,16,128]{3,2,1,0:T(8,128)}, f32[6,2,16,128]{3,2,1,0:T(8,128)S(1)}, u32[]{:S(2)}, u32[]{:S(2)}) collective-permute-start(f32[6,2,16,128]{3,2,1,0:T(8,128)} %get-tuple-element.11), channel_id=1, source_target_pairs={{0,16},{8,24},{16,0},{24,8},{32,48},{40,56},{48,32},{56,40},{64,80... | collective-permute-start | bytes 294920 | tf_op jit(solution)/shard_map/ppermute | solution.py:163
  34.1 7.1 %collective-permute-start.4 = (f32[6,2,16,128]{3,2,1,0:T(8,128)}, f32[6,2,16,128]{3,2,1,0:T(8,128)S(1)}, u32[]{:S(2)}, u32[]{:S(2)}) collective-permute-start(f32[6,2,16,128]{3,2,1,0:T(8,128)} %get-tuple-element.11), channel_id=1, source_target_pairs={{0,8},{8,16},{16,24},{24,0},{32,40},{40,48},{48,56},{56,32},{64,72... | collective-permute-start | bytes 294920 | tf_op jit(solution)/shard_map/ppermute | solution.py:163
  42.3 10.8 %copy-start.7 = (f32[2,16,128]{2,1,0:T(8,128)S(1)}, f32[2,16,128]{2,1,0:T(8,128)}, u32[]{:S(2)}) copy-start(f32[2,16,128]{2,1,0:T(8,128)} %get-tuple-element.35.beta_ref) | copy-start | bytes 49156
  42.4 10.9 %copy-start.6 = (f32[2,16,128]{2,1,0:T(8,128)S(1)}, f32[2,16,128]{2,1,0:T(8,128)}, u32[]{:S(2)}) copy-start(f32[2,16,128]{2,1,0:T(8,128)} %get-tuple-element.53.hi_ref) | copy-start | bytes 49156
  42.4 10.9 %copy-start.3 = (f32[64,16,128]{2,1,0:T(8,128)S(1)}, f32[64,16,128]{2,1,0:T(8,128)}, u32[]{:S(2)}) copy-start(f32[64,16,128]{2,1,0:T(8,128)} %get-tuple-element.13) | copy-start | bytes 1572868
  42.4 10.9 %copy-start.4 = (f32[64,16,128]{2,1,0:T(8,128)S(1)}, f32[64,16,128]{2,1,0:T(8,128)}, u32[]{:S(2)}) copy-start(f32[64,16,128]{2,1,0:T(8,128)} %get-tuple-element.14) | copy-start | bytes 1572868
  42.4 10.9 %copy-start.5 = (f32[64,16,128]{2,1,0:T(8,128)S(1)}, f32[64,16,128]{2,1,0:T(8,128)}, u32[]{:S(2)}) copy-start(f32[64,16,128]{2,1,0:T(8,128)} %get-tuple-element.15) | copy-start | bytes 1572868
  42.5 5.8 %collective-permute-start.5 = (f32[6,2,16,128]{3,2,1,0:T(8,128)S(1)}, f32[6,2,16,128]{3,2,1,0:T(8,128)S(1)}, u32[]{:S(2)}, u32[]{:S(2)}) collective-permute-start(f32[6,2,16,128]{3,2,1,0:T(8,128)S(1)} %fusion.31), channel_id=1, source_target_pairs={{0,96},{8,104},{16,112},{24,120},{32,0},{40,8},{48,16},{56,24},{64... | collective-permute-start | bytes 294920 | tf_op jit(solution)/shard_map/ppermute | solution.py:163
  45.7 6.2 %collective-permute-start.6 = (f32[6,2,16,128]{3,2,1,0:T(8,128)S(1)}, f32[6,2,16,128]{3,2,1,0:T(8,128)S(1)}, u32[]{:S(2)}, u32[]{:S(2)}) collective-permute-start(f32[6,2,16,128]{3,2,1,0:T(8,128)S(1)} %fusion.31), channel_id=1, source_target_pairs={{0,64},{8,72},{16,80},{24,88},{32,96},{40,104},{48,112},{56,120},{... | collective-permute-start | bytes 294920 | tf_op jit(solution)/shard_map/ppermute | solution.py:163
  46.5 6.5 %collective-permute-start.7 = (f32[6,2,16,128]{3,2,1,0:T(8,128)S(1)}, f32[6,2,16,128]{3,2,1,0:T(8,128)S(1)}, u32[]{:S(2)}, u32[]{:S(2)}) collective-permute-start(f32[6,2,16,128]{3,2,1,0:T(8,128)S(1)} %fusion.31), channel_id=1, source_target_pairs={{0,32},{8,40},{16,48},{24,56},{32,64},{40,72},{48,80},{56,88},{64,... | collective-permute-start | bytes 294920 | tf_op jit(solution)/shard_map/ppermute | solution.py:163
  53.3 1.1 %copy-start = (f32[64,16,128]{2,1,0:T(8,128)S(1)}, f32[64,16,128]{2,1,0:T(8,128)}, u32[]{:S(2)}) copy-start(f32[64,16,128]{2,1,0:T(8,128)} %get-tuple-element.9) | copy-start | bytes 1572868
  53.3 1.4 %copy-start.1 = (f32[64,16,128]{2,1,0:T(8,128)S(1)}, f32[64,16,128]{2,1,0:T(8,128)}, u32[]{:S(2)}) copy-start(f32[64,16,128]{2,1,0:T(8,128)} %get-tuple-element.10) | copy-start | bytes 1572868
  53.3 1.5 %copy-start.2 = (f32[64,16,128]{2,1,0:T(8,128)S(1)}, f32[64,16,128]{2,1,0:T(8,128)}, u32[]{:S(2)}) copy-start(f32[64,16,128]{2,1,0:T(8,128)} %get-tuple-element.12) | copy-start | bytes 1572868

commit v5 on v4

--- a/solution.py
+++ b/solution.py
@@ -15,21 +15,58 @@
     return 2.0 * lower * upper / (lower + upper)
 
 
-def local_kernel(rt_ref, ri_ref, ct_ref, ci_ref, src_ref, lo_ref, hi_ref, beta_ref,
-                 yt_ref, yi_ref, vt_ref, vi_ref, wt_ref, wi_ref, pack_ref):
+CHUNKS = 4
+
+
+def local_kernel(rt_hbm, ri_hbm, ct_hbm, ci_hbm, src_hbm, lo_ref, hi_ref, beta_ref,
+                 yt_hbm, yi_hbm, vt_hbm, vi_hbm, wt_hbm, wi_hbm, pack_ref,
+                 rt_ref, ri_ref, ct_ref, ci_ref, src_ref,
+                 yt_ref, yi_ref, vt_ref, vi_ref, wt_ref, wi_ref, in_sem, out_sem):
     z_cells = rt_ref.shape[0]
     y_cells = rt_ref.shape[2]
+    rows = z_cells // CHUNKS
+    ins = ((rt_hbm, rt_ref), (ri_hbm, ri_ref), (src_hbm, src_ref), (ct_hbm, ct_ref), (ci_hbm, ci_ref))
+    outs = ((yt_ref, yt_hbm), (yi_ref, yi_hbm), (vt_ref, vt_hbm), (vi_ref, vi_hbm), (wt_ref, wt_hbm), (wi_ref, wi_hbm))
+
+    def copy_in(i, c):
+        src_of, dst_of = ins[i]
+        return pltpu.make_async_copy(
+            src_of.at[pl.ds(c * rows, rows)], dst_of.at[pl.ds(c * rows, rows)], in_sem.at[i, c]
+        )
+
+    def copy_out(j, c):
+        src_of, dst_of = outs[j]
+        return pltpu.make_async_copy(
+            src_of.at[pl.ds(c * rows, rows)], dst_of.at[pl.ds(c * rows, rows)], out_sem.at[j, c]
+        )
+
+    for c in range(CHUNKS):
+        for i in (3, 4, 0, 1, 2):
+            copy_in(i, c).start()
+
+    cond_ready = set()
+
+    def wait_chunk(c):
+        for cc in (c, c + 1):
+            if cc < CHUNKS and cc not in cond_ready:
+                copy_in(3, cc).wait()
+                copy_in(4, cc).wait()
+                cond_ready.add(cc)
+        for i in (0, 1, 2):
+            copy_in(i, c).wait()
+
     fields = (
-        (rt_ref, ct_ref, yt_ref, vt_ref, wt_ref, 0, 1.0),
-        (ri_ref, ci_ref, yi_ref, vi_ref, wi_ref, 1, ion_rate),
+        (rt_ref, ct_ref, yt_ref, vt_ref, wt_ref, 0),
+        (ri_ref, ci_ref, yi_ref, vi_ref, wi_ref, 1),
     )
 
     def absorb_of(k, z):
         part = src_ref[z, :, k * y_cells:(k + 1) * y_cells]
         return part if k == 0 else ion_rate * part
 
+    wait_chunk(0)
     carry = []
-    for rhs_ref, c_ref, y_ref, v_ref, w_ref, k, _ in fields:
+    for rhs_ref, c_ref, y_ref, v_ref, w_ref, k in fields:
         below = lo_ref[k]
         above = face(c_ref[0], c_ref[1])
         main = 1.0 + below + above + absorb_of(k, 0)
@@ -44,7 +81,7 @@
 
     def fwd(z, carry):
         out = []
-        for n, (rhs_ref, c_ref, y_ref, v_ref, w_ref, k, _) in enumerate(fields):
+        for n, (rhs_ref, c_ref, y_ref, v_ref, w_ref, k) in enumerate(fields):
             below, f_prev, dy_prev, dv_prev = carry[4 * n:4 * n + 4]
             above = face(c_ref[z], c_ref[z + 1])
             main = 1.0 + below + above + absorb_of(k, z)
@@ -59,11 +96,17 @@
             out += [above, f, dy, dv]
         return tuple(out)
 
-    carry = lax.fori_loop(1, z_cells - 1, fwd, tuple(carry), unroll=8)
+    carry = tuple(carry)
+    for c in range(CHUNKS):
+        if c > 0:
+            wait_chunk(c)
+        low = max(1, c * rows)
+        high = min(z_cells - 1, (c + 1) * rows)
+        carry = lax.fori_loop(low, high, fwd, carry, unroll=8)
 
     z = z_cells - 1
     back = []
-    for n, (rhs_ref, c_ref, y_ref, v_ref, w_ref, k, _) in enumerate(fields):
+    for n, (rhs_ref, c_ref, y_ref, v_ref, w_ref, k) in enumerate(fields):
         below, f_prev, dy_prev, dv_prev = carry[4 * n:4 * n + 4]
         above = hi_ref[k]
         main = 1.0 + below + above + absorb_of(k, z)
@@ -76,10 +119,9 @@
         w_ref[z] = rp
         back += [dy, dv, rp]
 
-    def bwd(i, back):
-        z = z_cells - 2 - i
+    def bwd(z, back):
         out = []
-        for n, (rhs_ref, c_ref, y_ref, v_ref, w_ref, k, _) in enumerate(fields):
+        for n, (rhs_ref, c_ref, y_ref, v_ref, w_ref, k) in enumerate(fields):
             y_next, v_next, w_next = back[3 * n:3 * n + 3]
             f = w_ref[z]
             y_val = y_ref[z] - f * y_next
@@ -91,8 +133,16 @@
             out += [y_val, v_val, w_val]
         return tuple(out)
 
-    back = lax.fori_loop(0, z_cells - 1, bwd, tuple(back), unroll=8)
-    for n, (rhs_ref, c_ref, y_ref, v_ref, w_ref, k, _) in enumerate(fields):
+    back = tuple(back)
+    for c in reversed(range(CHUNKS)):
+        low = c * rows
+        high = min(z_cells - 1, (c + 1) * rows)
+        back = lax.fori_loop(
+            0, high - low, lambda i, b: bwd(high - 1 - i, b), back, unroll=8
+        )
+        for j in range(6):
+            copy_out(j, c).start()
+    for n, (rhs_ref, c_ref, y_ref, v_ref, w_ref, k) in enumerate(fields):
         y_first, v_first, w_first = back[3 * n:3 * n + 3]
         beta = beta_ref[k]
         alpha = hi_ref[k]
@@ -102,17 +152,26 @@
         pack_ref[3, k] = -w_ref[z_cells - 1] * alpha
         pack_ref[4, k] = y_first
         pack_ref[5, k] = y_ref[z_cells - 1]
+    for c in range(CHUNKS):
+        for j in range(6):
+            copy_out(j, c).wait()
 
 
 def local_solve(rhs_temp, rhs_ion, cond_temp, cond_ion, sources, lo, hi, beta):
     shape = jax.ShapeDtypeStruct(rhs_temp.shape, jnp.float32)
     pack = jax.ShapeDtypeStruct((6,) + lo.shape, jnp.float32)
     vmem = pl.BlockSpec(memory_space=pltpu.VMEM)
+    hbm = pl.BlockSpec(memory_space=pl.ANY)
+    plane = pltpu.VMEM(rhs_temp.shape, jnp.float32)
     return pl.pallas_call(
         local_kernel,
         out_shape=(shape,) * 6 + (pack,),
-        in_specs=[vmem] * 8,
-        out_specs=(vmem,) * 7,
+        in_specs=[hbm] * 5 + [vmem] * 3,
+        out_specs=(hbm,) * 6 + (vmem,),
+        scratch_shapes=[plane] * 4
+        + [pltpu.VMEM(sources.shape, jnp.float32)]
+        + [plane] * 6
+        + [pltpu.SemaphoreType.DMA((5, CHUNKS)), pltpu.SemaphoreType.DMA((6, CHUNKS))],
     )(rhs_temp, rhs_ion, cond_temp, cond_ion, sources, lo, hi, beta)
 
 

time: 56.1 us -> 57.1 us (1.018)
  Pallas kernels: 4.86 us -> 5.71 us
    pallas_call x1, Pallas kernels: 4.86 us -> 5.71 us  [local_solve(): pl.pallas_call(local_kernel, out_shape=(shape,) * 6 + (pack,), in_specs=[...]
where the time goes in v5:
time: 57.1 us; the launch traced here: 56.7 us
  starting transfers between devices  19.9 us (35%)
  waiting for transfers between devices  18.4 us (32%)
  Pallas kernels  5.71 us (10%)
  other arithmetic  5.48 us (10%)
  matrix products  4.72 us (8%)
  local copies, waits for them, and re-layouts  1.54 us (3%)
  between operations  0.92 us (2%)
    ppermute x6, waiting for transfers between devices, gather_ring(): got[s] = lax.ppermute(pack, 'gz', route)  11.3 us
    ppermute x6, starting transfers between devices, gather_ring(): got[s] = lax.ppermute(pack, 'gz', route)  10.7 us
    pallas_call x1, Pallas kernels, local_solve(): pl.pallas_call(local_kernel, out_shape=(shape,) * 6 + (pack,), in_specs=[...  5.71 us
    all_to_all x1, starting transfers between devices, deposit(): lax.all_to_all(send, 'gx', split_axis=0, concat_axis=0, tiled=True)  4.58 us
    ppermute x1, waiting for transfers between devices, body(): lax.ppermute(first, 'gz', [(i + 1, i) for i in range(chain - 1)])  4.33 us
    ppermute x1, starting transfers between devices, body(): lax.ppermute(last, 'gz', [(i, i + 1) for i in range(chain - 1)])  3.38 us
    dot_general x1, matrix products, deposit(): send = jnp.einsum('dsr,rk->dsk', pick, stacked, precision=HIGH)  2.51 us
    dot_general x1, matrix products, deposit(): sources = jnp.dot(spread, rows, precision=HIGH)  2.02 us
  transfers between devices with their start and end apart: 9, of which 9 were waited for; matrix products, arithmetic and copies ran while one was open for 4% of the time, Pallas kernels for 0%

profile of v5, /device:TPU:0, one launch (start us, length us, event | category | flops | bytes accessed | tf_op | source)
XLA Modules:
  0.0 56.7 jit_solution(2953997963963181708)
XLA Ops:
  0.6 0.7 %fusion.93 = (f32[256]{0:T(256)S(1)}, s32[256]{0:T(256)S(1)}) fusion(s32[256]{0:T(256)} %bitcast.604), kind=kLoop, calls=%fused_computation.217 | loop fusion | flops 5376 | bytes 3072 | tf_op jit(solution)/shard_map/convert_element_type | solution.py:264
  1.3 0.2 fusion.8
  1.5 0.2 fusion.10
  1.8 0.1 fusion.15
  1.9 2.5 %fusion.2 = f32[8,97,256]{2,1,0:T(8,128)} fusion(pred[8,97,256]{2,1,0:T(8,128)(4,1)S(1)} %get-tuple-element.58, pred[8,97,256]{2,1,0:T(8,128)(4,1)S(1)} %get-tuple-element.57, f32[256,256]{1,0:T(8,128)S(1)} %fusion.15, f32[256,128]{1,0:T(8,128)} %bitcast.605, f32[256,128]{1,0:T(8,128)} %bitcast.606), kind=kOutput, calls=%fused_computation.2 | convolution fusion | flops 610930688 | bytes 1716224 | tf_op jit(solution)/shard_map/dsr,rk->dsk/dot_general | solution.py:267
  4.4 4.6 %all-to-all-start = ((f32[8,97,256]{2,1,0:T(8,128)}), f32[8,97,256]{2,1,0:T(8,128)S(1)}, u32[]{:S(2)}, u32[]{:S(2)}) async-start(f32[8,97,256]{2,1,0:T(8,128)} %fusion.2), calls=%async_computation | async-start | bytes 1703936 | tf_op jit(solution)/shard_map/all_to_all | solution.py:268
  9.0 0.7 %fusion.96 = (f32[1,16,128]{2,1,0:T(8,128)S(1)}, f32[1,16,128]{2,1,0:T(8,128)S(1)}, f32[1,16,128]{2,1,0:T(8,128)S(1)}, f32[1,16,128]{2,1,0:T(8,128)S(1)}) fusion(f32[64,16,128]{2,1,0:T(8,128)} %ct_hbm.1, f32[64,16,128]{2,1,0:T(8,128)} %ci_hbm.1), kind=kLoop, calls=%fused_computation.223 | loop fusion | bytes 65536 | tf_op jit(solution)/shard_map/slice | solution.py:283
  9.7 1.3 %collective-permute-start.1 = (f32[2,16,128]{2,1,0:T(8,128)S(1)}, f32[2,16,128]{2,1,0:T(8,128)S(1)}, u32[]{:S(2)}, u32[]{:S(2)}) collective-permute-start(f32[2,16,128]{2,1,0:T(8,128)S(1)} %pad_maximum_fusion), channel_id=1, source_target_pairs={{8,0},{16,8},{24,16},{32,24},{40,32},{48,40},{56,48},{64,56},{72,6... | collective-permute-start | bytes 49160 | tf_op jit(solution)/shard_map/ppermute | solution.py:286
  11.0 4.3 %collective-permute-done.1 = f32[2,16,128]{2,1,0:T(8,128)S(1)} collective-permute-done((f32[2,16,128]{2,1,0:T(8,128)S(1)}, f32[2,16,128]{2,1,0:T(8,128)S(1)}, u32[]{:S(2)}, u32[]{:S(2)}) %collective-permute-start.1) | collective-permute-done | bytes 16416 | tf_op jit(solution)/shard_map/ppermute | solution.py:286
  15.4 0.6 %divide_select_fusion = (f32[2,16,128]{2,1,0:T(8,128)}, f32[2,16,128]{2,1,0:T(8,128)S(1)}) fusion(f32[2,16,128]{2,1,0:T(8,128)S(1)} %collective-permute-done.1, pred[]{:T(512)S(6)} %eq.204, f32[1,16,128]{2,1,0:T(8,128)S(1)} %get-tuple-element.59, f32[1,16,128]{2,1,0:T(8,128)S(1)} %get-tuple-element.38), kind=kLoop, calls=%fused_computation.189 | loop fusion | flops 24576 | bytes 65537 | tf_op jit(solution)/shard_map/jit(_where)/select_n | solution.py:288
  16.0 3.4 %collective-permute-start = (f32[2,16,128]{2,1,0:T(8,128)S(1)}, f32[2,16,128]{2,1,0:T(8,128)S(1)}, u32[]{:S(2)}, u32[]{:S(2)}) collective-permute-start(f32[2,16,128]{2,1,0:T(8,128)S(1)} %get-tuple-element.54), channel_id=1, source_target_pairs={{0,8},{8,16},{16,24},{24,32},{32,40},{40,48},{48,56},{56,64},{64,7... | collective-permute-start | bytes 49160 | tf_op jit(solution)/shard_map/ppermute | solution.py:285
  19.4 1.4 %collective-permute-done = f32[2,16,128]{2,1,0:T(8,128)S(1)} collective-permute-done((f32[2,16,128]{2,1,0:T(8,128)S(1)}, f32[2,16,128]{2,1,0:T(8,128)S(1)}, u32[]{:S(2)}, u32[]{:S(2)}) %collective-permute-start) | collective-permute-done | bytes 16416 | tf_op jit(solution)/shard_map/ppermute | solution.py:285
  20.8 0.6 %broadcast_select_fusion = (f32[2,16,128]{2,1,0:T(8,128)}, f32[2,16,128]{2,1,0:T(8,128)}) fusion(pred[]{:T(512)S(6)} %eq.203, f32[2,16,128]{2,1,0:T(8,128)S(1)} %collective-permute-done, f32[1,16,128]{2,1,0:T(8,128)S(1)} %get-tuple-element.60, f32[1,16,128]{2,1,0:T(8,128)S(1)} %get-tuple-element.37), kind=kLoop, calls=%fused_computation.206 | loop fusion | flops 32768 | bytes 65537 | tf_op jit(solution)/shard_map/jit(_where)/select_n | solution.py:290
  21.4 1.4 %all-to-all-done = f32[8,97,256]{2,1,0:T(8,128)S(1)} async-done(((f32[8,97,256]{2,1,0:T(8,128)}), f32[8,97,256]{2,1,0:T(8,128)S(1)}, u32[]{:S(2)}, u32[]{:S(2)}) %all-to-all-start) | async-done | bytes 794656 | tf_op jit(solution)/shard_map/all_to_all | solution.py:268
  22.8 0.1 sub.312
  22.9 0.1 slice.217
  23.0 2.0 %fusion.src_hbm = f32[64,16,256]{2,1,0:T(8,128)} fusion(f32[768,256,1]{1,0,2:T(8,128)S(1)} %bitcast.603, f32[768]{0:T(1024)S(1)} %sub.312, f32[64,16]{1,0:T(8,128)S(1)} %add_convert_fusion), kind=kOutput, calls=%fused_computation | convolution fusion | flops 1208745984 | bytes 1842176 | tf_op jit(solution)/shard_map/dot_general | solution.py:273
  25.0 5.7 %shard_map.86 = (f32[64,16,128]{2,1,0:T(8,128)}, f32[64,16,128]{2,1,0:T(8,128)}, f32[64,16,128]{2,1,0:T(8,128)}, f32[64,16,128]{2,1,0:T(8,128)}, f32[64,16,128]{...) custom-call(f32[64,16,128]{2,1,0:T(8,128)} %rt_hbm.1, f32[64,16,128]{2,1,0:T(8,128)} %ri_hbm.1, ...), custom_call_target="tpu_custom_call" | custom-call | tf_op jit(solution)/shard_map/pallas_call | solution.py:166
  30.7 4.3 %collective-permute-start.2 = (f32[6,2,16,128]{3,2,1,0:T(8,128)}, f32[6,2,16,128]{3,2,1,0:T(8,128)S(1)}, u32[]{:S(2)}, u32[]{:S(2)}) collective-permute-start(f32[6,2,16,128]{3,2,1,0:T(8,128)} %get-tuple-element.11), channel_id=1, source_target_pairs={{0,24},{8,0},{16,8},{24,16},{32,56},{40,32},{48,40},{56,48},{64,88... | collective-permute-start | bytes 294920 | tf_op jit(solution)/shard_map/ppermute | solution.py:222
  35.1 0.0 collective-permute-start.3
  35.1 0.9 %collective-permute-start.4 = (f32[6,2,16,128]{3,2,1,0:T(8,128)}, f32[6,2,16,128]{3,2,1,0:T(8,128)S(1)}, u32[]{:S(2)}, u32[]{:S(2)}) collective-permute-start(f32[6,2,16,128]{3,2,1,0:T(8,128)} %get-tuple-element.11), channel_id=1, source_target_pairs={{0,8},{8,16},{16,24},{24,0},{32,40},{40,48},{48,56},{56,32},{64,72... | collective-permute-start | bytes 294920 | tf_op jit(solution)/shard_map/ppermute | solution.py:222
  36.0 2.6 %collective-permute-done.2 = f32[6,2,16,128]{3,2,1,0:T(8,128)S(1)} collective-permute-done((f32[6,2,16,128]{3,2,1,0:T(8,128)}, f32[6,2,16,128]{3,2,1,0:T(8,128)S(1)}, u32[]{:S(2)}, u32[]{:S(2)}) %collective-permute-start.2) | collective-permute-done | bytes 98336 | tf_op jit(solution)/shard_map/ppermute | solution.py:222
  38.6 2.9 %collective-permute-done.3 = f32[6,2,16,128]{3,2,1,0:T(8,128)S(1)} collective-permute-done((f32[6,2,16,128]{3,2,1,0:T(8,128)}, f32[6,2,16,128]{3,2,1,0:T(8,128)S(1)}, u32[]{:S(2)}, u32[]{:S(2)}) %collective-permute-start.3) | collective-permute-done | bytes 98336 | tf_op jit(solution)/shard_map/ppermute | solution.py:222
  41.5 0.7 %collective-permute-done.4 = f32[6,2,16,128]{3,2,1,0:T(8,128)S(1)} collective-permute-done((f32[6,2,16,128]{3,2,1,0:T(8,128)}, f32[6,2,16,128]{3,2,1,0:T(8,128)S(1)}, u32[]{:S(2)}, u32[]{:S(2)}) %collective-permute-start.4) | collective-permute-done | bytes 98336 | tf_op jit(solution)/shard_map/ppermute | solution.py:222
  42.2 0.9 %select_select_fusion.6 = (f32[6,2,16,128]{3,2,1,0:T(8,128)S(1)}, f32[6,2,16,128]{3,2,1,0:T(8,128)S(1)}, f32[6,2,16,128]{3,2,1,0:T(8,128)S(1)}, f32[6,2,16,128]{3,2,1,0:T(8,128)S(1)}) fusion(f32[6,2,16,128]{3,2,1,0:T(8,128)S(1)} %collective-permute-done.2, f32[6,2,16,128]{3,2,1,0:T(8,128)S(1)} %collective-permute-done.3, ...), kind=kLoop, calls=%fused_computation.30 | loop fusion | flops 294912 | bytes 786444 | tf_op jit(solution)/shard_map/jit(_where)/select_n | solution.py:227
  43.3 0.0 copy-start.7
  43.3 0.0 copy-start.6
  43.3 0.0 copy-start.3
  43.3 0.0 copy-start.4
  43.4 0.0 copy-start.5
  43.4 3.3 %collective-permute-start.5 = (f32[6,2,16,128]{3,2,1,0:T(8,128)S(1)}, f32[6,2,16,128]{3,2,1,0:T(8,128)S(1)}, u32[]{:S(2)}, u32[]{:S(2)}) collective-permute-start(f32[6,2,16,128]{3,2,1,0:T(8,128)S(1)} %fusion.31), channel_id=1, source_target_pairs={{0,96},{8,104},{16,112},{24,120},{32,0},{40,8},{48,16},{56,24},{64... | collective-permute-start | bytes 294920 | tf_op jit(solution)/shard_map/ppermute | solution.py:222
  46.7 0.8 %collective-permute-start.6 = (f32[6,2,16,128]{3,2,1,0:T(8,128)S(1)}, f32[6,2,16,128]{3,2,1,0:T(8,128)S(1)}, u32[]{:S(2)}, u32[]{:S(2)}) collective-permute-start(f32[6,2,16,128]{3,2,1,0:T(8,128)S(1)} %fusion.31), channel_id=1, source_target_pairs={{0,64},{8,72},{16,80},{24,88},{32,96},{40,104},{48,112},{56,120},{... | collective-permute-start | bytes 294920 | tf_op jit(solution)/shard_map/ppermute | solution.py:222
  47.4 1.3 %collective-permute-start.7 = (f32[6,2,16,128]{3,2,1,0:T(8,128)S(1)}, f32[6,2,16,128]{3,2,1,0:T(8,128)S(1)}, u32[]{:S(2)}, u32[]{:S(2)}) collective-permute-start(f32[6,2,16,128]{3,2,1,0:T(8,128)S(1)} %fusion.31), channel_id=1, source_target_pairs={{0,32},{8,40},{16,48},{24,56},{32,64},{40,72},{48,80},{56,88},{64,... | collective-permute-start | bytes 294920 | tf_op jit(solution)/shard_map/ppermute | solution.py:222
  48.8 0.4 collective-permute-done.5
  49.2 3.7 %collective-permute-done.6 = f32[6,2,16,128]{3,2,1,0:T(8,128)S(1)} collective-permute-done((f32[6,2,16,128]{3,2,1,0:T(8,128)S(1)}, f32[6,2,16,128]{3,2,1,0:T(8,128)S(1)}, u32[]{:S(2)}, u32[]{:S(2)}) %collective-permute-start.6) | collective-permute-done | bytes 98336 | tf_op jit(solution)/shard_map/ppermute | solution.py:222
  52.9 1.1 %collective-permute-done.7 = f32[6,2,16,128]{3,2,1,0:T(8,128)S(1)} collective-permute-done((f32[6,2,16,128]{3,2,1,0:T(8,128)S(1)}, f32[6,2,16,128]{3,2,1,0:T(8,128)S(1)}, u32[]{:S(2)}, u32[]{:S(2)}) %collective-permute-start.7) | collective-permute-done | bytes 98336 | tf_op jit(solution)/shard_map/ppermute | solution.py:222
  53.9 0.1 select_select_fusion.1
  54.0 0.1 fusion.50
  54.1 0.0 copy-done.7
  54.1 0.1 select_select_fusion.8
  54.2 0.0 copy-done.6
  54.2 0.0 copy-done.3
  54.2 0.0 copy-done.4
  54.2 0.0 copy-done.5
  54.2 0.0 copy-start
  54.3 0.0 copy-start.1
  54.3 0.0 copy-start.2
  54.3 0.9 %multiply_add_fusion = f32[64,16,128]{2,1,0:T(8,128)} fusion(f32[64,16,128]{2,1,0:T(8,128)S(1)} %copy-done.5, f32[64,16,128]{2,1,0:T(8,128)S(1)} %copy-done.3, f32[64,16,128]{2,1,0:T(8,128)S(1)} %copy-done.4, f32[16,128]{1,0:T(8,128)S(1)} %get-tuple-element.51, f32[16,128]{1,0:T(8,128)S(1)} %get-tuple-element.49), kind=kLoop, calls=%fused_computation.19 | loop fusion | flops 524288 | bytes 2113536 | tf_op jit(solution)/shard_map/add | solution.py:340
  55.2 0.1 copy-done
  55.3 0.3 copy-done.1
  55.6 0.2 copy-done.2
  55.8 0.9 %multiply_add_fusion.1 = f32[64,16,128]{2,1,0:T(8,128)} fusion(f32[64,16,128]{2,1,0:T(8,128)S(1)} %copy-done.2, f32[64,16,128]{2,1,0:T(8,128)S(1)} %copy-done, f32[64,16,128]{2,1,0:T(8,128)S(1)} %copy-done.1, f32[16,128]{1,0:T(8,128)S(1)} %get-tuple-element.52, f32[16,128]{1,0:T(8,128)S(1)} %get-tuple-element.50), kind=kLoop, calls=%fused_computation.20 | loop fusion | flops 524288 | bytes 2113536 | tf_op jit(solution)/shard_map/add | solution.py:340
  (15 shorter events, 0.2 us)
Async XLA Ops:
  4.4 18.4 %all-to-all-start = ((f32[8,97,256]{2,1,0:T(8,128)}), f32[8,97,256]{2,1,0:T(8,128)S(1)}, u32[]{:S(2)}, u32[]{:S(2)}) async-start(f32[8,97,256]{2,1,0:T(8,128)} %fusion.2), calls=%async_computation | async-start | bytes 1703936 | tf_op jit(solution)/shard_map/all_to_all | solution.py:268
  9.7 5.6 %collective-permute-start.1 = (f32[2,16,128]{2,1,0:T(8,128)S(1)}, f32[2,16,128]{2,1,0:T(8,128)S(1)}, u32[]{:S(2)}, u32[]{:S(2)}) collective-permute-start(f32[2,16,128]{2,1,0:T(8,128)S(1)} %pad_maximum_fusion), channel_id=1, source_target_pairs={{8,0},{16,8},{24,16},{32,24},{40,32},{48,40},{56,48},{64,56},{72,6... | collective-permute-start | bytes 49160 | tf_op jit(solution)/shard_map/ppermute | solution.py:286
  16.0 4.8 %collective-permute-start = (f32[2,16,128]{2,1,0:T(8,128)S(1)}, f32[2,16,128]{2,1,0:T(8,128)S(1)}, u32[]{:S(2)}, u32[]{:S(2)}) collective-permute-start(f32[2,16,128]{2,1,0:T(8,128)S(1)} %get-tuple-element.54), channel_id=1, source_target_pairs={{0,8},{8,16},{16,24},{24,32},{32,40},{40,48},{48,56},{56,64},{64,7... | collective-permute-start | bytes 49160 | tf_op jit(solution)/shard_map/ppermute | solution.py:285
  30.7 7.9 %collective-permute-start.2 = (f32[6,2,16,128]{3,2,1,0:T(8,128)}, f32[6,2,16,128]{3,2,1,0:T(8,128)S(1)}, u32[]{:S(2)}, u32[]{:S(2)}) collective-permute-start(f32[6,2,16,128]{3,2,1,0:T(8,128)} %get-tuple-element.11), channel_id=1, source_target_pairs={{0,24},{8,0},{16,8},{24,16},{32,56},{40,32},{48,40},{56,48},{64,88... | collective-permute-start | bytes 294920 | tf_op jit(solution)/shard_map/ppermute | solution.py:222
  35.1 6.4 %collective-permute-start.3 = (f32[6,2,16,128]{3,2,1,0:T(8,128)}, f32[6,2,16,128]{3,2,1,0:T(8,128)S(1)}, u32[]{:S(2)}, u32[]{:S(2)}) collective-permute-start(f32[6,2,16,128]{3,2,1,0:T(8,128)} %get-tuple-element.11), channel_id=1, source_target_pairs={{0,16},{8,24},{16,0},{24,8},{32,48},{40,56},{48,32},{56,40},{64,80... | collective-permute-start | bytes 294920 | tf_op jit(solution)/shard_map/ppermute | solution.py:222
  35.1 7.1 %collective-permute-start.4 = (f32[6,2,16,128]{3,2,1,0:T(8,128)}, f32[6,2,16,128]{3,2,1,0:T(8,128)S(1)}, u32[]{:S(2)}, u32[]{:S(2)}) collective-permute-start(f32[6,2,16,128]{3,2,1,0:T(8,128)} %get-tuple-element.11), channel_id=1, source_target_pairs={{0,8},{8,16},{16,24},{24,0},{32,40},{40,48},{48,56},{56,32},{64,72... | collective-permute-start | bytes 294920 | tf_op jit(solution)/shard_map/ppermute | solution.py:222
  43.3 10.8 %copy-start.7 = (f32[2,16,128]{2,1,0:T(8,128)S(1)}, f32[2,16,128]{2,1,0:T(8,128)}, u32[]{:S(2)}) copy-start(f32[2,16,128]{2,1,0:T(8,128)} %get-tuple-element.35.beta_ref) | copy-start | bytes 49156
  43.3 10.9 %copy-start.6 = (f32[2,16,128]{2,1,0:T(8,128)S(1)}, f32[2,16,128]{2,1,0:T(8,128)}, u32[]{:S(2)}) copy-start(f32[2,16,128]{2,1,0:T(8,128)} %get-tuple-element.53.hi_ref) | copy-start | bytes 49156
  43.3 10.9 %copy-start.3 = (f32[64,16,128]{2,1,0:T(8,128)S(1)}, f32[64,16,128]{2,1,0:T(8,128)}, u32[]{:S(2)}) copy-start(f32[64,16,128]{2,1,0:T(8,128)} %get-tuple-element.13) | copy-start | bytes 1572868
  43.3 10.9 %copy-start.4 = (f32[64,16,128]{2,1,0:T(8,128)S(1)}, f32[64,16,128]{2,1,0:T(8,128)}, u32[]{:S(2)}) copy-start(f32[64,16,128]{2,1,0:T(8,128)} %get-tuple-element.14) | copy-start | bytes 1572868
  43.4 10.9 %copy-start.5 = (f32[64,16,128]{2,1,0:T(8,128)S(1)}, f32[64,16,128]{2,1,0:T(8,128)}, u32[]{:S(2)}) copy-start(f32[64,16,128]{2,1,0:T(8,128)} %get-tuple-element.15) | copy-start | bytes 1572868
  43.4 5.8 %collective-permute-start.5 = (f32[6,2,16,128]{3,2,1,0:T(8,128)S(1)}, f32[6,2,16,128]{3,2,1,0:T(8,128)S(1)}, u32[]{:S(2)}, u32[]{:S(2)}) collective-permute-start(f32[6,2,16,128]{3,2,1,0:T(8,128)S(1)} %fusion.31), channel_id=1, source_target_pairs={{0,96},{8,104},{16,112},{24,120},{32,0},{40,8},{48,16},{56,24},{64... | collective-permute-start | bytes 294920 | tf_op jit(solution)/shard_map/ppermute | solution.py:222
  46.7 6.2 %collective-permute-start.6 = (f32[6,2,16,128]{3,2,1,0:T(8,128)S(1)}, f32[6,2,16,128]{3,2,1,0:T(8,128)S(1)}, u32[]{:S(2)}, u32[]{:S(2)}) collective-permute-start(f32[6,2,16,128]{3,2,1,0:T(8,128)S(1)} %fusion.31), channel_id=1, source_target_pairs={{0,64},{8,72},{16,80},{24,88},{32,96},{40,104},{48,112},{56,120},{... | collective-permute-start | bytes 294920 | tf_op jit(solution)/shard_map/ppermute | solution.py:222
  47.4 6.5 %collective-permute-start.7 = (f32[6,2,16,128]{3,2,1,0:T(8,128)S(1)}, f32[6,2,16,128]{3,2,1,0:T(8,128)S(1)}, u32[]{:S(2)}, u32[]{:S(2)}) collective-permute-start(f32[6,2,16,128]{3,2,1,0:T(8,128)S(1)} %fusion.31), channel_id=1, source_target_pairs={{0,32},{8,40},{16,48},{24,56},{32,64},{40,72},{48,80},{56,88},{64,... | collective-permute-start | bytes 294920 | tf_op jit(solution)/shard_map/ppermute | solution.py:222
  54.2 1.1 %copy-start = (f32[64,16,128]{2,1,0:T(8,128)S(1)}, f32[64,16,128]{2,1,0:T(8,128)}, u32[]{:S(2)}) copy-start(f32[64,16,128]{2,1,0:T(8,128)} %get-tuple-element.9) | copy-start | bytes 1572868
  54.3 1.4 %copy-start.1 = (f32[64,16,128]{2,1,0:T(8,128)S(1)}, f32[64,16,128]{2,1,0:T(8,128)}, u32[]{:S(2)}) copy-start(f32[64,16,128]{2,1,0:T(8,128)} %get-tuple-element.10) | copy-start | bytes 1572868
  54.3 1.5 %copy-start.2 = (f32[64,16,128]{2,1,0:T(8,128)S(1)}, f32[64,16,128]{2,1,0:T(8,128)}, u32[]{:S(2)}) copy-start(f32[64,16,128]{2,1,0:T(8,128)} %get-tuple-element.12) | copy-start | bytes 1572868

commit v6 on v4

--- a/solution.py
+++ b/solution.py
@@ -15,13 +15,13 @@
     return 2.0 * lower * upper / (lower + upper)
 
 
-def local_kernel(rt_ref, ri_ref, ct_ref, ci_ref, src_ref, lo_ref, hi_ref, beta_ref,
+def local_kernel(rt_ref, ri_ref, ct_ref, ci_ref, mt_ref, mi_ref, src_ref, lo_ref, hi_ref, beta_ref,
                  yt_ref, yi_ref, vt_ref, vi_ref, wt_ref, wi_ref, pack_ref):
     z_cells = rt_ref.shape[0]
     y_cells = rt_ref.shape[2]
     fields = (
-        (rt_ref, ct_ref, yt_ref, vt_ref, wt_ref, 0, 1.0),
-        (ri_ref, ci_ref, yi_ref, vi_ref, wi_ref, 1, ion_rate),
+        (rt_ref, ct_ref, yt_ref, vt_ref, wt_ref, 0, mt_ref),
+        (ri_ref, ci_ref, yi_ref, vi_ref, wi_ref, 1, mi_ref),
     )
 
     def absorb_of(k, z):
@@ -31,7 +31,7 @@
     carry = []
     for rhs_ref, c_ref, y_ref, v_ref, w_ref, k, _ in fields:
         below = lo_ref[k]
-        above = face(c_ref[0], c_ref[1])
+        above = c_ref[0]
         main = 1.0 + below + above + absorb_of(k, 0)
         rp = 1.0 / main
         f = -above * rp
@@ -44,10 +44,10 @@
 
     def fwd(z, carry):
         out = []
-        for n, (rhs_ref, c_ref, y_ref, v_ref, w_ref, k, _) in enumerate(fields):
+        for n, (rhs_ref, c_ref, y_ref, v_ref, w_ref, k, m_ref) in enumerate(fields):
             below, f_prev, dy_prev, dv_prev = carry[4 * n:4 * n + 4]
-            above = face(c_ref[z], c_ref[z + 1])
-            main = 1.0 + below + above + absorb_of(k, z)
+            above = c_ref[z]
+            main = m_ref[z] + absorb_of(k, z)
             pivot = main + below * f_prev
             rp = 1.0 / pivot
             f = -above * rp
@@ -104,16 +104,16 @@
         pack_ref[5, k] = y_ref[z_cells - 1]
 
 
-def local_solve(rhs_temp, rhs_ion, cond_temp, cond_ion, sources, lo, hi, beta):
+def local_solve(rhs_temp, rhs_ion, cond_temp, cond_ion, main_temp, main_ion, sources, lo, hi, beta):
     shape = jax.ShapeDtypeStruct(rhs_temp.shape, jnp.float32)
     pack = jax.ShapeDtypeStruct((6,) + lo.shape, jnp.float32)
     vmem = pl.BlockSpec(memory_space=pltpu.VMEM)
     return pl.pallas_call(
         local_kernel,
         out_shape=(shape,) * 6 + (pack,),
-        in_specs=[vmem] * 8,
+        in_specs=[vmem] * 10,
         out_specs=(vmem,) * 7,
-    )(rhs_temp, rhs_ion, cond_temp, cond_ion, sources, lo, hi, beta)
+    )(rhs_temp, rhs_ion, cond_temp, cond_ion, main_temp, main_ion, sources, lo, hi, beta)
 
 
 def chain_solve(packs, rights):
@@ -230,8 +230,15 @@
 
     beta = jnp.where(position == 0, 0.0, lo)
     alpha = hi
+    faces, mains = [], []
+    for cond in (cond_temp, cond_ion):
+        inner = face(cond[:-1], cond[1:])
+        edge = jnp.zeros_like(cond[:1])
+        above = jnp.concatenate([inner, edge])
+        faces.append(above)
+        mains.append(1.0 + jnp.concatenate([edge, inner]) + above)
     yt, yi, vt, vi, wt, wi, pack = local_solve(
-        rhs_temp, rhs_ion, cond_temp, cond_ion, sources, lo, hi, beta
+        rhs_temp, rhs_ion, faces[0], faces[1], mains[0], mains[1], sources, lo, hi, beta
     )
     size = 4 if chain % 4 == 0 and chain > 4 else chain
     groups_z = chain // size

time: 56.1 us -> 56.1 us (level)
  other arithmetic: 5.48 us -> 7.04 us
  local copies, waits for them, and re-layouts: 1.54 us -> 0.79 us
    ppermute x1, waiting for transfers between devices: 4.33 us -> 2.75 us  [body(): lax.ppermute(first, 'gz', [(i + 1, i) for i in range(chain - 1)])]
    add x0 -> x1, other arithmetic: none -> 1.39 us  [body(): mains.append(1.0 + jnp.concatenate([edge, inner]) + above)]
    slice x1, local copies, waits for them, and re-layouts: 0.75 us -> 0.01 us  [body(): first = jnp.stack([cond_temp[0], cond_ion[0]])]
    ppermute x6, starting transfers between devices: 10.6 us -> 9.87 us  [gather_ring(): got[s] = lax.ppermute(pack, 'gz', route)]
    all_to_all x1, waiting for transfers between devices: 1.4 us -> 2.11 us  [deposit(): lax.all_to_all(send, 'gx', split_axis=0, concat_axis=0, tiled=True)]
  transfers between devices with their start and end apart: 9 -> 9, of which waited for: 9 -> 9; matrix products, arithmetic and copies ran while one was open for 4% -> 5% of each run, Pallas kernels for 0% -> 0%
where the time goes in v6:
time: 56.1 us; the launch traced here: 55.8 us
  starting transfers between devices  19.3 us (34%)
  waiting for transfers between devices  18 us (32%)
  other arithmetic  7.04 us (13%)
  Pallas kernels  5.1 us (9%)
  matrix products  4.7 us (8%)
  between operations  0.95 us (2%)
  local copies, waits for them, and re-layouts  0.79 us (1%)
    ppermute x6, waiting for transfers between devices, gather_ring(): got[s] = lax.ppermute(pack, 'gz', route)  11.7 us
    ppermute x6, starting transfers between devices, gather_ring(): got[s] = lax.ppermute(pack, 'gz', route)  9.87 us
    pallas_call x1, Pallas kernels, local_solve(): pl.pallas_call(local_kernel, out_shape=(shape,) * 6 + (pack,), in_specs=[...  5.1 us
    all_to_all x1, starting transfers between devices, deposit(): lax.all_to_all(send, 'gx', split_axis=0, concat_axis=0, tiled=True)  4.71 us
    ppermute x1, starting transfers between devices, body(): lax.ppermute(last, 'gz', [(i, i + 1) for i in range(chain - 1)])  3.38 us
    ppermute x1, waiting for transfers between devices, body(): lax.ppermute(first, 'gz', [(i + 1, i) for i in range(chain - 1)])  2.75 us
    dot_general x1, matrix products, deposit(): send = jnp.einsum('dsr,rk->dsk', pick, stacked, precision=HIGH)  2.5 us
    all_to_all x1, waiting for transfers between devices, deposit(): lax.all_to_all(send, 'gx', split_axis=0, concat_axis=0, tiled=True)  2.11 us
  transfers between devices with their start and end apart: 9, of which 9 were waited for; matrix products, arithmetic and copies ran while one was open for 5% of the time, Pallas kernels for 0%

profile of v6, /device:TPU:0, one launch (start us, length us, event | category | flops | bytes accessed | tf_op | source)
XLA Modules:
  0.0 55.8 jit_solution(15210694787107602001)
XLA Ops:
  0.6 0.7 %fusion.93 = (f32[256]{0:T(256)S(1)}, s32[256]{0:T(256)S(1)}) fusion(s32[256]{0:T(256)} %bitcast.604), kind=kLoop, calls=%fused_computation.221 | loop fusion | flops 5376 | bytes 3072 | tf_op jit(solution)/shard_map/convert_element_type | solution.py:205
  1.3 0.2 fusion.8
  1.5 0.2 fusion.10
  1.8 0.1 fusion.15
  1.9 2.5 %fusion.2 = f32[8,97,256]{2,1,0:T(8,128)} fusion(pred[8,97,256]{2,1,0:T(8,128)(4,1)S(1)} %get-tuple-element.62, pred[8,97,256]{2,1,0:T(8,128)(4,1)S(1)} %get-tuple-element.61, f32[256,256]{1,0:T(8,128)S(1)} %fusion.15, f32[256,128]{1,0:T(8,128)} %bitcast.605, f32[256,128]{1,0:T(8,128)} %bitcast.606), kind=kOutput, calls=%fused_computation.2 | convolution fusion | flops 610930688 | bytes 1716224 | tf_op jit(solution)/shard_map/dsr,rk->dsk/dot_general | solution.py:208
  4.4 0.0 copy-start
  4.4 0.0 copy-start.1
  4.4 4.7 %all-to-all-start = ((f32[8,97,256]{2,1,0:T(8,128)}), f32[8,97,256]{2,1,0:T(8,128)S(1)}, u32[]{:S(2)}, u32[]{:S(2)}) async-start(f32[8,97,256]{2,1,0:T(8,128)} %fusion.2), calls=%async_computation | async-start | bytes 1703936 | tf_op jit(solution)/shard_map/all_to_all | solution.py:209
  9.1 0.0 copy-done
  9.1 0.0 copy-done.1
  9.2 1.3 %collective-permute-start.1 = (f32[2,16,128]{2,1,0:T(8,128)S(1)}, f32[2,16,128]{2,1,0:T(8,128)S(1)}, u32[]{:S(2)}, u32[]{:S(2)}) collective-permute-start(f32[2,16,128]{2,1,0:T(8,128)S(1)} %pad_maximum_fusion), channel_id=1, source_target_pairs={{8,0},{16,8},{24,16},{32,24},{40,32},{48,40},{56,48},{64,56},{72,6... | collective-permute-start | bytes 49160 | tf_op jit(solution)/shard_map/ppermute | solution.py:227
  10.5 0.1 add_divide_fusion
  10.6 0.1 add_divide_fusion.1
  10.7 1.4 %add_add_fusion = (f32[64,16,128]{2,1,0:T(8,128)}, f32[64,16,128]{2,1,0:T(8,128)}, f32[64,16,128]{2,1,0:T(8,128)}, f32[64,16,128]{2,1,0:T(8,128)}) fusion(f32[63,16,128]{2,1,0:T(8,128)S(1)} %add_divide_fusion, f32[63,16,128]{2,1,0:T(8,128)S(1)} %add_divide_fusion.1), kind=kLoop, calls=%fused_computation.21 | loop fusion | flops 524288 | bytes 3129344 | tf_op jit(solution)/shard_map/add | solution.py:239
  12.0 2.7 %collective-permute-done.1 = f32[2,16,128]{2,1,0:T(8,128)S(1)} collective-permute-done((f32[2,16,128]{2,1,0:T(8,128)S(1)}, f32[2,16,128]{2,1,0:T(8,128)S(1)}, u32[]{:S(2)}, u32[]{:S(2)}) %collective-permute-start.1) | collective-permute-done | bytes 16416 | tf_op jit(solution)/shard_map/ppermute | solution.py:227
  14.8 0.6 %divide_select_fusion = (f32[2,16,128]{2,1,0:T(8,128)}, f32[2,16,128]{2,1,0:T(8,128)S(1)}) fusion(f32[2,16,128]{2,1,0:T(8,128)S(1)} %collective-permute-done.1, pred[]{:T(512)S(6)} %eq.204, f32[1,16,128]{2,1,0:T(8,128)S(1)} %get-tuple-element.65, f32[1,16,128]{2,1,0:T(8,128)S(1)} %get-tuple-element.38), kind=kLoop, calls=%fused_computation.193 | loop fusion | flops 24576 | bytes 65537 | tf_op jit(solution)/shard_map/jit(_where)/select_n | solution.py:229
  15.4 3.4 %collective-permute-start = (f32[2,16,128]{2,1,0:T(8,128)S(1)}, f32[2,16,128]{2,1,0:T(8,128)S(1)}, u32[]{:S(2)}, u32[]{:S(2)}) collective-permute-start(f32[2,16,128]{2,1,0:T(8,128)S(1)} %get-tuple-element.58), channel_id=1, source_target_pairs={{0,8},{8,16},{16,24},{24,32},{32,40},{40,48},{48,56},{56,64},{64,7... | collective-permute-start | bytes 49160 | tf_op jit(solution)/shard_map/ppermute | solution.py:226
  18.8 1.4 %collective-permute-done = f32[2,16,128]{2,1,0:T(8,128)S(1)} collective-permute-done((f32[2,16,128]{2,1,0:T(8,128)S(1)}, f32[2,16,128]{2,1,0:T(8,128)S(1)}, u32[]{:S(2)}, u32[]{:S(2)}) %collective-permute-start) | collective-permute-done | bytes 16416 | tf_op jit(solution)/shard_map/ppermute | solution.py:226
  20.2 0.6 %broadcast_select_fusion = (f32[2,16,128]{2,1,0:T(8,128)}, f32[2,16,128]{2,1,0:T(8,128)}) fusion(pred[]{:T(512)S(6)} %eq.203, f32[2,16,128]{2,1,0:T(8,128)S(1)} %collective-permute-done, f32[1,16,128]{2,1,0:T(8,128)S(1)} %get-tuple-element.66, f32[1,16,128]{2,1,0:T(8,128)S(1)} %get-tuple-element.37), kind=kLoop, calls=%fused_computation.210 | loop fusion | flops 32768 | bytes 65537 | tf_op jit(solution)/shard_map/jit(_where)/select_n | solution.py:231
  20.8 2.1 %all-to-all-done = f32[8,97,256]{2,1,0:T(8,128)S(1)} async-done(((f32[8,97,256]{2,1,0:T(8,128)}), f32[8,97,256]{2,1,0:T(8,128)S(1)}, u32[]{:S(2)}, u32[]{:S(2)}) %all-to-all-start) | async-done | bytes 794656 | tf_op jit(solution)/shard_map/all_to_all | solution.py:209
  23.0 0.1 sub.312
  23.0 0.1 slice.233
  23.1 2.0 %fusion.src_ref = f32[64,16,256]{2,1,0:T(8,128)} fusion(f32[768,256,1]{1,0,2:T(8,128)S(1)} %bitcast.603, f32[768]{0:T(1024)S(1)} %sub.312, f32[64,16]{1,0:T(8,128)S(1)} %add_convert_fusion), kind=kOutput, calls=%fused_computation | convolution fusion | flops 1208745984 | bytes 1842176 | tf_op jit(solution)/shard_map/dot_general | solution.py:214
  25.1 5.1 %shard_map.86 = (f32[64,16,128]{2,1,0:T(8,128)}, f32[64,16,128]{2,1,0:T(8,128)}, f32[64,16,128]{2,1,0:T(8,128)}, f32[64,16,128]{2,1,0:T(8,128)}, f32[64,16,128]{...) custom-call(f32[64,16,128]{2,1,0:T(8,128)} %rt_ref.1, f32[64,16,128]{2,1,0:T(8,128)} %ri_ref.1, ...), custom_call_target="tpu_custom_call" | custom-call | tf_op jit(solution)/shard_map/pallas_call | solution.py:111
  30.2 3.6 %collective-permute-start.2 = (f32[6,2,16,128]{3,2,1,0:T(8,128)}, f32[6,2,16,128]{3,2,1,0:T(8,128)S(1)}, u32[]{:S(2)}, u32[]{:S(2)}) collective-permute-start(f32[6,2,16,128]{3,2,1,0:T(8,128)} %get-tuple-element.11), channel_id=1, source_target_pairs={{0,24},{8,0},{16,8},{24,16},{32,56},{40,32},{48,40},{56,48},{64,88... | collective-permute-start | bytes 294920 | tf_op jit(solution)/shard_map/ppermute | solution.py:163
  33.8 0.0 collective-permute-start.3
  33.8 0.9 %collective-permute-start.4 = (f32[6,2,16,128]{3,2,1,0:T(8,128)}, f32[6,2,16,128]{3,2,1,0:T(8,128)S(1)}, u32[]{:S(2)}, u32[]{:S(2)}) collective-permute-start(f32[6,2,16,128]{3,2,1,0:T(8,128)} %get-tuple-element.11), channel_id=1, source_target_pairs={{0,8},{8,16},{16,24},{24,0},{32,40},{40,48},{48,56},{56,32},{64,72... | collective-permute-start | bytes 294920 | tf_op jit(solution)/shard_map/ppermute | solution.py:163
  34.7 2.6 %collective-permute-done.2 = f32[6,2,16,128]{3,2,1,0:T(8,128)S(1)} collective-permute-done((f32[6,2,16,128]{3,2,1,0:T(8,128)}, f32[6,2,16,128]{3,2,1,0:T(8,128)S(1)}, u32[]{:S(2)}, u32[]{:S(2)}) %collective-permute-start.2) | collective-permute-done | bytes 98336 | tf_op jit(solution)/shard_map/ppermute | solution.py:163
  37.3 2.9 %collective-permute-done.3 = f32[6,2,16,128]{3,2,1,0:T(8,128)S(1)} collective-permute-done((f32[6,2,16,128]{3,2,1,0:T(8,128)}, f32[6,2,16,128]{3,2,1,0:T(8,128)S(1)}, u32[]{:S(2)}, u32[]{:S(2)}) %collective-permute-start.3) | collective-permute-done | bytes 98336 | tf_op jit(solution)/shard_map/ppermute | solution.py:163
  40.2 0.7 %collective-permute-done.4 = f32[6,2,16,128]{3,2,1,0:T(8,128)S(1)} collective-permute-done((f32[6,2,16,128]{3,2,1,0:T(8,128)}, f32[6,2,16,128]{3,2,1,0:T(8,128)S(1)}, u32[]{:S(2)}, u32[]{:S(2)}) %collective-permute-start.4) | collective-permute-done | bytes 98336 | tf_op jit(solution)/shard_map/ppermute | solution.py:163
  40.9 0.9 %select_select_fusion.6 = (f32[6,2,16,128]{3,2,1,0:T(8,128)S(1)}, f32[6,2,16,128]{3,2,1,0:T(8,128)S(1)}, f32[6,2,16,128]{3,2,1,0:T(8,128)S(1)}, f32[6,2,16,128]{3,2,1,0:T(8,128)S(1)}) fusion(f32[6,2,16,128]{3,2,1,0:T(8,128)S(1)} %collective-permute-done.2, f32[6,2,16,128]{3,2,1,0:T(8,128)S(1)} %collective-permute-done.3, ...), kind=kLoop, calls=%fused_computation.34 | loop fusion | flops 294912 | bytes 786444 | tf_op jit(solution)/shard_map/jit(_where)/select_n | solution.py:168
  42.0 0.0 copy-start.8
  42.0 0.0 copy-start.9
  42.1 0.0 copy-start.5
  42.1 0.0 copy-start.6
  42.1 0.0 copy-start.7
  42.1 4.0 %collective-permute-start.5 = (f32[6,2,16,128]{3,2,1,0:T(8,128)S(1)}, f32[6,2,16,128]{3,2,1,0:T(8,128)S(1)}, u32[]{:S(2)}, u32[]{:S(2)}) collective-permute-start(f32[6,2,16,128]{3,2,1,0:T(8,128)S(1)} %fusion.31), channel_id=1, source_target_pairs={{0,96},{8,104},{16,112},{24,120},{32,0},{40,8},{48,16},{56,24},{64... | collective-permute-start | bytes 294920 | tf_op jit(solution)/shard_map/ppermute | solution.py:163
  46.1 0.1 collective-permute-start.6
  46.2 1.3 %collective-permute-start.7 = (f32[6,2,16,128]{3,2,1,0:T(8,128)S(1)}, f32[6,2,16,128]{3,2,1,0:T(8,128)S(1)}, u32[]{:S(2)}, u32[]{:S(2)}) collective-permute-start(f32[6,2,16,128]{3,2,1,0:T(8,128)S(1)} %fusion.31), channel_id=1, source_target_pairs={{0,32},{8,40},{16,48},{24,56},{32,64},{40,72},{48,80},{56,88},{64,... | collective-permute-start | bytes 294920 | tf_op jit(solution)/shard_map/ppermute | solution.py:163
  47.5 2.2 %collective-permute-done.5 = f32[6,2,16,128]{3,2,1,0:T(8,128)S(1)} collective-permute-done((f32[6,2,16,128]{3,2,1,0:T(8,128)S(1)}, f32[6,2,16,128]{3,2,1,0:T(8,128)S(1)}, u32[]{:S(2)}, u32[]{:S(2)}) %collective-permute-start.5) | collective-permute-done | bytes 98336 | tf_op jit(solution)/shard_map/ppermute | solution.py:163
  49.6 2.7 %collective-permute-done.6 = f32[6,2,16,128]{3,2,1,0:T(8,128)S(1)} collective-permute-done((f32[6,2,16,128]{3,2,1,0:T(8,128)S(1)}, f32[6,2,16,128]{3,2,1,0:T(8,128)S(1)}, u32[]{:S(2)}, u32[]{:S(2)}) %collective-permute-start.6) | collective-permute-done | bytes 98336 | tf_op jit(solution)/shard_map/ppermute | solution.py:163
  52.3 0.7 %collective-permute-done.7 = f32[6,2,16,128]{3,2,1,0:T(8,128)S(1)} collective-permute-done((f32[6,2,16,128]{3,2,1,0:T(8,128)S(1)}, f32[6,2,16,128]{3,2,1,0:T(8,128)S(1)}, u32[]{:S(2)}, u32[]{:S(2)}) %collective-permute-start.7) | collective-permute-done | bytes 98336 | tf_op jit(solution)/shard_map/ppermute | solution.py:163
  53.0 0.1 select_select_fusion.1
  53.1 0.1 fusion.50
  53.2 0.1 select_select_fusion.8
  53.3 0.0 copy-done.8
  53.3 0.0 copy-done.9
  53.3 0.0 copy-done.5
  53.4 0.0 copy-done.6
  53.4 0.0 copy-done.7
  53.4 0.0 copy-start.2
  53.4 0.0 copy-start.3
  53.4 0.0 copy-start.4
  53.4 0.9 %multiply_add_fusion.1 = f32[64,16,128]{2,1,0:T(8,128)} fusion(f32[64,16,128]{2,1,0:T(8,128)S(1)} %copy-done.7, f32[64,16,128]{2,1,0:T(8,128)S(1)} %copy-done.5, f32[64,16,128]{2,1,0:T(8,128)S(1)} %copy-done.6, f32[16,128]{1,0:T(8,128)S(1)} %get-tuple-element.56, f32[16,128]{1,0:T(8,128)S(1)} %get-tuple-element.54), kind=kLoop, calls=%fused_computation.20 | loop fusion | flops 524288 | bytes 2113536 | tf_op jit(solution)/shard_map/add | solution.py:288
  54.3 0.1 copy-done.2
  54.4 0.3 copy-done.3
  54.8 0.2 copy-done.4
  54.9 0.9 %multiply_add_fusion = f32[64,16,128]{2,1,0:T(8,128)} fusion(f32[64,16,128]{2,1,0:T(8,128)S(1)} %copy-done.4, f32[64,16,128]{2,1,0:T(8,128)S(1)} %copy-done.2, f32[64,16,128]{2,1,0:T(8,128)S(1)} %copy-done.3, f32[16,128]{1,0:T(8,128)S(1)} %get-tuple-element.55, f32[16,128]{1,0:T(8,128)S(1)} %get-tuple-element.53), kind=kLoop, calls=%fused_computation.19 | loop fusion | flops 524288 | bytes 2113536 | tf_op jit(solution)/shard_map/add | solution.py:288
  (16 shorter events, 0.2 us)
Async XLA Ops:
  4.4 4.7 %copy-start = (f32[64,16,128]{2,1,0:T(8,128)S(1)}, f32[64,16,128]{2,1,0:T(8,128)}, u32[]{:S(2)}) copy-start(f32[64,16,128]{2,1,0:T(8,128)} %param.10) | copy-start | bytes 1572868
  4.4 4.7 %copy-start.1 = (f32[64,16,128]{2,1,0:T(8,128)S(1)}, f32[64,16,128]{2,1,0:T(8,128)}, u32[]{:S(2)}) copy-start(f32[64,16,128]{2,1,0:T(8,128)} %param.9) | copy-start | bytes 1572868
  4.4 18.5 %all-to-all-start = ((f32[8,97,256]{2,1,0:T(8,128)}), f32[8,97,256]{2,1,0:T(8,128)S(1)}, u32[]{:S(2)}, u32[]{:S(2)}) async-start(f32[8,97,256]{2,1,0:T(8,128)} %fusion.2), calls=%async_computation | async-start | bytes 1703936 | tf_op jit(solution)/shard_map/all_to_all | solution.py:209
  9.2 5.6 %collective-permute-start.1 = (f32[2,16,128]{2,1,0:T(8,128)S(1)}, f32[2,16,128]{2,1,0:T(8,128)S(1)}, u32[]{:S(2)}, u32[]{:S(2)}) collective-permute-start(f32[2,16,128]{2,1,0:T(8,128)S(1)} %pad_maximum_fusion), channel_id=1, source_target_pairs={{8,0},{16,8},{24,16},{32,24},{40,32},{48,40},{56,48},{64,56},{72,6... | collective-permute-start | bytes 49160 | tf_op jit(solution)/shard_map/ppermute | solution.py:227
  15.4 4.8 %collective-permute-start = (f32[2,16,128]{2,1,0:T(8,128)S(1)}, f32[2,16,128]{2,1,0:T(8,128)S(1)}, u32[]{:S(2)}, u32[]{:S(2)}) collective-permute-start(f32[2,16,128]{2,1,0:T(8,128)S(1)} %get-tuple-element.58), channel_id=1, source_target_pairs={{0,8},{8,16},{16,24},{24,32},{32,40},{40,48},{48,56},{56,64},{64,7... | collective-permute-start | bytes 49160 | tf_op jit(solution)/shard_map/ppermute | solution.py:226
  30.2 7.1 %collective-permute-start.2 = (f32[6,2,16,128]{3,2,1,0:T(8,128)}, f32[6,2,16,128]{3,2,1,0:T(8,128)S(1)}, u32[]{:S(2)}, u32[]{:S(2)}) collective-permute-start(f32[6,2,16,128]{3,2,1,0:T(8,128)} %get-tuple-element.11), channel_id=1, source_target_pairs={{0,24},{8,0},{16,8},{24,16},{32,56},{40,32},{48,40},{56,48},{64,88... | collective-permute-start | bytes 294920 | tf_op jit(solution)/shard_map/ppermute | solution.py:163
  33.8 6.4 %collective-permute-start.3 = (f32[6,2,16,128]{3,2,1,0:T(8,128)}, f32[6,2,16,128]{3,2,1,0:T(8,128)S(1)}, u32[]{:S(2)}, u32[]{:S(2)}) collective-permute-start(f32[6,2,16,128]{3,2,1,0:T(8,128)} %get-tuple-element.11), channel_id=1, source_target_pairs={{0,16},{8,24},{16,0},{24,8},{32,48},{40,56},{48,32},{56,40},{64,80... | collective-permute-start | bytes 294920 | tf_op jit(solution)/shard_map/ppermute | solution.py:163
  33.8 7.1 %collective-permute-start.4 = (f32[6,2,16,128]{3,2,1,0:T(8,128)}, f32[6,2,16,128]{3,2,1,0:T(8,128)S(1)}, u32[]{:S(2)}, u32[]{:S(2)}) collective-permute-start(f32[6,2,16,128]{3,2,1,0:T(8,128)} %get-tuple-element.11), channel_id=1, source_target_pairs={{0,8},{8,16},{16,24},{24,0},{32,40},{40,48},{48,56},{56,32},{64,72... | collective-permute-start | bytes 294920 | tf_op jit(solution)/shard_map/ppermute | solution.py:163
  42.0 11.3 %copy-start.8 = (f32[2,16,128]{2,1,0:T(8,128)S(1)}, f32[2,16,128]{2,1,0:T(8,128)}, u32[]{:S(2)}) copy-start(f32[2,16,128]{2,1,0:T(8,128)} %get-tuple-element.57.hi_ref) | copy-start | bytes 49156
  42.0 11.3 %copy-start.9 = (f32[2,16,128]{2,1,0:T(8,128)S(1)}, f32[2,16,128]{2,1,0:T(8,128)}, u32[]{:S(2)}) copy-start(f32[2,16,128]{2,1,0:T(8,128)} %get-tuple-element.35.beta_ref) | copy-start | bytes 49156
  42.1 11.3 %copy-start.5 = (f32[64,16,128]{2,1,0:T(8,128)S(1)}, f32[64,16,128]{2,1,0:T(8,128)}, u32[]{:S(2)}) copy-start(f32[64,16,128]{2,1,0:T(8,128)} %get-tuple-element.9) | copy-start | bytes 1572868
  42.1 11.3 %copy-start.6 = (f32[64,16,128]{2,1,0:T(8,128)S(1)}, f32[64,16,128]{2,1,0:T(8,128)}, u32[]{:S(2)}) copy-start(f32[64,16,128]{2,1,0:T(8,128)} %get-tuple-element.10) | copy-start | bytes 1572868
  42.1 11.3 %copy-start.7 = (f32[64,16,128]{2,1,0:T(8,128)S(1)}, f32[64,16,128]{2,1,0:T(8,128)}, u32[]{:S(2)}) copy-start(f32[64,16,128]{2,1,0:T(8,128)} %get-tuple-element.12) | copy-start | bytes 1572868
  42.1 7.5 %collective-permute-start.5 = (f32[6,2,16,128]{3,2,1,0:T(8,128)S(1)}, f32[6,2,16,128]{3,2,1,0:T(8,128)S(1)}, u32[]{:S(2)}, u32[]{:S(2)}) collective-permute-start(f32[6,2,16,128]{3,2,1,0:T(8,128)S(1)} %fusion.31), channel_id=1, source_target_pairs={{0,96},{8,104},{16,112},{24,120},{32,0},{40,8},{48,16},{56,24},{64... | collective-permute-start | bytes 294920 | tf_op jit(solution)/shard_map/ppermute | solution.py:163
  46.1 6.2 %collective-permute-start.6 = (f32[6,2,16,128]{3,2,1,0:T(8,128)S(1)}, f32[6,2,16,128]{3,2,1,0:T(8,128)S(1)}, u32[]{:S(2)}, u32[]{:S(2)}) collective-permute-start(f32[6,2,16,128]{3,2,1,0:T(8,128)S(1)} %fusion.31), channel_id=1, source_target_pairs={{0,64},{8,72},{16,80},{24,88},{32,96},{40,104},{48,112},{56,120},{... | collective-permute-start | bytes 294920 | tf_op jit(solution)/shard_map/ppermute | solution.py:163
  46.2 6.9 %collective-permute-start.7 = (f32[6,2,16,128]{3,2,1,0:T(8,128)S(1)}, f32[6,2,16,128]{3,2,1,0:T(8,128)S(1)}, u32[]{:S(2)}, u32[]{:S(2)}) collective-permute-start(f32[6,2,16,128]{3,2,1,0:T(8,128)S(1)} %fusion.31), channel_id=1, source_target_pairs={{0,32},{8,40},{16,48},{24,56},{32,64},{40,72},{48,80},{56,88},{64,... | collective-permute-start | bytes 294920 | tf_op jit(solution)/shard_map/ppermute | solution.py:163
  53.4 1.1 %copy-start.2 = (f32[64,16,128]{2,1,0:T(8,128)S(1)}, f32[64,16,128]{2,1,0:T(8,128)}, u32[]{:S(2)}) copy-start(f32[64,16,128]{2,1,0:T(8,128)} %get-tuple-element.13) | copy-start | bytes 1572868
  53.4 1.4 %copy-start.3 = (f32[64,16,128]{2,1,0:T(8,128)S(1)}, f32[64,16,128]{2,1,0:T(8,128)}, u32[]{:S(2)}) copy-start(f32[64,16,128]{2,1,0:T(8,128)} %get-tuple-element.14) | copy-start | bytes 1572868
  53.4 1.5 %copy-start.4 = (f32[64,16,128]{2,1,0:T(8,128)S(1)}, f32[64,16,128]{2,1,0:T(8,128)}, u32[]{:S(2)}) copy-start(f32[64,16,128]{2,1,0:T(8,128)} %get-tuple-element.15) | copy-start | bytes 1572868

commit v7 on v4

--- a/solution.py
+++ b/solution.py
@@ -59,7 +59,7 @@
             out += [above, f, dy, dv]
         return tuple(out)
 
-    carry = lax.fori_loop(1, z_cells - 1, fwd, tuple(carry), unroll=8)
+    carry = lax.fori_loop(1, z_cells - 1, fwd, tuple(carry), unroll=True)
 
     z = z_cells - 1
     back = []
@@ -91,7 +91,7 @@
             out += [y_val, v_val, w_val]
         return tuple(out)
 
-    back = lax.fori_loop(0, z_cells - 1, bwd, tuple(back), unroll=8)
+    back = lax.fori_loop(0, z_cells - 1, bwd, tuple(back), unroll=True)
     for n, (rhs_ref, c_ref, y_ref, v_ref, w_ref, k, _) in enumerate(fields):
         y_first, v_first, w_first = back[3 * n:3 * n + 3]
         beta = beta_ref[k]

time: 56.1 us -> 55.5 us (0.989)
  Pallas kernels: 4.86 us -> 4.22 us
    pallas_call x1, Pallas kernels: 4.86 us -> 4.22 us  [local_solve(): pl.pallas_call(local_kernel, out_shape=(shape,) * 6 + (pack,), in_specs=[...]
where the time goes in v7:
time: 55.5 us; the launch traced here: 55.1 us
  starting transfers between devices  19.8 us (36%)
  waiting for transfers between devices  18.4 us (33%)
  other arithmetic  5.48 us (10%)
  matrix products  4.72 us (9%)
  Pallas kernels  4.22 us (8%)
  local copies, waits for them, and re-layouts  1.54 us (3%)
  between operations  0.91 us (2%)
    ppermute x6, waiting for transfers between devices, gather_ring(): got[s] = lax.ppermute(pack, 'gz', route)  11.3 us
    ppermute x6, starting transfers between devices, gather_ring(): got[s] = lax.ppermute(pack, 'gz', route)  10.6 us
    all_to_all x1, starting transfers between devices, deposit(): lax.all_to_all(send, 'gx', split_axis=0, concat_axis=0, tiled=True)  4.58 us
    ppermute x1, waiting for transfers between devices, body(): lax.ppermute(first, 'gz', [(i + 1, i) for i in range(chain - 1)])  4.33 us
    pallas_call x1, Pallas kernels, local_solve(): pl.pallas_call(local_kernel, out_shape=(shape,) * 6 + (pack,), in_specs=[...  4.22 us
    ppermute x1, starting transfers between devices, body(): lax.ppermute(last, 'gz', [(i, i + 1) for i in range(chain - 1)])  3.38 us
    dot_general x1, matrix products, deposit(): send = jnp.einsum('dsr,rk->dsk', pick, stacked, precision=HIGH)  2.51 us
    dot_general x1, matrix products, deposit(): sources = jnp.dot(spread, rows, precision=HIGH)  2.02 us
  transfers between devices with their start and end apart: 9, of which 9 were waited for; matrix products, arithmetic and copies ran while one was open for 4% of the time, Pallas kernels for 0%

profile of v7, /device:TPU:0, one launch (start us, length us, event | category | flops | bytes accessed | tf_op | source)
XLA Modules:
  0.0 55.1 jit_solution(11856860209009885704)
XLA Ops:
  0.6 0.7 %fusion.93 = (f32[256]{0:T(256)S(1)}, s32[256]{0:T(256)S(1)}) fusion(s32[256]{0:T(256)} %bitcast.604), kind=kLoop, calls=%fused_computation.217 | loop fusion | flops 5376 | bytes 3072 | tf_op jit(solution)/shard_map/convert_element_type | solution.py:205
  1.3 0.2 fusion.8
  1.5 0.2 fusion.10
  1.8 0.1 fusion.15
  1.9 2.5 %fusion.2 = f32[8,97,256]{2,1,0:T(8,128)} fusion(pred[8,97,256]{2,1,0:T(8,128)(4,1)S(1)} %get-tuple-element.58, pred[8,97,256]{2,1,0:T(8,128)(4,1)S(1)} %get-tuple-element.57, f32[256,256]{1,0:T(8,128)S(1)} %fusion.15, f32[256,128]{1,0:T(8,128)} %bitcast.605, f32[256,128]{1,0:T(8,128)} %bitcast.606), kind=kOutput, calls=%fused_computation.2 | convolution fusion | flops 610930688 | bytes 1716224 | tf_op jit(solution)/shard_map/dsr,rk->dsk/dot_general | solution.py:208
  4.4 4.6 %all-to-all-start = ((f32[8,97,256]{2,1,0:T(8,128)}), f32[8,97,256]{2,1,0:T(8,128)S(1)}, u32[]{:S(2)}, u32[]{:S(2)}) async-start(f32[8,97,256]{2,1,0:T(8,128)} %fusion.2), calls=%async_computation | async-start | bytes 1703936 | tf_op jit(solution)/shard_map/all_to_all | solution.py:209
  9.0 0.7 %fusion.96 = (f32[1,16,128]{2,1,0:T(8,128)S(1)}, f32[1,16,128]{2,1,0:T(8,128)S(1)}, f32[1,16,128]{2,1,0:T(8,128)S(1)}, f32[1,16,128]{2,1,0:T(8,128)S(1)}) fusion(f32[64,16,128]{2,1,0:T(8,128)} %ct_ref.1, f32[64,16,128]{2,1,0:T(8,128)} %ci_ref.1), kind=kLoop, calls=%fused_computation.223 | loop fusion | bytes 65536 | tf_op jit(solution)/shard_map/slice | solution.py:224
  9.7 1.3 %collective-permute-start.1 = (f32[2,16,128]{2,1,0:T(8,128)S(1)}, f32[2,16,128]{2,1,0:T(8,128)S(1)}, u32[]{:S(2)}, u32[]{:S(2)}) collective-permute-start(f32[2,16,128]{2,1,0:T(8,128)S(1)} %pad_maximum_fusion), channel_id=1, source_target_pairs={{8,0},{16,8},{24,16},{32,24},{40,32},{48,40},{56,48},{64,56},{72,6... | collective-permute-start | bytes 49160 | tf_op jit(solution)/shard_map/ppermute | solution.py:227
  11.0 4.3 %collective-permute-done.1 = f32[2,16,128]{2,1,0:T(8,128)S(1)} collective-permute-done((f32[2,16,128]{2,1,0:T(8,128)S(1)}, f32[2,16,128]{2,1,0:T(8,128)S(1)}, u32[]{:S(2)}, u32[]{:S(2)}) %collective-permute-start.1) | collective-permute-done | bytes 16416 | tf_op jit(solution)/shard_map/ppermute | solution.py:227
  15.4 0.6 %divide_select_fusion = (f32[2,16,128]{2,1,0:T(8,128)}, f32[2,16,128]{2,1,0:T(8,128)S(1)}) fusion(f32[2,16,128]{2,1,0:T(8,128)S(1)} %collective-permute-done.1, pred[]{:T(512)S(6)} %eq.204, f32[1,16,128]{2,1,0:T(8,128)S(1)} %get-tuple-element.59, f32[1,16,128]{2,1,0:T(8,128)S(1)} %get-tuple-element.38), kind=kLoop, calls=%fused_computation.189 | loop fusion | flops 24576 | bytes 65537 | tf_op jit(solution)/shard_map/jit(_where)/select_n | solution.py:229
  16.0 3.4 %collective-permute-start = (f32[2,16,128]{2,1,0:T(8,128)S(1)}, f32[2,16,128]{2,1,0:T(8,128)S(1)}, u32[]{:S(2)}, u32[]{:S(2)}) collective-permute-start(f32[2,16,128]{2,1,0:T(8,128)S(1)} %get-tuple-element.54), channel_id=1, source_target_pairs={{0,8},{8,16},{16,24},{24,32},{32,40},{40,48},{48,56},{56,64},{64,7... | collective-permute-start | bytes 49160 | tf_op jit(solution)/shard_map/ppermute | solution.py:226
  19.4 1.4 %collective-permute-done = f32[2,16,128]{2,1,0:T(8,128)S(1)} collective-permute-done((f32[2,16,128]{2,1,0:T(8,128)S(1)}, f32[2,16,128]{2,1,0:T(8,128)S(1)}, u32[]{:S(2)}, u32[]{:S(2)}) %collective-permute-start) | collective-permute-done | bytes 16416 | tf_op jit(solution)/shard_map/ppermute | solution.py:226
  20.8 0.6 %broadcast_select_fusion = (f32[2,16,128]{2,1,0:T(8,128)}, f32[2,16,128]{2,1,0:T(8,128)}) fusion(pred[]{:T(512)S(6)} %eq.203, f32[2,16,128]{2,1,0:T(8,128)S(1)} %collective-permute-done, f32[1,16,128]{2,1,0:T(8,128)S(1)} %get-tuple-element.60, f32[1,16,128]{2,1,0:T(8,128)S(1)} %get-tuple-element.37), kind=kLoop, calls=%fused_computation.206 | loop fusion | flops 32768 | bytes 65537 | tf_op jit(solution)/shard_map/jit(_where)/select_n | solution.py:231
  21.4 1.4 %all-to-all-done = f32[8,97,256]{2,1,0:T(8,128)S(1)} async-done(((f32[8,97,256]{2,1,0:T(8,128)}), f32[8,97,256]{2,1,0:T(8,128)S(1)}, u32[]{:S(2)}, u32[]{:S(2)}) %all-to-all-start) | async-done | bytes 794656 | tf_op jit(solution)/shard_map/all_to_all | solution.py:209
  22.8 0.1 sub.312
  22.9 0.1 slice.217
  23.0 2.0 %fusion.src_ref = f32[64,16,256]{2,1,0:T(8,128)} fusion(f32[768,256,1]{1,0,2:T(8,128)S(1)} %bitcast.603, f32[768]{0:T(1024)S(1)} %sub.312, f32[64,16]{1,0:T(8,128)S(1)} %add_convert_fusion), kind=kOutput, calls=%fused_computation | convolution fusion | flops 1208745984 | bytes 1842176 | tf_op jit(solution)/shard_map/dot_general | solution.py:214
  25.0 4.2 %shard_map.86 = (f32[64,16,128]{2,1,0:T(8,128)}, f32[64,16,128]{2,1,0:T(8,128)}, f32[64,16,128]{2,1,0:T(8,128)}, f32[64,16,128]{2,1,0:T(8,128)}, f32[64,16,128]{...) custom-call(f32[64,16,128]{2,1,0:T(8,128)} %rt_ref.1, f32[64,16,128]{2,1,0:T(8,128)} %ri_ref.1, ...), custom_call_target="tpu_custom_call" | custom-call | tf_op jit(solution)/shard_map/pallas_call | solution.py:111
  29.2 4.3 %collective-permute-start.2 = (f32[6,2,16,128]{3,2,1,0:T(8,128)}, f32[6,2,16,128]{3,2,1,0:T(8,128)S(1)}, u32[]{:S(2)}, u32[]{:S(2)}) collective-permute-start(f32[6,2,16,128]{3,2,1,0:T(8,128)} %get-tuple-element.11), channel_id=1, source_target_pairs={{0,24},{8,0},{16,8},{24,16},{32,56},{40,32},{48,40},{56,48},{64,88... | collective-permute-start | bytes 294920 | tf_op jit(solution)/shard_map/ppermute | solution.py:163
  33.5 0.0 collective-permute-start.3
  33.5 0.9 %collective-permute-start.4 = (f32[6,2,16,128]{3,2,1,0:T(8,128)}, f32[6,2,16,128]{3,2,1,0:T(8,128)S(1)}, u32[]{:S(2)}, u32[]{:S(2)}) collective-permute-start(f32[6,2,16,128]{3,2,1,0:T(8,128)} %get-tuple-element.11), channel_id=1, source_target_pairs={{0,8},{8,16},{16,24},{24,0},{32,40},{40,48},{48,56},{56,32},{64,72... | collective-permute-start | bytes 294920 | tf_op jit(solution)/shard_map/ppermute | solution.py:163
  34.4 2.6 %collective-permute-done.2 = f32[6,2,16,128]{3,2,1,0:T(8,128)S(1)} collective-permute-done((f32[6,2,16,128]{3,2,1,0:T(8,128)}, f32[6,2,16,128]{3,2,1,0:T(8,128)S(1)}, u32[]{:S(2)}, u32[]{:S(2)}) %collective-permute-start.2) | collective-permute-done | bytes 98336 | tf_op jit(solution)/shard_map/ppermute | solution.py:163
  37.0 2.9 %collective-permute-done.3 = f32[6,2,16,128]{3,2,1,0:T(8,128)S(1)} collective-permute-done((f32[6,2,16,128]{3,2,1,0:T(8,128)}, f32[6,2,16,128]{3,2,1,0:T(8,128)S(1)}, u32[]{:S(2)}, u32[]{:S(2)}) %collective-permute-start.3) | collective-permute-done | bytes 98336 | tf_op jit(solution)/shard_map/ppermute | solution.py:163
  39.9 0.7 %collective-permute-done.4 = f32[6,2,16,128]{3,2,1,0:T(8,128)S(1)} collective-permute-done((f32[6,2,16,128]{3,2,1,0:T(8,128)}, f32[6,2,16,128]{3,2,1,0:T(8,128)S(1)}, u32[]{:S(2)}, u32[]{:S(2)}) %collective-permute-start.4) | collective-permute-done | bytes 98336 | tf_op jit(solution)/shard_map/ppermute | solution.py:163
  40.6 0.9 %select_select_fusion.6 = (f32[6,2,16,128]{3,2,1,0:T(8,128)S(1)}, f32[6,2,16,128]{3,2,1,0:T(8,128)S(1)}, f32[6,2,16,128]{3,2,1,0:T(8,128)S(1)}, f32[6,2,16,128]{3,2,1,0:T(8,128)S(1)}) fusion(f32[6,2,16,128]{3,2,1,0:T(8,128)S(1)} %collective-permute-done.2, f32[6,2,16,128]{3,2,1,0:T(8,128)S(1)} %collective-permute-done.3, ...), kind=kLoop, calls=%fused_computation.30 | loop fusion | flops 294912 | bytes 786444 | tf_op jit(solution)/shard_map/jit(_where)/select_n | solution.py:168
  41.7 0.0 copy-start.7
  41.8 0.0 copy-start.6
  41.8 0.0 copy-start.3
  41.8 0.0 copy-start.4
  41.8 0.0 copy-start.5
  41.8 3.3 %collective-permute-start.5 = (f32[6,2,16,128]{3,2,1,0:T(8,128)S(1)}, f32[6,2,16,128]{3,2,1,0:T(8,128)S(1)}, u32[]{:S(2)}, u32[]{:S(2)}) collective-permute-start(f32[6,2,16,128]{3,2,1,0:T(8,128)S(1)} %fusion.31), channel_id=1, source_target_pairs={{0,96},{8,104},{16,112},{24,120},{32,0},{40,8},{48,16},{56,24},{64... | collective-permute-start | bytes 294920 | tf_op jit(solution)/shard_map/ppermute | solution.py:163
  45.1 0.8 %collective-permute-start.6 = (f32[6,2,16,128]{3,2,1,0:T(8,128)S(1)}, f32[6,2,16,128]{3,2,1,0:T(8,128)S(1)}, u32[]{:S(2)}, u32[]{:S(2)}) collective-permute-start(f32[6,2,16,128]{3,2,1,0:T(8,128)S(1)} %fusion.31), channel_id=1, source_target_pairs={{0,64},{8,72},{16,80},{24,88},{32,96},{40,104},{48,112},{56,120},{... | collective-permute-start | bytes 294920 | tf_op jit(solution)/shard_map/ppermute | solution.py:163
  45.9 1.3 %collective-permute-start.7 = (f32[6,2,16,128]{3,2,1,0:T(8,128)S(1)}, f32[6,2,16,128]{3,2,1,0:T(8,128)S(1)}, u32[]{:S(2)}, u32[]{:S(2)}) collective-permute-start(f32[6,2,16,128]{3,2,1,0:T(8,128)S(1)} %fusion.31), channel_id=1, source_target_pairs={{0,32},{8,40},{16,48},{24,56},{32,64},{40,72},{48,80},{56,88},{64,... | collective-permute-start | bytes 294920 | tf_op jit(solution)/shard_map/ppermute | solution.py:163
  47.2 0.4 collective-permute-done.5
  47.6 3.7 %collective-permute-done.6 = f32[6,2,16,128]{3,2,1,0:T(8,128)S(1)} collective-permute-done((f32[6,2,16,128]{3,2,1,0:T(8,128)S(1)}, f32[6,2,16,128]{3,2,1,0:T(8,128)S(1)}, u32[]{:S(2)}, u32[]{:S(2)}) %collective-permute-start.6) | collective-permute-done | bytes 98336 | tf_op jit(solution)/shard_map/ppermute | solution.py:163
  51.3 1.1 %collective-permute-done.7 = f32[6,2,16,128]{3,2,1,0:T(8,128)S(1)} collective-permute-done((f32[6,2,16,128]{3,2,1,0:T(8,128)S(1)}, f32[6,2,16,128]{3,2,1,0:T(8,128)S(1)}, u32[]{:S(2)}, u32[]{:S(2)}) %collective-permute-start.7) | collective-permute-done | bytes 98336 | tf_op jit(solution)/shard_map/ppermute | solution.py:163
  52.3 0.1 select_select_fusion.1
  52.4 0.1 fusion.50
  52.5 0.0 copy-done.7
  52.5 0.1 select_select_fusion.8
  52.6 0.0 copy-done.6
  52.6 0.0 copy-done.3
  52.7 0.0 copy-done.4
  52.7 0.0 copy-done.5
  52.7 0.0 copy-start
  52.7 0.0 copy-start.1
  52.7 0.0 copy-start.2
  52.7 0.9 %multiply_add_fusion = f32[64,16,128]{2,1,0:T(8,128)} fusion(f32[64,16,128]{2,1,0:T(8,128)S(1)} %copy-done.5, f32[64,16,128]{2,1,0:T(8,128)S(1)} %copy-done.3, f32[64,16,128]{2,1,0:T(8,128)S(1)} %copy-done.4, f32[16,128]{1,0:T(8,128)S(1)} %get-tuple-element.51, f32[16,128]{1,0:T(8,128)S(1)} %get-tuple-element.49), kind=kLoop, calls=%fused_computation.19 | loop fusion | flops 524288 | bytes 2113536 | tf_op jit(solution)/shard_map/add | solution.py:281
  53.6 0.1 copy-done
  53.7 0.3 copy-done.1
  54.1 0.2 copy-done.2
  54.2 0.9 %multiply_add_fusion.1 = f32[64,16,128]{2,1,0:T(8,128)} fusion(f32[64,16,128]{2,1,0:T(8,128)S(1)} %copy-done.2, f32[64,16,128]{2,1,0:T(8,128)S(1)} %copy-done, f32[64,16,128]{2,1,0:T(8,128)S(1)} %copy-done.1, f32[16,128]{1,0:T(8,128)S(1)} %get-tuple-element.52, f32[16,128]{1,0:T(8,128)S(1)} %get-tuple-element.50), kind=kLoop, calls=%fused_computation.20 | loop fusion | flops 524288 | bytes 2113536 | tf_op jit(solution)/shard_map/add | solution.py:281
  (15 shorter events, 0.2 us)
Async XLA Ops:
  4.4 18.4 %all-to-all-start = ((f32[8,97,256]{2,1,0:T(8,128)}), f32[8,97,256]{2,1,0:T(8,128)S(1)}, u32[]{:S(2)}, u32[]{:S(2)}) async-start(f32[8,97,256]{2,1,0:T(8,128)} %fusion.2), calls=%async_computation | async-start | bytes 1703936 | tf_op jit(solution)/shard_map/all_to_all | solution.py:209
  9.7 5.6 %collective-permute-start.1 = (f32[2,16,128]{2,1,0:T(8,128)S(1)}, f32[2,16,128]{2,1,0:T(8,128)S(1)}, u32[]{:S(2)}, u32[]{:S(2)}) collective-permute-start(f32[2,16,128]{2,1,0:T(8,128)S(1)} %pad_maximum_fusion), channel_id=1, source_target_pairs={{8,0},{16,8},{24,16},{32,24},{40,32},{48,40},{56,48},{64,56},{72,6... | collective-permute-start | bytes 49160 | tf_op jit(solution)/shard_map/ppermute | solution.py:227
  16.0 4.8 %collective-permute-start = (f32[2,16,128]{2,1,0:T(8,128)S(1)}, f32[2,16,128]{2,1,0:T(8,128)S(1)}, u32[]{:S(2)}, u32[]{:S(2)}) collective-permute-start(f32[2,16,128]{2,1,0:T(8,128)S(1)} %get-tuple-element.54), channel_id=1, source_target_pairs={{0,8},{8,16},{16,24},{24,32},{32,40},{40,48},{48,56},{56,64},{64,7... | collective-permute-start | bytes 49160 | tf_op jit(solution)/shard_map/ppermute | solution.py:226
  29.2 7.8 %collective-permute-start.2 = (f32[6,2,16,128]{3,2,1,0:T(8,128)}, f32[6,2,16,128]{3,2,1,0:T(8,128)S(1)}, u32[]{:S(2)}, u32[]{:S(2)}) collective-permute-start(f32[6,2,16,128]{3,2,1,0:T(8,128)} %get-tuple-element.11), channel_id=1, source_target_pairs={{0,24},{8,0},{16,8},{24,16},{32,56},{40,32},{48,40},{56,48},{64,88... | collective-permute-start | bytes 294920 | tf_op jit(solution)/shard_map/ppermute | solution.py:163
  33.5 6.4 %collective-permute-start.3 = (f32[6,2,16,128]{3,2,1,0:T(8,128)}, f32[6,2,16,128]{3,2,1,0:T(8,128)S(1)}, u32[]{:S(2)}, u32[]{:S(2)}) collective-permute-start(f32[6,2,16,128]{3,2,1,0:T(8,128)} %get-tuple-element.11), channel_id=1, source_target_pairs={{0,16},{8,24},{16,0},{24,8},{32,48},{40,56},{48,32},{56,40},{64,80... | collective-permute-start | bytes 294920 | tf_op jit(solution)/shard_map/ppermute | solution.py:163
  33.5 7.1 %collective-permute-start.4 = (f32[6,2,16,128]{3,2,1,0:T(8,128)}, f32[6,2,16,128]{3,2,1,0:T(8,128)S(1)}, u32[]{:S(2)}, u32[]{:S(2)}) collective-permute-start(f32[6,2,16,128]{3,2,1,0:T(8,128)} %get-tuple-element.11), channel_id=1, source_target_pairs={{0,8},{8,16},{16,24},{24,0},{32,40},{40,48},{48,56},{56,32},{64,72... | collective-permute-start | bytes 294920 | tf_op jit(solution)/shard_map/ppermute | solution.py:163
  41.7 10.8 %copy-start.7 = (f32[2,16,128]{2,1,0:T(8,128)S(1)}, f32[2,16,128]{2,1,0:T(8,128)}, u32[]{:S(2)}) copy-start(f32[2,16,128]{2,1,0:T(8,128)} %get-tuple-element.35.beta_ref) | copy-start | bytes 49156
  41.8 10.9 %copy-start.6 = (f32[2,16,128]{2,1,0:T(8,128)S(1)}, f32[2,16,128]{2,1,0:T(8,128)}, u32[]{:S(2)}) copy-start(f32[2,16,128]{2,1,0:T(8,128)} %get-tuple-element.53.hi_ref) | copy-start | bytes 49156
  41.8 10.9 %copy-start.3 = (f32[64,16,128]{2,1,0:T(8,128)S(1)}, f32[64,16,128]{2,1,0:T(8,128)}, u32[]{:S(2)}) copy-start(f32[64,16,128]{2,1,0:T(8,128)} %get-tuple-element.13) | copy-start | bytes 1572868
  41.8 10.9 %copy-start.4 = (f32[64,16,128]{2,1,0:T(8,128)S(1)}, f32[64,16,128]{2,1,0:T(8,128)}, u32[]{:S(2)}) copy-start(f32[64,16,128]{2,1,0:T(8,128)} %get-tuple-element.14) | copy-start | bytes 1572868
  41.8 10.9 %copy-start.5 = (f32[64,16,128]{2,1,0:T(8,128)S(1)}, f32[64,16,128]{2,1,0:T(8,128)}, u32[]{:S(2)}) copy-start(f32[64,16,128]{2,1,0:T(8,128)} %get-tuple-element.15) | copy-start | bytes 1572868
  41.8 5.8 %collective-permute-start.5 = (f32[6,2,16,128]{3,2,1,0:T(8,128)S(1)}, f32[6,2,16,128]{3,2,1,0:T(8,128)S(1)}, u32[]{:S(2)}, u32[]{:S(2)}) collective-permute-start(f32[6,2,16,128]{3,2,1,0:T(8,128)S(1)} %fusion.31), channel_id=1, source_target_pairs={{0,96},{8,104},{16,112},{24,120},{32,0},{40,8},{48,16},{56,24},{64... | collective-permute-start | bytes 294920 | tf_op jit(solution)/shard_map/ppermute | solution.py:163
  45.1 6.2 %collective-permute-start.6 = (f32[6,2,16,128]{3,2,1,0:T(8,128)S(1)}, f32[6,2,16,128]{3,2,1,0:T(8,128)S(1)}, u32[]{:S(2)}, u32[]{:S(2)}) collective-permute-start(f32[6,2,16,128]{3,2,1,0:T(8,128)S(1)} %fusion.31), channel_id=1, source_target_pairs={{0,64},{8,72},{16,80},{24,88},{32,96},{40,104},{48,112},{56,120},{... | collective-permute-start | bytes 294920 | tf_op jit(solution)/shard_map/ppermute | solution.py:163
  45.9 6.5 %collective-permute-start.7 = (f32[6,2,16,128]{3,2,1,0:T(8,128)S(1)}, f32[6,2,16,128]{3,2,1,0:T(8,128)S(1)}, u32[]{:S(2)}, u32[]{:S(2)}) collective-permute-start(f32[6,2,16,128]{3,2,1,0:T(8,128)S(1)} %fusion.31), channel_id=1, source_target_pairs={{0,32},{8,40},{16,48},{24,56},{32,64},{40,72},{48,80},{56,88},{64,... | collective-permute-start | bytes 294920 | tf_op jit(solution)/shard_map/ppermute | solution.py:163
  52.7 1.1 %copy-start = (f32[64,16,128]{2,1,0:T(8,128)S(1)}, f32[64,16,128]{2,1,0:T(8,128)}, u32[]{:S(2)}) copy-start(f32[64,16,128]{2,1,0:T(8,128)} %get-tuple-element.9) | copy-start | bytes 1572868
  52.7 1.4 %copy-start.1 = (f32[64,16,128]{2,1,0:T(8,128)S(1)}, f32[64,16,128]{2,1,0:T(8,128)}, u32[]{:S(2)}) copy-start(f32[64,16,128]{2,1,0:T(8,128)} %get-tuple-element.10) | copy-start | bytes 1572868
  52.7 1.5 %copy-start.2 = (f32[64,16,128]{2,1,0:T(8,128)S(1)}, f32[64,16,128]{2,1,0:T(8,128)}, u32[]{:S(2)}) copy-start(f32[64,16,128]{2,1,0:T(8,128)} %get-tuple-element.12) | copy-start | bytes 1572868

commit v8 on v5

--- a/solution.py
+++ b/solution.py
@@ -102,7 +102,7 @@
             wait_chunk(c)
         low = max(1, c * rows)
         high = min(z_cells - 1, (c + 1) * rows)
-        carry = lax.fori_loop(low, high, fwd, carry, unroll=8)
+        carry = lax.fori_loop(low, high, fwd, carry, unroll=True)
 
     z = z_cells - 1
     back = []
@@ -138,7 +138,7 @@
         low = c * rows
         high = min(z_cells - 1, (c + 1) * rows)
         back = lax.fori_loop(
-            0, high - low, lambda i, b: bwd(high - 1 - i, b), back, unroll=8
+            0, high - low, lambda i, b: bwd(high - 1 - i, b), back, unroll=True
         )
         for j in range(6):
             copy_out(j, c).start()

time: 57.1 us -> 57 us (level)
  no operation moved by 1% of the time
where the time goes in v8:
time: 57 us; the launch traced here: 56.5 us
  starting transfers between devices  19.9 us (35%)
  waiting for transfers between devices  18.4 us (32%)
  Pallas kernels  5.56 us (10%)
  other arithmetic  5.48 us (10%)
  matrix products  4.72 us (8%)
  local copies, waits for them, and re-layouts  1.54 us (3%)
  between operations  0.92 us (2%)
    ppermute x6, waiting for transfers between devices, gather_ring(): got[s] = lax.ppermute(pack, 'gz', route)  11.3 us
    ppermute x6, starting transfers between devices, gather_ring(): got[s] = lax.ppermute(pack, 'gz', route)  10.7 us
    pallas_call x1, Pallas kernels, local_solve(): pl.pallas_call(local_kernel, out_shape=(shape,) * 6 + (pack,), in_specs=[...  5.56 us
    all_to_all x1, starting transfers between devices, deposit(): lax.all_to_all(send, 'gx', split_axis=0, concat_axis=0, tiled=True)  4.58 us
    ppermute x1, waiting for transfers between devices, body(): lax.ppermute(first, 'gz', [(i + 1, i) for i in range(chain - 1)])  4.33 us
    ppermute x1, starting transfers between devices, body(): lax.ppermute(last, 'gz', [(i, i + 1) for i in range(chain - 1)])  3.38 us
    dot_general x1, matrix products, deposit(): send = jnp.einsum('dsr,rk->dsk', pick, stacked, precision=HIGH)  2.51 us
    dot_general x1, matrix products, deposit(): sources = jnp.dot(spread, rows, precision=HIGH)  2.02 us
  transfers between devices with their start and end apart: 9, of which 9 were waited for; matrix products, arithmetic and copies ran while one was open for 4% of the time, Pallas kernels for 0%

profile of v8, /device:TPU:0, one launch (start us, length us, event | category | flops | bytes accessed | tf_op | source)
XLA Modules:
  0.0 56.5 jit_solution(13815947762674367305)
XLA Ops:
  0.6 0.7 %fusion.93 = (f32[256]{0:T(256)S(1)}, s32[256]{0:T(256)S(1)}) fusion(s32[256]{0:T(256)} %bitcast.604), kind=kLoop, calls=%fused_computation.217 | loop fusion | flops 5376 | bytes 3072 | tf_op jit(solution)/shard_map/convert_element_type | solution.py:264
  1.3 0.2 fusion.8
  1.5 0.2 fusion.10
  1.8 0.1 fusion.15
  1.9 2.5 %fusion.2 = f32[8,97,256]{2,1,0:T(8,128)} fusion(pred[8,97,256]{2,1,0:T(8,128)(4,1)S(1)} %get-tuple-element.58, pred[8,97,256]{2,1,0:T(8,128)(4,1)S(1)} %get-tuple-element.57, f32[256,256]{1,0:T(8,128)S(1)} %fusion.15, f32[256,128]{1,0:T(8,128)} %bitcast.605, f32[256,128]{1,0:T(8,128)} %bitcast.606), kind=kOutput, calls=%fused_computation.2 | convolution fusion | flops 610930688 | bytes 1716224 | tf_op jit(solution)/shard_map/dsr,rk->dsk/dot_general | solution.py:267
  4.4 4.6 %all-to-all-start = ((f32[8,97,256]{2,1,0:T(8,128)}), f32[8,97,256]{2,1,0:T(8,128)S(1)}, u32[]{:S(2)}, u32[]{:S(2)}) async-start(f32[8,97,256]{2,1,0:T(8,128)} %fusion.2), calls=%async_computation | async-start | bytes 1703936 | tf_op jit(solution)/shard_map/all_to_all | solution.py:268
  9.0 0.7 %fusion.96 = (f32[1,16,128]{2,1,0:T(8,128)S(1)}, f32[1,16,128]{2,1,0:T(8,128)S(1)}, f32[1,16,128]{2,1,0:T(8,128)S(1)}, f32[1,16,128]{2,1,0:T(8,128)S(1)}) fusion(f32[64,16,128]{2,1,0:T(8,128)} %ct_hbm.1, f32[64,16,128]{2,1,0:T(8,128)} %ci_hbm.1), kind=kLoop, calls=%fused_computation.223 | loop fusion | bytes 65536 | tf_op jit(solution)/shard_map/slice | solution.py:283
  9.7 1.3 %collective-permute-start.1 = (f32[2,16,128]{2,1,0:T(8,128)S(1)}, f32[2,16,128]{2,1,0:T(8,128)S(1)}, u32[]{:S(2)}, u32[]{:S(2)}) collective-permute-start(f32[2,16,128]{2,1,0:T(8,128)S(1)} %pad_maximum_fusion), channel_id=1, source_target_pairs={{8,0},{16,8},{24,16},{32,24},{40,32},{48,40},{56,48},{64,56},{72,6... | collective-permute-start | bytes 49160 | tf_op jit(solution)/shard_map/ppermute | solution.py:286
  11.0 4.3 %collective-permute-done.1 = f32[2,16,128]{2,1,0:T(8,128)S(1)} collective-permute-done((f32[2,16,128]{2,1,0:T(8,128)S(1)}, f32[2,16,128]{2,1,0:T(8,128)S(1)}, u32[]{:S(2)}, u32[]{:S(2)}) %collective-permute-start.1) | collective-permute-done | bytes 16416 | tf_op jit(solution)/shard_map/ppermute | solution.py:286
  15.4 0.6 %divide_select_fusion = (f32[2,16,128]{2,1,0:T(8,128)}, f32[2,16,128]{2,1,0:T(8,128)S(1)}) fusion(f32[2,16,128]{2,1,0:T(8,128)S(1)} %collective-permute-done.1, pred[]{:T(512)S(6)} %eq.204, f32[1,16,128]{2,1,0:T(8,128)S(1)} %get-tuple-element.59, f32[1,16,128]{2,1,0:T(8,128)S(1)} %get-tuple-element.38), kind=kLoop, calls=%fused_computation.189 | loop fusion | flops 24576 | bytes 65537 | tf_op jit(solution)/shard_map/jit(_where)/select_n | solution.py:288
  16.0 3.4 %collective-permute-start = (f32[2,16,128]{2,1,0:T(8,128)S(1)}, f32[2,16,128]{2,1,0:T(8,128)S(1)}, u32[]{:S(2)}, u32[]{:S(2)}) collective-permute-start(f32[2,16,128]{2,1,0:T(8,128)S(1)} %get-tuple-element.54), channel_id=1, source_target_pairs={{0,8},{8,16},{16,24},{24,32},{32,40},{40,48},{48,56},{56,64},{64,7... | collective-permute-start | bytes 49160 | tf_op jit(solution)/shard_map/ppermute | solution.py:285
  19.4 1.4 %collective-permute-done = f32[2,16,128]{2,1,0:T(8,128)S(1)} collective-permute-done((f32[2,16,128]{2,1,0:T(8,128)S(1)}, f32[2,16,128]{2,1,0:T(8,128)S(1)}, u32[]{:S(2)}, u32[]{:S(2)}) %collective-permute-start) | collective-permute-done | bytes 16416 | tf_op jit(solution)/shard_map/ppermute | solution.py:285
  20.8 0.6 %broadcast_select_fusion = (f32[2,16,128]{2,1,0:T(8,128)}, f32[2,16,128]{2,1,0:T(8,128)}) fusion(pred[]{:T(512)S(6)} %eq.203, f32[2,16,128]{2,1,0:T(8,128)S(1)} %collective-permute-done, f32[1,16,128]{2,1,0:T(8,128)S(1)} %get-tuple-element.60, f32[1,16,128]{2,1,0:T(8,128)S(1)} %get-tuple-element.37), kind=kLoop, calls=%fused_computation.206 | loop fusion | flops 32768 | bytes 65537 | tf_op jit(solution)/shard_map/jit(_where)/select_n | solution.py:290
  21.4 1.4 %all-to-all-done = f32[8,97,256]{2,1,0:T(8,128)S(1)} async-done(((f32[8,97,256]{2,1,0:T(8,128)}), f32[8,97,256]{2,1,0:T(8,128)S(1)}, u32[]{:S(2)}, u32[]{:S(2)}) %all-to-all-start) | async-done | bytes 794656 | tf_op jit(solution)/shard_map/all_to_all | solution.py:268
  22.8 0.1 sub.312
  22.9 0.1 slice.217
  23.0 2.0 %fusion.src_hbm = f32[64,16,256]{2,1,0:T(8,128)} fusion(f32[768,256,1]{1,0,2:T(8,128)S(1)} %bitcast.603, f32[768]{0:T(1024)S(1)} %sub.312, f32[64,16]{1,0:T(8,128)S(1)} %add_convert_fusion), kind=kOutput, calls=%fused_computation | convolution fusion | flops 1208745984 | bytes 1842176 | tf_op jit(solution)/shard_map/dot_general | solution.py:273
  25.0 5.6 %shard_map.86 = (f32[64,16,128]{2,1,0:T(8,128)}, f32[64,16,128]{2,1,0:T(8,128)}, f32[64,16,128]{2,1,0:T(8,128)}, f32[64,16,128]{2,1,0:T(8,128)}, f32[64,16,128]{...) custom-call(f32[64,16,128]{2,1,0:T(8,128)} %rt_hbm.1, f32[64,16,128]{2,1,0:T(8,128)} %ri_hbm.1, ...), custom_call_target="tpu_custom_call" | custom-call | tf_op jit(solution)/shard_map/pallas_call | solution.py:166
  30.6 4.3 %collective-permute-start.2 = (f32[6,2,16,128]{3,2,1,0:T(8,128)}, f32[6,2,16,128]{3,2,1,0:T(8,128)S(1)}, u32[]{:S(2)}, u32[]{:S(2)}) collective-permute-start(f32[6,2,16,128]{3,2,1,0:T(8,128)} %get-tuple-element.11), channel_id=1, source_target_pairs={{0,24},{8,0},{16,8},{24,16},{32,56},{40,32},{48,40},{56,48},{64,88... | collective-permute-start | bytes 294920 | tf_op jit(solution)/shard_map/ppermute | solution.py:222
  34.9 0.0 collective-permute-start.3
  34.9 0.9 %collective-permute-start.4 = (f32[6,2,16,128]{3,2,1,0:T(8,128)}, f32[6,2,16,128]{3,2,1,0:T(8,128)S(1)}, u32[]{:S(2)}, u32[]{:S(2)}) collective-permute-start(f32[6,2,16,128]{3,2,1,0:T(8,128)} %get-tuple-element.11), channel_id=1, source_target_pairs={{0,8},{8,16},{16,24},{24,0},{32,40},{40,48},{48,56},{56,32},{64,72... | collective-permute-start | bytes 294920 | tf_op jit(solution)/shard_map/ppermute | solution.py:222
  35.9 2.6 %collective-permute-done.2 = f32[6,2,16,128]{3,2,1,0:T(8,128)S(1)} collective-permute-done((f32[6,2,16,128]{3,2,1,0:T(8,128)}, f32[6,2,16,128]{3,2,1,0:T(8,128)S(1)}, u32[]{:S(2)}, u32[]{:S(2)}) %collective-permute-start.2) | collective-permute-done | bytes 98336 | tf_op jit(solution)/shard_map/ppermute | solution.py:222
  38.5 2.9 %collective-permute-done.3 = f32[6,2,16,128]{3,2,1,0:T(8,128)S(1)} collective-permute-done((f32[6,2,16,128]{3,2,1,0:T(8,128)}, f32[6,2,16,128]{3,2,1,0:T(8,128)S(1)}, u32[]{:S(2)}, u32[]{:S(2)}) %collective-permute-start.3) | collective-permute-done | bytes 98336 | tf_op jit(solution)/shard_map/ppermute | solution.py:222
  41.3 0.7 %collective-permute-done.4 = f32[6,2,16,128]{3,2,1,0:T(8,128)S(1)} collective-permute-done((f32[6,2,16,128]{3,2,1,0:T(8,128)}, f32[6,2,16,128]{3,2,1,0:T(8,128)S(1)}, u32[]{:S(2)}, u32[]{:S(2)}) %collective-permute-start.4) | collective-permute-done | bytes 98336 | tf_op jit(solution)/shard_map/ppermute | solution.py:222
  42.0 0.9 %select_select_fusion.6 = (f32[6,2,16,128]{3,2,1,0:T(8,128)S(1)}, f32[6,2,16,128]{3,2,1,0:T(8,128)S(1)}, f32[6,2,16,128]{3,2,1,0:T(8,128)S(1)}, f32[6,2,16,128]{3,2,1,0:T(8,128)S(1)}) fusion(f32[6,2,16,128]{3,2,1,0:T(8,128)S(1)} %collective-permute-done.2, f32[6,2,16,128]{3,2,1,0:T(8,128)S(1)} %collective-permute-done.3, ...), kind=kLoop, calls=%fused_computation.30 | loop fusion | flops 294912 | bytes 786444 | tf_op jit(solution)/shard_map/jit(_where)/select_n | solution.py:227
  43.1 0.0 copy-start.7
  43.2 0.0 copy-start.6
  43.2 0.0 copy-start.3
  43.2 0.0 copy-start.4
  43.2 0.0 copy-start.5
  43.2 3.3 %collective-permute-start.5 = (f32[6,2,16,128]{3,2,1,0:T(8,128)S(1)}, f32[6,2,16,128]{3,2,1,0:T(8,128)S(1)}, u32[]{:S(2)}, u32[]{:S(2)}) collective-permute-start(f32[6,2,16,128]{3,2,1,0:T(8,128)S(1)} %fusion.31), channel_id=1, source_target_pairs={{0,96},{8,104},{16,112},{24,120},{32,0},{40,8},{48,16},{56,24},{64... | collective-permute-start | bytes 294920 | tf_op jit(solution)/shard_map/ppermute | solution.py:222
  46.5 0.8 %collective-permute-start.6 = (f32[6,2,16,128]{3,2,1,0:T(8,128)S(1)}, f32[6,2,16,128]{3,2,1,0:T(8,128)S(1)}, u32[]{:S(2)}, u32[]{:S(2)}) collective-permute-start(f32[6,2,16,128]{3,2,1,0:T(8,128)S(1)} %fusion.31), channel_id=1, source_target_pairs={{0,64},{8,72},{16,80},{24,88},{32,96},{40,104},{48,112},{56,120},{... | collective-permute-start | bytes 294920 | tf_op jit(solution)/shard_map/ppermute | solution.py:222
  47.3 1.3 %collective-permute-start.7 = (f32[6,2,16,128]{3,2,1,0:T(8,128)S(1)}, f32[6,2,16,128]{3,2,1,0:T(8,128)S(1)}, u32[]{:S(2)}, u32[]{:S(2)}) collective-permute-start(f32[6,2,16,128]{3,2,1,0:T(8,128)S(1)} %fusion.31), channel_id=1, source_target_pairs={{0,32},{8,40},{16,48},{24,56},{32,64},{40,72},{48,80},{56,88},{64,... | collective-permute-start | bytes 294920 | tf_op jit(solution)/shard_map/ppermute | solution.py:222
  48.6 0.4 collective-permute-done.5
  49.0 3.7 %collective-permute-done.6 = f32[6,2,16,128]{3,2,1,0:T(8,128)S(1)} collective-permute-done((f32[6,2,16,128]{3,2,1,0:T(8,128)S(1)}, f32[6,2,16,128]{3,2,1,0:T(8,128)S(1)}, u32[]{:S(2)}, u32[]{:S(2)}) %collective-permute-start.6) | collective-permute-done | bytes 98336 | tf_op jit(solution)/shard_map/ppermute | solution.py:222
  52.7 1.1 %collective-permute-done.7 = f32[6,2,16,128]{3,2,1,0:T(8,128)S(1)} collective-permute-done((f32[6,2,16,128]{3,2,1,0:T(8,128)S(1)}, f32[6,2,16,128]{3,2,1,0:T(8,128)S(1)}, u32[]{:S(2)}, u32[]{:S(2)}) %collective-permute-start.7) | collective-permute-done | bytes 98336 | tf_op jit(solution)/shard_map/ppermute | solution.py:222
  53.8 0.1 select_select_fusion.1
  53.8 0.1 fusion.50
  53.9 0.0 copy-done.7
  54.0 0.1 select_select_fusion.8
  54.0 0.0 copy-done.6
  54.1 0.0 copy-done.3
  54.1 0.0 copy-done.4
  54.1 0.0 copy-done.5
  54.1 0.0 copy-start
  54.1 0.0 copy-start.1
  54.1 0.0 copy-start.2
  54.1 0.9 %multiply_add_fusion = f32[64,16,128]{2,1,0:T(8,128)} fusion(f32[64,16,128]{2,1,0:T(8,128)S(1)} %copy-done.5, f32[64,16,128]{2,1,0:T(8,128)S(1)} %copy-done.3, f32[64,16,128]{2,1,0:T(8,128)S(1)} %copy-done.4, f32[16,128]{1,0:T(8,128)S(1)} %get-tuple-element.51, f32[16,128]{1,0:T(8,128)S(1)} %get-tuple-element.49), kind=kLoop, calls=%fused_computation.19 | loop fusion | flops 524288 | bytes 2113536 | tf_op jit(solution)/shard_map/add | solution.py:340
  55.0 0.1 copy-done
  55.2 0.3 copy-done.1
  55.5 0.2 copy-done.2
  55.7 0.9 %multiply_add_fusion.1 = f32[64,16,128]{2,1,0:T(8,128)} fusion(f32[64,16,128]{2,1,0:T(8,128)S(1)} %copy-done.2, f32[64,16,128]{2,1,0:T(8,128)S(1)} %copy-done, f32[64,16,128]{2,1,0:T(8,128)S(1)} %copy-done.1, f32[16,128]{1,0:T(8,128)S(1)} %get-tuple-element.52, f32[16,128]{1,0:T(8,128)S(1)} %get-tuple-element.50), kind=kLoop, calls=%fused_computation.20 | loop fusion | flops 524288 | bytes 2113536 | tf_op jit(solution)/shard_map/add | solution.py:340
  (15 shorter events, 0.2 us)
Async XLA Ops:
  4.4 18.4 %all-to-all-start = ((f32[8,97,256]{2,1,0:T(8,128)}), f32[8,97,256]{2,1,0:T(8,128)S(1)}, u32[]{:S(2)}, u32[]{:S(2)}) async-start(f32[8,97,256]{2,1,0:T(8,128)} %fusion.2), calls=%async_computation | async-start | bytes 1703936 | tf_op jit(solution)/shard_map/all_to_all | solution.py:268
  9.7 5.6 %collective-permute-start.1 = (f32[2,16,128]{2,1,0:T(8,128)S(1)}, f32[2,16,128]{2,1,0:T(8,128)S(1)}, u32[]{:S(2)}, u32[]{:S(2)}) collective-permute-start(f32[2,16,128]{2,1,0:T(8,128)S(1)} %pad_maximum_fusion), channel_id=1, source_target_pairs={{8,0},{16,8},{24,16},{32,24},{40,32},{48,40},{56,48},{64,56},{72,6... | collective-permute-start | bytes 49160 | tf_op jit(solution)/shard_map/ppermute | solution.py:286
  16.0 4.8 %collective-permute-start = (f32[2,16,128]{2,1,0:T(8,128)S(1)}, f32[2,16,128]{2,1,0:T(8,128)S(1)}, u32[]{:S(2)}, u32[]{:S(2)}) collective-permute-start(f32[2,16,128]{2,1,0:T(8,128)S(1)} %get-tuple-element.54), channel_id=1, source_target_pairs={{0,8},{8,16},{16,24},{24,32},{32,40},{40,48},{48,56},{56,64},{64,7... | collective-permute-start | bytes 49160 | tf_op jit(solution)/shard_map/ppermute | solution.py:285
  30.6 7.9 %collective-permute-start.2 = (f32[6,2,16,128]{3,2,1,0:T(8,128)}, f32[6,2,16,128]{3,2,1,0:T(8,128)S(1)}, u32[]{:S(2)}, u32[]{:S(2)}) collective-permute-start(f32[6,2,16,128]{3,2,1,0:T(8,128)} %get-tuple-element.11), channel_id=1, source_target_pairs={{0,24},{8,0},{16,8},{24,16},{32,56},{40,32},{48,40},{56,48},{64,88... | collective-permute-start | bytes 294920 | tf_op jit(solution)/shard_map/ppermute | solution.py:222
  34.9 6.4 %collective-permute-start.3 = (f32[6,2,16,128]{3,2,1,0:T(8,128)}, f32[6,2,16,128]{3,2,1,0:T(8,128)S(1)}, u32[]{:S(2)}, u32[]{:S(2)}) collective-permute-start(f32[6,2,16,128]{3,2,1,0:T(8,128)} %get-tuple-element.11), channel_id=1, source_target_pairs={{0,16},{8,24},{16,0},{24,8},{32,48},{40,56},{48,32},{56,40},{64,80... | collective-permute-start | bytes 294920 | tf_op jit(solution)/shard_map/ppermute | solution.py:222
  34.9 7.1 %collective-permute-start.4 = (f32[6,2,16,128]{3,2,1,0:T(8,128)}, f32[6,2,16,128]{3,2,1,0:T(8,128)S(1)}, u32[]{:S(2)}, u32[]{:S(2)}) collective-permute-start(f32[6,2,16,128]{3,2,1,0:T(8,128)} %get-tuple-element.11), channel_id=1, source_target_pairs={{0,8},{8,16},{16,24},{24,0},{32,40},{40,48},{48,56},{56,32},{64,72... | collective-permute-start | bytes 294920 | tf_op jit(solution)/shard_map/ppermute | solution.py:222
  43.1 10.8 %copy-start.7 = (f32[2,16,128]{2,1,0:T(8,128)S(1)}, f32[2,16,128]{2,1,0:T(8,128)}, u32[]{:S(2)}) copy-start(f32[2,16,128]{2,1,0:T(8,128)} %get-tuple-element.35.beta_ref) | copy-start | bytes 49156
  43.2 10.9 %copy-start.6 = (f32[2,16,128]{2,1,0:T(8,128)S(1)}, f32[2,16,128]{2,1,0:T(8,128)}, u32[]{:S(2)}) copy-start(f32[2,16,128]{2,1,0:T(8,128)} %get-tuple-element.53.hi_ref) | copy-start | bytes 49156
  43.2 10.9 %copy-start.3 = (f32[64,16,128]{2,1,0:T(8,128)S(1)}, f32[64,16,128]{2,1,0:T(8,128)}, u32[]{:S(2)}) copy-start(f32[64,16,128]{2,1,0:T(8,128)} %get-tuple-element.13) | copy-start | bytes 1572868
  43.2 10.9 %copy-start.4 = (f32[64,16,128]{2,1,0:T(8,128)S(1)}, f32[64,16,128]{2,1,0:T(8,128)}, u32[]{:S(2)}) copy-start(f32[64,16,128]{2,1,0:T(8,128)} %get-tuple-element.14) | copy-start | bytes 1572868
  43.2 10.9 %copy-start.5 = (f32[64,16,128]{2,1,0:T(8,128)S(1)}, f32[64,16,128]{2,1,0:T(8,128)}, u32[]{:S(2)}) copy-start(f32[64,16,128]{2,1,0:T(8,128)} %get-tuple-element.15) | copy-start | bytes 1572868
  43.2 5.8 %collective-permute-start.5 = (f32[6,2,16,128]{3,2,1,0:T(8,128)S(1)}, f32[6,2,16,128]{3,2,1,0:T(8,128)S(1)}, u32[]{:S(2)}, u32[]{:S(2)}) collective-permute-start(f32[6,2,16,128]{3,2,1,0:T(8,128)S(1)} %fusion.31), channel_id=1, source_target_pairs={{0,96},{8,104},{16,112},{24,120},{32,0},{40,8},{48,16},{56,24},{64... | collective-permute-start | bytes 294920 | tf_op jit(solution)/shard_map/ppermute | solution.py:222
  46.5 6.2 %collective-permute-start.6 = (f32[6,2,16,128]{3,2,1,0:T(8,128)S(1)}, f32[6,2,16,128]{3,2,1,0:T(8,128)S(1)}, u32[]{:S(2)}, u32[]{:S(2)}) collective-permute-start(f32[6,2,16,128]{3,2,1,0:T(8,128)S(1)} %fusion.31), channel_id=1, source_target_pairs={{0,64},{8,72},{16,80},{24,88},{32,96},{40,104},{48,112},{56,120},{... | collective-permute-start | bytes 294920 | tf_op jit(solution)/shard_map/ppermute | solution.py:222
  47.3 6.5 %collective-permute-start.7 = (f32[6,2,16,128]{3,2,1,0:T(8,128)S(1)}, f32[6,2,16,128]{3,2,1,0:T(8,128)S(1)}, u32[]{:S(2)}, u32[]{:S(2)}) collective-permute-start(f32[6,2,16,128]{3,2,1,0:T(8,128)S(1)} %fusion.31), channel_id=1, source_target_pairs={{0,32},{8,40},{16,48},{24,56},{32,64},{40,72},{48,80},{56,88},{64,... | collective-permute-start | bytes 294920 | tf_op jit(solution)/shard_map/ppermute | solution.py:222
  54.1 1.1 %copy-start = (f32[64,16,128]{2,1,0:T(8,128)S(1)}, f32[64,16,128]{2,1,0:T(8,128)}, u32[]{:S(2)}) copy-start(f32[64,16,128]{2,1,0:T(8,128)} %get-tuple-element.9) | copy-start | bytes 1572868
  54.1 1.4 %copy-start.1 = (f32[64,16,128]{2,1,0:T(8,128)S(1)}, f32[64,16,128]{2,1,0:T(8,128)}, u32[]{:S(2)}) copy-start(f32[64,16,128]{2,1,0:T(8,128)} %get-tuple-element.10) | copy-start | bytes 1572868
  54.1 1.5 %copy-start.2 = (f32[64,16,128]{2,1,0:T(8,128)S(1)}, f32[64,16,128]{2,1,0:T(8,128)}, u32[]{:S(2)}) copy-start(f32[64,16,128]{2,1,0:T(8,128)} %get-tuple-element.12) | copy-start | bytes 1572868
